TPU v7x, 32 devices: a whole 2x2x4 slice. The times are simulated.
32 devices in a mesh: grp: 2 (over x), gx: 16 (over z, y, core).
Axes of the slice: x: 2, y: 2, z: 4, core: 2. Of those that a mesh axis runs over, the one named last changes fastest.
Arguments:
- volume: float32 [1024, 128, 128], P(('grp', 'gx')), parts along dimension 0, may hold values from -6 to 6
- level_set: float32 [1024, 128, 128], P(('grp', 'gx')), parts along dimension 0, may hold values from -6 to 6
Outputs:
- edge_map: float32 [1024, 128, 128], P(('grp', 'gx')), parts along dimension 0
- advanced: float32 [1024, 128, 128], P(('grp', 'gx')), parts along dimension 0
There are 2 independent parts, one for each index of `grp`. A program takes and returns all parts, laid end to end along the dimension named above; each array names one. Nothing has to cross between parts.
All inputs are finite; a program needn't handle non-finite values.
Results may differ from a plain program's by a relative error of at most 0.00002.
Values sent between devices are 32-bit elements; how exact they have to be, the bound alone decides.
No kernel may reach another device: no remote copies, remote signals or barrier semaphores. Data moves between devices by JAX's collectives and lax.ppermute only.
A program may use at most 64 MiB of HBM per device.

v0:
```python
import math

import numpy as np

import jax
import jax.numpy as jnp
from jax import lax
from jax.sharding import PartitionSpec as P

RADIUS = 12


def shifted(block, axis, distance):
    devices = range(lax.axis_size(axis))
    route = [(i - distance, i) for i in devices if i - distance in devices]
    return lax.ppermute(block, axis, route)


def extended_2(block, sides, width):
    for axis, dim in sides:
        count = lax.axis_size(axis)
        forward = [(i, i + 1) for i in range(count - 1)]
        backward = [(target, source) for source, target in forward]
        low = lax.ppermute(
            lax.slice_in_dim(block, block.shape[dim] - width, None, axis=dim), axis, forward
        )
        high = lax.ppermute(lax.slice_in_dim(block, 0, width, axis=dim), axis, backward)
        block = jnp.concatenate([low, block, high], axis=dim)
    return block


def blur_taps():
    raw = [math.exp(-(offset * offset) / 18.0) for offset in range(-RADIUS, RADIUS + 1)]
    total = sum(raw)
    return [value / total for value in raw]


def band(rows, cols, shift):
    taps = blur_taps()
    table = np.zeros((rows, cols), np.float32)
    for i in range(rows):
        for k in range(-RADIUS, RADIUS + 1):
            j = i + shift + k
            if 0 <= j < cols:
                table[i, j] = taps[k + RADIUS]
    return jnp.asarray(table)


def pad_axis(array, axis, width):
    widths = [(0, 0), (0, 0), (0, 0)]
    widths[axis] = (width, width)
    return jnp.pad(array, widths)


def blur_padded(padded, axis, count):
    taps = blur_taps()
    result = taps[0] * lax.slice_in_dim(padded, 0, count, axis=axis)
    for offset in range(1, len(taps)):
        result = result + taps[offset] * lax.slice_in_dim(padded, offset, offset + count, axis=axis)
    return result


def central_grads(padded):
    inner = padded[1:-1]
    side = jnp.pad(inner, ((0, 0), (1, 1), (1, 1)))
    grad_x = (padded[2:] - padded[:-2]) * 0.5
    grad_y = (side[:, 2:, 1:-1] - side[:, :-2, 1:-1]) * 0.5
    grad_z = (side[:, 1:-1, 2:] - side[:, 1:-1, :-2]) * 0.5
    return (grad_x, grad_y, grad_z)


def edge_from(padded):
    grad_x, grad_y, grad_z = central_grads(padded)
    return 1.0 / (1.0 + 6000.0 * (grad_x * grad_x + grad_y * grad_y + grad_z * grad_z))


def weno(first, second, third, fourth, fifth):
    cand_one = (2.0 * first - 7.0 * second + 11.0 * third) / 6.0
    cand_two = (-second + 5.0 * third + 2.0 * fourth) / 6.0
    cand_three = (2.0 * third + 5.0 * fourth - fifth) / 6.0
    part_a = first - 2.0 * second + third
    part_b = first - 4.0 * second + 3.0 * third
    smooth_one = 13.0 / 12.0 * part_a * part_a + 0.25 * part_b * part_b
    part_a = second - 2.0 * third + fourth
    part_b = second - fourth
    smooth_two = 13.0 / 12.0 * part_a * part_a + 0.25 * part_b * part_b
    part_a = third - 2.0 * fourth + fifth
    part_b = 3.0 * third - 4.0 * fourth + fifth
    smooth_three = 13.0 / 12.0 * part_a * part_a + 0.25 * part_b * part_b
    denom_one = 1e-06 + smooth_one
    denom_two = 1e-06 + smooth_two
    denom_three = 1e-06 + smooth_three
    weight_one = 0.1 / (denom_one * denom_one)
    weight_two = 0.6 / (denom_two * denom_two)
    weight_three = 0.3 / (denom_three * denom_three)
    return (weight_one * cand_one + weight_two * cand_two + weight_three * cand_three) / (
        weight_one + weight_two + weight_three
    )


def upwind(padded, axis, count):
    diffs = lax.slice_in_dim(padded, 1, padded.shape[axis], axis=axis) - lax.slice_in_dim(
        padded, 0, padded.shape[axis] - 1, axis=axis
    )
    pieces = [lax.slice_in_dim(diffs, offset, offset + count, axis=axis) for offset in range(6)]
    minus = weno(pieces[0], pieces[1], pieces[2], pieces[3], pieces[4])
    plus = weno(pieces[5], pieces[4], pieces[3], pieces[2], pieces[1])
    return (minus, plus)


def rates(padded, edge, slope):
    count = padded.shape[0] - 6
    field = padded[3:-3]
    rows_y = field.shape[1]
    rows_z = field.shape[2]
    minus_x, plus_x = upwind(padded, 0, count)
    minus_y, plus_y = upwind(pad_axis(field, 1, 3), 1, rows_y)
    minus_z, plus_z = upwind(pad_axis(field, 2, 3), 2, rows_z)
    near = jnp.pad(padded[2:-2], ((0, 0), (1, 1), (1, 1)))

    def beside_all(step_x, step_y, step_z):
        return near[
            1 + step_x : 1 + step_x + count,
            1 + step_y : 1 + step_y + rows_y,
            1 + step_z : 1 + step_z + rows_z,
        ]

    centre = beside_all(0, 0, 0)
    first_x = (beside_all(1, 0, 0) - beside_all(-1, 0, 0)) * 0.5
    first_y = (beside_all(0, 1, 0) - beside_all(0, -1, 0)) * 0.5
    first_z = (beside_all(0, 0, 1) - beside_all(0, 0, -1)) * 0.5
    second_xx = beside_all(1, 0, 0) - 2.0 * centre + beside_all(-1, 0, 0)
    second_yy = beside_all(0, 1, 0) - 2.0 * centre + beside_all(0, -1, 0)
    second_zz = beside_all(0, 0, 1) - 2.0 * centre + beside_all(0, 0, -1)
    mixed_xy = (
        beside_all(1, 1, 0) - beside_all(1, -1, 0) - beside_all(-1, 1, 0) + beside_all(-1, -1, 0)
    ) * 0.25
    mixed_xz = (
        beside_all(1, 0, 1) - beside_all(1, 0, -1) - beside_all(-1, 0, 1) + beside_all(-1, 0, -1)
    ) * 0.25
    mixed_yz = (
        beside_all(0, 1, 1) - beside_all(0, 1, -1) - beside_all(0, -1, 1) + beside_all(0, -1, -1)
    ) * 0.25
    square_x = first_x * first_x
    square_y = first_y * first_y
    square_z = first_z * first_z
    numerator = (
        second_xx * (square_y + square_z)
        + second_yy * (square_x + square_z)
        + second_zz * (square_x + square_y)
    )
    numerator = numerator - 2.0 * (
        first_x * first_y * mixed_xy + first_x * first_z * mixed_xz + first_y * first_z * mixed_yz
    )
    curvature = numerator / (square_x + square_y + square_z + 1.0)
    speed_x = -slope[0]
    speed_y = -slope[1]
    speed_z = -slope[2]
    transport = jnp.maximum(speed_x, 0.0) * minus_x + jnp.minimum(speed_x, 0.0) * plus_x
    transport = transport + jnp.maximum(speed_y, 0.0) * minus_y + jnp.minimum(speed_y, 0.0) * plus_y
    transport = transport + jnp.maximum(speed_z, 0.0) * minus_z + jnp.minimum(speed_z, 0.0) * plus_z
    return edge * curvature - transport


def shards(volume, level_set):
    rows, rows_y, rows_z = volume.shape
    exact = lax.Precision.HIGHEST
    blurred = jnp.dot(
        volume.reshape(rows * rows_y, rows_z), band(rows_z, rows_z, 0).T, precision=exact
    ).reshape(rows, rows_y, rows_z)
    blurred = jnp.einsum("yv,xvz->xyz", band(rows_y, rows_y, 0), blurred, precision=exact)
    reach = -(-RADIUS // rows)
    jobs = []
    needed = min(rows, RADIUS)
    jobs.append((1, blurred[rows - needed :]))
    jobs.append((-1, blurred[:needed]))
    moved = [shifted(piece, "gx", signed_hops) for signed_hops, piece in jobs]
    below = [moved[2 * (reach - 1)]]
    above = [moved[1]]
    extended = jnp.concatenate(below + [blurred] + above, axis=0)
    blurred = jnp.dot(
        band(rows, extended.shape[0], needed),
        extended.reshape(extended.shape[0], rows_y * rows_z),
        precision=exact,
    ).reshape(rows, rows_y, rows_z)
    wider = extended_2(blurred, (("gx", 0),), 2)
    edge_wide = edge_from(wider)
    positions = lax.axis_index("gx") * rows - 1 + jnp.arange(rows + 2, dtype=jnp.int32)
    inside = (positions >= 0) & (positions < rows * lax.axis_size("gx"))
    edge_wide = jnp.where(inside[:, None, None], edge_wide, 0.0)
    edge = edge_wide[1:-1]
    slope = central_grads(edge_wide)

    def rate_of(field):
        padded = extended_2(field, (("gx", 0),), 3)
        return rates(padded, edge, slope)

    section_one = level_set + 0.1 * rate_of(level_set)
    section_two = 0.75 * level_set + 0.25 * (section_one + 0.1 * rate_of(section_one))
    advanced = 1.0 / 3.0 * level_set + 2.0 / 3.0 * (section_two + 0.1 * rate_of(section_two))
    return (edge, advanced)


def solution(mesh):
    return jax.shard_map(
        shards,
        mesh=mesh,
        in_specs=(P(("grp", "gx"), None, None), P(("grp", "gx"), None, None)),
        out_specs=(P(("grp", "gx"), None, None), P(("grp", "gx"), None, None)),
        check_vma=False,
    )
```

profile of v0, /device:TPU:1, one launch (start us, length us, event | category | flops | bytes accessed | tf_op | source)
XLA Modules:
  0.0 263.8 jit_solution(16540057749609807213)
XLA Ops:
  2.2 2.8 %fusion.428 = f32[128,32,128]{2,0,1:T(8,128)S(1)} fusion(f32[128,128,1]{1,0,2:T(8,128)} %constant.140, f32[32,128,128]{2,1,0:T(8,128)S(1)} %copy-done), kind=kOutput, calls=%fused_computation.667 | convolution fusion | flops 805306368 | bytes 4259840 | tf_op jit(solution)/shard_map/dot_general | solution.py:168
  9.6 4.5 %collective-permute-start = (f32[12,128,128]{1,2,0:T(8,128)}, f32[12,128,128]{1,2,0:T(8,128)S(1)}, u32[]{:S(2)}, u32[]{:S(2)}) collective-permute-start(f32[12,128,128]{1,2,0:T(8,128)} %get-tuple-element.10), channel_id=1, source_target_pairs={{0,1},{1,2},{2,3},{3,4},{4,5},{5,6},{6,7},{7,8},{8,9},{9,10},{10,1... | collective-permute-start | bytes 2359304 | tf_op jit(solution)/shard_map/ppermute | solution.py:16
  14.1 1.9 collective-permute-start.1
  16.8 3.6 %collective-permute-start.5 = (f32[3,128,128]{2,1,0:T(8,128)}, f32[3,128,128]{2,1,0:T(8,128)S(1)}, u32[]{:S(2)}, u32[]{:S(2)}) collective-permute-start(f32[3,128,128]{2,1,0:T(8,128)} %get-tuple-element.7), channel_id=1, source_target_pairs={{0,1},{1,2},{2,3},{3,4},{4,5},{5,6},{6,7},{7,8},{8,9},{9,10},{10,1... | collective-permute-start | bytes 589832 | tf_op jit(solution)/shard_map/ppermute | solution.py:24
  20.4 2.4 collective-permute-start.4
  24.6 4.2 %fusion.3 = f32[32,128,133]{2,1,0:T(8,128)} fusion(f32[32,128,128]{2,1,0:T(8,128)S(1)} %copy-done.3), kind=kLoop, calls=%fused_computation.67 | loop fusion | flops 544768 | bytes 4276224 | tf_op jit(solution)/shard_map/sub | solution.py:102
  28.8 7.2 %collective-permute-done.5 = f32[3,128,128]{2,1,0:T(8,128)S(1)} collective-permute-done((f32[3,128,128]{2,1,0:T(8,128)}, f32[3,128,128]{2,1,0:T(8,128)S(1)}, u32[]{:S(2)}, u32[]{:S(2)}) %collective-permute-start.5) | collective-permute-done | bytes 196640 | tf_op jit(solution)/shard_map/ppermute | solution.py:24
  39.0 3.3 %pad_maximum_fusion = f32[56,128,128]{1,2,0:T(8,128)} fusion(f32[12,128,128]{1,2,0:T(8,128)} %collective-permute-done.1, f32[32,128,128]{1,2,0:T(8,128)S(1)} %copy-done.7, f32[12,128,128]{1,2,0:T(8,128)S(1)} %collective-permute-done), kind=kLoop, calls=%fused_computation.73 | loop fusion | flops 1835008 | bytes 7340032 | tf_op jit(solution)/shard_map/concatenate | solution.py:180
  42.4 5.3 %copy.7 = f32[56,128,128]{2,1,0:T(8,128)} copy(f32[56,128,128]{1,2,0:T(8,128)} %pad_maximum_fusion) | data formatting | bytes 7340032 | tf_op jit(solution)/shard_map/concatenate | solution.py:180
  47.7 6.3 %fusion.6 = f32[32,16384]{1,0:T(8,128)S(1)} fusion(f32[32,56]{1,0:T(8,128)S(1)} %copy-done.9, f32[7,8,128,128]{3,2,1,0:T(8,128)} %bitcast.30), kind=kOutput, calls=%fused_computation.70 | convolution fusion | flops 352321536 | bytes 5774336 | tf_op jit(solution)/shard_map/dot_general | solution.py:181
  56.0 4.5 %collective-permute-start.3 = (f32[2,128,128]{2,1,0:T(8,128)S(1)}, f32[2,128,128]{2,1,0:T(8,128)S(1)}, u32[]{:S(2)}, u32[]{:S(2)}) collective-permute-start(f32[2,128,128]{2,1,0:T(8,128)S(1)} %bitcast.33), channel_id=1, source_target_pairs={{0,1},{1,2},{2,3},{3,4},{4,5},{5,6},{6,7},{7,8},{8,9},{9,10},{10,1... | collective-permute-start | bytes 393224 | tf_op jit(solution)/shard_map/ppermute | solution.py:24
  60.5 4.4 %slice_subtract_fusion.2 = f32[37,128,128]{2,1,0:T(8,128)} fusion(f32[38,128,128]{2,1,0:T(8,128)} %constant_dynamic-update-slice_fusion), kind=kLoop, calls=%fused_computation.186 | loop fusion | flops 606208 | bytes 7274496 | tf_op jit(solution)/shard_map/sub | solution.py:102
  64.9 3.2 %slice.671 = f32[34,128,128]{2,1,0:T(8,128)} slice(f32[38,128,128]{2,1,0:T(8,128)} %constant_dynamic-update-slice_fusion), slice={[2:36], [0:128], [0:128]} | slice | bytes 4456448 | tf_op jit(solution)/shard_map/slice | solution.py:119
  68.5 2.9 %select_maximum_fusion = f32[34,130,130]{2,1,0:T(8,128)S(1)} fusion(f32[2,128,128]{2,1,0:T(8,128)S(1)} %collective-permute-done.2, f32[32,128,128]{2,1,0:T(8,128)S(1)} %bitcast.28, f32[2,128,128]{2,1,0:T(8,128)S(1)} %collective-permute-done.3), kind=kLoop, calls=%fused_computation.62 | loop fusion | flops 8619000 | bytes 4657696 | tf_op jit(solution)/shard_map/concatenate | solution.py:28
  71.5 2.6 fusion.20
  77.0 50.5 %multiply_add_fusion.16 = f32[32,128,128]{2,1,0:T(8,128)} fusion(f32[32,128,128]{2,1,0:T(8,128)S(1)} %copy-done.3, f32[32,128,133]{2,1,0:T(8,128)} %fusion.3, f32[32,133,128]{2,1,0:T(8,128)} %slice_subtract_fusion.7, f32[37,128,128]{2,1,0:T(8,128)} %slice_subtract_fusion.2, f32[32,128,128]{2,1,0:T(8,128)} %slice.670, f32[34,128,128]{2,1,0:T(8,128)} %slice.671, ...), kind=kLoop, calls=%fused_computation.604 | loop fusion | flops 237502464 | bytes 50855936 | tf_op jit(solution)/shard_map/add | solution.py:198
  128.5 4.2 %slice_subtract_fusion.6 = f32[32,133,128]{2,1,0:T(8,128)} fusion(f32[32,128,128]{2,1,0:T(8,128)} %multiply_add_fusion.16), kind=kLoop, calls=%fused_computation.202 | loop fusion | flops 544768 | bytes 4276224 | tf_op jit(solution)/shard_map/sub | solution.py:102
  134.6 3.9 %collective-permute-start.7 = (f32[3,128,128]{2,1,0:T(8,128)S(1)}, f32[3,128,128]{2,1,0:T(8,128)S(1)}, u32[]{:S(2)}, u32[]{:S(2)}) collective-permute-start(f32[3,128,128]{2,1,0:T(8,128)S(1)} %get-tuple-element.4), channel_id=1, source_target_pairs={{0,1},{1,2},{2,3},{3,4},{4,5},{5,6},{6,7},{7,8},{8,9},{9,10},{10,1... | collective-permute-start | bytes 589832 | tf_op jit(solution)/shard_map/ppermute | solution.py:24
  138.5 4.2 %fusion.4 = f32[32,128,133]{2,1,0:T(8,128)} fusion(f32[32,128,128]{2,1,0:T(8,128)S(1)} %copy-done.5), kind=kLoop, calls=%fused_computation.68 | loop fusion | flops 544768 | bytes 4276224 | tf_op jit(solution)/shard_map/sub | solution.py:102
  146.2 48.8 %multiply_add_fusion.8 = f32[32,128,128]{2,1,0:T(8,128)} fusion(f32[32,128,128]{2,1,0:T(8,128)} %multiply_add_fusion.16, f32[32,128,133]{2,1,0:T(8,128)} %fusion.4, f32[32,133,128]{2,1,0:T(8,128)} %slice_subtract_fusion.6, f32[37,128,128]{2,1,0:T(8,128)} %slice_subtract_fusion.1, f32[32,128,128]{2,1,0:T(8,128)} %slice.670, f32[34,128,128]{2,1,0:T(8,128)} %slice.696, ...), kind=kLoop, calls=%fused_computation.554 | loop fusion | flops 239075328 | bytes 52953088 | tf_op jit(solution)/shard_map/add | solution.py:199
  196.1 4.2 %slice_subtract_fusion.5 = f32[32,133,128]{2,1,0:T(8,128)} fusion(f32[32,128,128]{2,1,0:T(8,128)} %multiply_add_fusion.8), kind=kLoop, calls=%fused_computation.201 | loop fusion | flops 544768 | bytes 4276224 | tf_op jit(solution)/shard_map/sub | solution.py:102
  202.2 3.9 %collective-permute-start.9 = (f32[3,128,128]{2,1,0:T(8,128)S(1)}, f32[3,128,128]{2,1,0:T(8,128)S(1)}, u32[]{:S(2)}, u32[]{:S(2)}) collective-permute-start(f32[3,128,128]{2,1,0:T(8,128)S(1)} %get-tuple-element.2), channel_id=1, source_target_pairs={{0,1},{1,2},{2,3},{3,4},{4,5},{5,6},{6,7},{7,8},{8,9},{9,10},{10,1... | collective-permute-start | bytes 589832 | tf_op jit(solution)/shard_map/ppermute | solution.py:24
  206.1 4.2 %fusion.5 = f32[32,128,133]{2,1,0:T(8,128)} fusion(f32[32,128,128]{2,1,0:T(8,128)S(1)} %copy-done.4), kind=kLoop, calls=%fused_computation.69 | loop fusion | flops 544768 | bytes 4276224 | tf_op jit(solution)/shard_map/sub | solution.py:102
  213.9 49.6 %multiply_add_fusion = f32[32,128,128]{2,1,0:T(8,128)} fusion(f32[32,128,128]{2,1,0:T(8,128)} %multiply_add_fusion.8, f32[32,128,133]{2,1,0:T(8,128)} %fusion.5, f32[32,133,128]{2,1,0:T(8,128)} %slice_subtract_fusion.5, f32[37,128,128]{2,1,0:T(8,128)} %slice_subtract_fusion, f32[32,128,128]{2,1,0:T(8,128)} %slice.670, f32[34,128,128]{2,1,0:T(8,128)} %slice.719, ...), kind=kLoop, calls=%fused_computation.504 | loop fusion | flops 239075328 | bytes 52953088 | tf_op jit(solution)/shard_map/add | solution.py:200
  (53 shorter events, 30.1 us)
Async XLA Ops:
  0.6 1.6 copy-start
  0.6 4.4 %copy-start.8 = (f32[128,128,1]{1,0,2:T(8,128)S(1)}, f32[128,128,1]{1,0,2:T(8,128)}, u32[]{:S(2)}) copy-start(f32[128,128,1]{1,0,2:T(8,128)} %constant.140) | copy-start | bytes 196612
  7.0 1.3 copy-start.6
  8.3 7.8 %copy-start.3 = (f32[32,128,128]{2,1,0:T(8,128)S(1)}, f32[32,128,128]{2,1,0:T(8,128)}, u32[]{:S(2)}) copy-start(f32[32,128,128]{2,1,0:T(8,128)} %param.6) | copy-start | bytes 6291460
  9.6 29.4 %collective-permute-start = (f32[12,128,128]{1,2,0:T(8,128)}, f32[12,128,128]{1,2,0:T(8,128)S(1)}, u32[]{:S(2)}, u32[]{:S(2)}) collective-permute-start(f32[12,128,128]{1,2,0:T(8,128)} %get-tuple-element.10), channel_id=1, source_target_pairs={{0,1},{1,2},{2,3},{3,4},{4,5},{5,6},{6,7},{7,8},{8,9},{9,10},{10,1... | collective-permute-start | bytes 2359304 | tf_op jit(solution)/shard_map/ppermute | solution.py:16
  14.1 24.9 %collective-permute-start.1 = (f32[12,128,128]{1,2,0:T(8,128)}, f32[12,128,128]{1,2,0:T(8,128)}, u32[]{:S(2)}, u32[]{:S(2)}) collective-permute-start(f32[12,128,128]{1,2,0:T(8,128)} %get-tuple-element.11), channel_id=1, source_target_pairs={{1,0},{2,1},{3,2},{4,3},{5,4},{6,5},{7,6},{8,7},{9,8},{10,9},{11,1... | collective-permute-start | bytes 2359304 | tf_op jit(solution)/shard_map/ppermute | solution.py:16
  16.8 19.2 %collective-permute-start.5 = (f32[3,128,128]{2,1,0:T(8,128)}, f32[3,128,128]{2,1,0:T(8,128)S(1)}, u32[]{:S(2)}, u32[]{:S(2)}) collective-permute-start(f32[3,128,128]{2,1,0:T(8,128)} %get-tuple-element.7), channel_id=1, source_target_pairs={{0,1},{1,2},{2,3},{3,4},{4,5},{5,6},{6,7},{7,8},{8,9},{9,10},{10,1... | collective-permute-start | bytes 589832 | tf_op jit(solution)/shard_map/ppermute | solution.py:24
  20.4 17.9 %collective-permute-start.4 = (f32[3,128,128]{2,1,0:T(8,128)S(1)}, f32[3,128,128]{2,1,0:T(8,128)S(1)}, u32[]{:S(2)}, u32[]{:S(2)}) collective-permute-start(f32[3,128,128]{2,1,0:T(8,128)S(1)} %get-tuple-element.6), channel_id=1, source_target_pairs={{1,0},{2,1},{3,2},{4,3},{5,4},{6,5},{7,6},{8,7},{9,8},{10,9},{11,1... | collective-permute-start | bytes 589832 | tf_op jit(solution)/shard_map/ppermute | solution.py:27
  36.7 2.3 copy-start.7
  42.4 5.3 %copy-start.9 = (f32[32,56]{1,0:T(8,128)S(1)}, f32[32,56]{1,0:T(8,128)}, u32[]{:S(2)}) copy-start(f32[32,56]{1,0:T(8,128)} %constant.117.clone) | copy-start | bytes 21508
  54.1 14.4 %collective-permute-start.2 = (f32[2,128,128]{2,1,0:T(8,128)S(1)}, f32[2,128,128]{2,1,0:T(8,128)S(1)}, u32[]{:S(2)}, u32[]{:S(2)}) collective-permute-start(f32[2,128,128]{2,1,0:T(8,128)S(1)} %bitcast.32), channel_id=1, source_target_pairs={{1,0},{2,1},{3,2},{4,3},{5,4},{6,5},{7,6},{8,7},{9,8},{10,9},{11,1... | collective-permute-start | bytes 393224 | tf_op jit(solution)/shard_map/ppermute | solution.py:27
  56.0 12.5 %collective-permute-start.3 = (f32[2,128,128]{2,1,0:T(8,128)S(1)}, f32[2,128,128]{2,1,0:T(8,128)S(1)}, u32[]{:S(2)}, u32[]{:S(2)}) collective-permute-start(f32[2,128,128]{2,1,0:T(8,128)S(1)} %bitcast.33), channel_id=1, source_target_pairs={{0,1},{1,2},{2,3},{3,4},{4,5},{5,6},{6,7},{7,8},{8,9},{9,10},{10,1... | collective-permute-start | bytes 393224 | tf_op jit(solution)/shard_map/ppermute | solution.py:24
  74.0 1.4 copy-start.2
  128.5 10.0 %copy-start.5 = (f32[32,128,128]{2,1,0:T(8,128)S(1)}, f32[32,128,128]{2,1,0:T(8,128)}, u32[]{:S(2)}) copy-start(f32[32,128,128]{2,1,0:T(8,128)} %multiply_add_fusion.16) | copy-start | bytes 6291460
  132.7 10.0 %collective-permute-start.6 = (f32[3,128,128]{2,1,0:T(8,128)S(1)}, f32[3,128,128]{2,1,0:T(8,128)S(1)}, u32[]{:S(2)}, u32[]{:S(2)}) collective-permute-start(f32[3,128,128]{2,1,0:T(8,128)S(1)} %get-tuple-element.5), channel_id=1, source_target_pairs={{1,0},{2,1},{3,2},{4,3},{5,4},{6,5},{7,6},{8,7},{9,8},{10,9},{11,1... | collective-permute-start | bytes 589832 | tf_op jit(solution)/shard_map/ppermute | solution.py:27
  134.6 8.1 %collective-permute-start.7 = (f32[3,128,128]{2,1,0:T(8,128)S(1)}, f32[3,128,128]{2,1,0:T(8,128)S(1)}, u32[]{:S(2)}, u32[]{:S(2)}) collective-permute-start(f32[3,128,128]{2,1,0:T(8,128)S(1)} %get-tuple-element.4), channel_id=1, source_target_pairs={{0,1},{1,2},{2,3},{3,4},{4,5},{5,6},{6,7},{7,8},{8,9},{9,10},{10,1... | collective-permute-start | bytes 589832 | tf_op jit(solution)/shard_map/ppermute | solution.py:24
  196.1 10.0 %copy-start.4 = (f32[32,128,128]{2,1,0:T(8,128)S(1)}, f32[32,128,128]{2,1,0:T(8,128)}, u32[]{:S(2)}) copy-start(f32[32,128,128]{2,1,0:T(8,128)} %multiply_add_fusion.8) | copy-start | bytes 6291460
  200.2 10.0 %collective-permute-start.8 = (f32[3,128,128]{2,1,0:T(8,128)S(1)}, f32[3,128,128]{2,1,0:T(8,128)S(1)}, u32[]{:S(2)}, u32[]{:S(2)}) collective-permute-start(f32[3,128,128]{2,1,0:T(8,128)S(1)} %get-tuple-element.3), channel_id=1, source_target_pairs={{1,0},{2,1},{3,2},{4,3},{5,4},{6,5},{7,6},{8,7},{9,8},{10,9},{11,1... | collective-permute-start | bytes 589832 | tf_op jit(solution)/shard_map/ppermute | solution.py:27
  202.2 8.1 %collective-permute-start.9 = (f32[3,128,128]{2,1,0:T(8,128)S(1)}, f32[3,128,128]{2,1,0:T(8,128)S(1)}, u32[]{:S(2)}, u32[]{:S(2)}) collective-permute-start(f32[3,128,128]{2,1,0:T(8,128)S(1)} %get-tuple-element.2), channel_id=1, source_target_pairs={{0,1},{1,2},{2,3},{3,4},{4,5},{5,6},{6,7},{7,8},{8,9},{9,10},{10,1... | collective-permute-start | bytes 589832 | tf_op jit(solution)/shard_map/ppermute | solution.py:24
  213.9 49.6 %copy-start.1 = (f32[32,128,128]{2,1,0:T(8,128)S(1)}, f32[32,128,128]{2,1,0:T(8,128)}, u32[]{:S(2)}) copy-start(f32[32,128,128]{2,1,0:T(8,128)} %param.5) | copy-start | bytes 6291460
where the time goes:
time: 268 us; the launch traced here: 264 us
  other arithmetic  189 us (71%)
  starting transfers between devices  30.4 us (11%)
  local copies, waits for them, and re-layouts  25.4 us (9%)
  matrix products  11 us (4%)
  waiting for transfers between devices  7.23 us (3%)
    add x1, other arithmetic, shards(): section_one = level_set + 0.1 * rate_of(level_set)  50.5 us
    add x1, other arithmetic, shards(): 1.0 / 3.0 * level_set  49.6 us
    add x1, other arithmetic, shards(): 0.75 * level_set + 0.25 * (section_one + 0.1 * rate_of(section_one))  48.8 us
    sub x9, other arithmetic, upwind(): lax.slice_in_dim(padded, 1, padded.shape[axis], axis=axis)  30.3 us
    ppermute x4, starting transfers between devices, extended_2(): lax.ppermute(lax.slice_in_dim(block, block.shape[dim] - width, None, axis...  15.8 us
    ppermute x4, starting transfers between devices, extended_2(): lax.ppermute(lax.slice_in_dim(block, 0, width, axis=dim), axis, backward)  8.18 us
    ppermute x4, waiting for transfers between devices, extended_2(): lax.ppermute(lax.slice_in_dim(block, block.shape[dim] - width, None, axis...  7.22 us
    unnamed x26, local copies, waits for them, and re-layouts  7.18 us
  transfers between devices with their start and end apart: 10, of which 1 were waited for; matrix products, arithmetic and copies ran while one was open for 10% of the time, Pallas kernels for 0%

commit v1 on v0

--- a/solution.py
+++ b/solution.py
@@ -5,6 +5,8 @@
 import jax
 import jax.numpy as jnp
 from jax import lax
+from jax.experimental import pallas as pl
+from jax.experimental.pallas import tpu as pltpu
 from jax.sharding import PartitionSpec as P
 
 RADIUS = 12
@@ -75,9 +77,9 @@
 
 
 def weno(first, second, third, fourth, fifth):
-    cand_one = (2.0 * first - 7.0 * second + 11.0 * third) / 6.0
-    cand_two = (-second + 5.0 * third + 2.0 * fourth) / 6.0
-    cand_three = (2.0 * third + 5.0 * fourth - fifth) / 6.0
+    cand_one = 2.0 * first - 7.0 * second + 11.0 * third
+    cand_two = -second + 5.0 * third + 2.0 * fourth
+    cand_three = 2.0 * third + 5.0 * fourth - fifth
     part_a = first - 2.0 * second + third
     part_b = first - 4.0 * second + 3.0 * third
     smooth_one = 13.0 / 12.0 * part_a * part_a + 0.25 * part_b * part_b
@@ -90,76 +92,118 @@
     denom_one = 1e-06 + smooth_one
     denom_two = 1e-06 + smooth_two
     denom_three = 1e-06 + smooth_three
-    weight_one = 0.1 / (denom_one * denom_one)
-    weight_two = 0.6 / (denom_two * denom_two)
-    weight_three = 0.3 / (denom_three * denom_three)
+    square_one = denom_one * denom_one
+    square_two = denom_two * denom_two
+    square_three = denom_three * denom_three
+    weight_one = 0.1 * (square_two * square_three)
+    weight_two = 0.6 * (square_one * square_three)
+    weight_three = 0.3 * (square_one * square_two)
     return (weight_one * cand_one + weight_two * cand_two + weight_three * cand_three) / (
-        weight_one + weight_two + weight_three
+        6.0 * (weight_one + weight_two + weight_three)
     )
 
 
-def upwind(padded, axis, count):
-    diffs = lax.slice_in_dim(padded, 1, padded.shape[axis], axis=axis) - lax.slice_in_dim(
-        padded, 0, padded.shape[axis] - 1, axis=axis
-    )
-    pieces = [lax.slice_in_dim(diffs, offset, offset + count, axis=axis) for offset in range(6)]
-    minus = weno(pieces[0], pieces[1], pieces[2], pieces[3], pieces[4])
-    plus = weno(pieces[5], pieces[4], pieces[3], pieces[2], pieces[1])
-    return (minus, plus)
-
-
-def rates(padded, edge, slope):
-    count = padded.shape[0] - 6
-    field = padded[3:-3]
-    rows_y = field.shape[1]
-    rows_z = field.shape[2]
-    minus_x, plus_x = upwind(padded, 0, count)
-    minus_y, plus_y = upwind(pad_axis(field, 1, 3), 1, rows_y)
-    minus_z, plus_z = upwind(pad_axis(field, 2, 3), 2, rows_z)
-    near = jnp.pad(padded[2:-2], ((0, 0), (1, 1), (1, 1)))
-
-    def beside_all(step_x, step_y, step_z):
-        return near[
-            1 + step_x : 1 + step_x + count,
-            1 + step_y : 1 + step_y + rows_y,
-            1 + step_z : 1 + step_z + rows_z,
-        ]
-
-    centre = beside_all(0, 0, 0)
-    first_x = (beside_all(1, 0, 0) - beside_all(-1, 0, 0)) * 0.5
-    first_y = (beside_all(0, 1, 0) - beside_all(0, -1, 0)) * 0.5
-    first_z = (beside_all(0, 0, 1) - beside_all(0, 0, -1)) * 0.5
-    second_xx = beside_all(1, 0, 0) - 2.0 * centre + beside_all(-1, 0, 0)
-    second_yy = beside_all(0, 1, 0) - 2.0 * centre + beside_all(0, -1, 0)
-    second_zz = beside_all(0, 0, 1) - 2.0 * centre + beside_all(0, 0, -1)
-    mixed_xy = (
-        beside_all(1, 1, 0) - beside_all(1, -1, 0) - beside_all(-1, 1, 0) + beside_all(-1, -1, 0)
-    ) * 0.25
-    mixed_xz = (
-        beside_all(1, 0, 1) - beside_all(1, 0, -1) - beside_all(-1, 0, 1) + beside_all(-1, 0, -1)
-    ) * 0.25
-    mixed_yz = (
-        beside_all(0, 1, 1) - beside_all(0, 1, -1) - beside_all(0, -1, 1) + beside_all(0, -1, -1)
-    ) * 0.25
-    square_x = first_x * first_x
-    square_y = first_y * first_y
-    square_z = first_z * first_z
-    numerator = (
-        second_xx * (square_y + square_z)
-        + second_yy * (square_x + square_z)
-        + second_zz * (square_x + square_y)
-    )
-    numerator = numerator - 2.0 * (
-        first_x * first_y * mixed_xy + first_x * first_z * mixed_xz + first_y * first_z * mixed_yz
-    )
-    curvature = numerator / (square_x + square_y + square_z + 1.0)
-    speed_x = -slope[0]
-    speed_y = -slope[1]
-    speed_z = -slope[2]
-    transport = jnp.maximum(speed_x, 0.0) * minus_x + jnp.minimum(speed_x, 0.0) * plus_x
-    transport = transport + jnp.maximum(speed_y, 0.0) * minus_y + jnp.minimum(speed_y, 0.0) * plus_y
-    transport = transport + jnp.maximum(speed_z, 0.0) * minus_z + jnp.minimum(speed_z, 0.0) * plus_z
-    return edge * curvature - transport
+def upwind(values, speed):
+    diffs = [values[k + 1] - values[k] for k in range(6)]
+    ahead = speed > 0.0
+    chosen = [jnp.where(ahead, diffs[k], diffs[5 - k]) for k in range(5)]
+    return speed * weno(*chosen)
+
+
+SUB = 8
+HALO = 3
+
+
+def stage_kernel(scale_level, scale_step, rows_block):
+    def kernel(p_ref, edge_ref, sx_ref, sy_ref, sz_ref, ls_ref, out_ref):
+        rows_y = out_ref.shape[1]
+        rows_z = out_ref.shape[2]
+        block = pl.program_id(0)
+        lane = lax.broadcasted_iota(jnp.int32, (SUB, rows_z), 1)
+
+        def along_z(tile, step):
+            moved = pltpu.roll(tile, (-step) % rows_z, 1)
+            keep = (lane + step >= 0) & (lane + step < rows_z)
+            return jnp.where(keep, moved, 0.0)
+
+        def row(r, carry):
+            centre_row = block * rows_block + r + HALO
+            for chunk in range(rows_y // SUB):
+                top = SUB + chunk * SUB
+
+                def at(step_x, step_y):
+                    return p_ref[centre_row + step_x, pl.ds(top + step_y, SUB), :]
+
+                centre = at(0, 0)
+                line_x = [at(k, 0) for k in range(-HALO, HALO + 1)]
+                line_y = [at(0, k) for k in range(-HALO, HALO + 1)]
+                line_z = [along_z(centre, k) for k in range(-HALO, HALO + 1)]
+                here = pl.ds(chunk * SUB, SUB)
+                speed_x = -sx_ref[r, here, :]
+                speed_y = -sy_ref[r, here, :]
+                speed_z = -sz_ref[r, here, :]
+                flow_x = upwind(line_x, speed_x)
+                flow_y = upwind(line_y, speed_y)
+                flow_z = upwind(line_z, speed_z)
+                up_x = line_x[HALO + 1]
+                down_x = line_x[HALO - 1]
+                up_y = line_y[HALO + 1]
+                down_y = line_y[HALO - 1]
+                up_z = line_z[HALO + 1]
+                down_z = line_z[HALO - 1]
+                first_x = (up_x - down_x) * 0.5
+                first_y = (up_y - down_y) * 0.5
+                first_z = (up_z - down_z) * 0.5
+                second_xx = up_x - 2.0 * centre + down_x
+                second_yy = up_y - 2.0 * centre + down_y
+                second_zz = up_z - 2.0 * centre + down_z
+                mixed_xy = (at(1, 1) - at(1, -1) - at(-1, 1) + at(-1, -1)) * 0.25
+                mixed_xz = (
+                    along_z(up_x, 1) - along_z(up_x, -1) - along_z(down_x, 1) + along_z(down_x, -1)
+                ) * 0.25
+                mixed_yz = (
+                    along_z(up_y, 1) - along_z(up_y, -1) - along_z(down_y, 1) + along_z(down_y, -1)
+                ) * 0.25
+                square_x = first_x * first_x
+                square_y = first_y * first_y
+                square_z = first_z * first_z
+                numerator = (
+                    second_xx * (square_y + square_z)
+                    + second_yy * (square_x + square_z)
+                    + second_zz * (square_x + square_y)
+                )
+                numerator = numerator - 2.0 * (
+                    first_x * first_y * mixed_xy
+                    + first_x * first_z * mixed_xz
+                    + first_y * first_z * mixed_yz
+                )
+                curvature = numerator / (square_x + square_y + square_z + 1.0)
+                transport = flow_x + flow_y + flow_z
+                rate = edge_ref[r, here, :] * curvature - transport
+                moved = centre + 0.1 * rate
+                if scale_level is None:
+                    out_ref[r, here, :] = moved
+                else:
+                    out_ref[r, here, :] = scale_level * ls_ref[r, here, :] + scale_step * moved
+            return carry
+
+        lax.fori_loop(0, rows_block, row, 0)
+
+    return kernel
+
+
+def stage(padded, edge, slope, level_set, scale_level, scale_step):
+    rows, rows_y, rows_z = level_set.shape
+    rows_block = SUB if rows % SUB == 0 else rows
+    whole = pl.BlockSpec(padded.shape, lambda i: (0, 0, 0))
+    part = pl.BlockSpec((rows_block, rows_y, rows_z), lambda i: (i, 0, 0))
+    return pl.pallas_call(
+        stage_kernel(scale_level, scale_step, rows_block),
+        grid=(rows // rows_block,),
+        in_specs=[whole, part, part, part, part, part],
+        out_specs=part,
+        out_shape=jax.ShapeDtypeStruct(level_set.shape, level_set.dtype),
+    )(padded, edge, slope[0], slope[1], slope[2], level_set)
 
 
 def shards(volume, level_set):
@@ -191,13 +235,14 @@
     edge = edge_wide[1:-1]
     slope = central_grads(edge_wide)
 
-    def rate_of(field):
-        padded = extended_2(field, (("gx", 0),), 3)
-        return rates(padded, edge, slope)
-
-    section_one = level_set + 0.1 * rate_of(level_set)
-    section_two = 0.75 * level_set + 0.25 * (section_one + 0.1 * rate_of(section_one))
-    advanced = 1.0 / 3.0 * level_set + 2.0 / 3.0 * (section_two + 0.1 * rate_of(section_two))
+    def step(field, scale_level, scale_step):
+        padded = extended_2(field, (("gx", 0),), HALO)
+        padded = jnp.pad(padded, ((0, 0), (SUB, SUB), (0, 0)))
+        return stage(padded, edge, slope, level_set, scale_level, scale_step)
+
+    section_one = step(level_set, None, None)
+    section_two = step(section_one, 0.75, 0.25)
+    advanced = step(section_two, 1.0 / 3.0, 2.0 / 3.0)
     return (edge, advanced)
 
 

time: 268 us -> 178 us (0.66); the launches traced: 264 us -> 177 us
  other arithmetic: 189 us -> 23.3 us
  Pallas kernels: 0 us -> 79.1 us
  waiting for transfers between devices: 7.23 us -> 20.8 us
  local copies, waits for them, and re-layouts: 25.4 us -> 13.8 us
    add x3 -> x0, other arithmetic: 149 us -> none  [the longest x1 50.5 us: shards(): section_one = level_set + 0.1 * rate_of(level_set)]
    pallas_call x0 -> x3, Pallas kernels: none -> 79.1 us  [stage(): pl.pallas_call(stage_kernel(scale_level, scale_step, rows_block), grid=(r...]
    sub x9 -> x0, other arithmetic: 30.3 us -> none  [upwind(): lax.slice_in_dim(padded, 1, padded.shape[axis], axis=axis)]
    ppermute x2, waiting for transfers between devices: 0.01 us -> 10.5 us  [shifted(): return lax.ppermute(block, axis, route)]
    ppermute x4, waiting for transfers between devices: 0.01 us -> 9.46 us  [extended_2(): lax.ppermute(lax.slice_in_dim(block, 0, width, axis=dim), axis, backward)]
    slice x5 -> x0, local copies, waits for them, and re-layouts: 8.8 us -> none  [the longest x3 6.53 us: rates(): near = jnp.pad(padded[2:-2], ((0, 0), (1, 1), (1, 1)))]
    concatenate x3 -> x4, other arithmetic: 3.45 us -> 11.4 us  [extended_2(): block = jnp.concatenate([low, block, high], axis=dim)]
    ppermute x4, waiting for transfers between devices: 7.22 us -> 0.84 us  [extended_2(): lax.ppermute(lax.slice_in_dim(block, block.shape[dim] - width, None, axis...]
  transfers between devices with their start and end apart: 10 -> 10, of which waited for: 1 -> 5; matrix products, arithmetic and copies ran while one was open for 10% -> 11% of each run, Pallas kernels for 0% -> 0%
where the time goes in v1:
time: 178 us; the launch traced here: 177 us
  Pallas kernels  79.1 us (44%)
  starting transfers between devices  28.5 us (16%)
  other arithmetic  23.3 us (13%)
  waiting for transfers between devices  20.8 us (12%)
  local copies, waits for them, and re-layouts  13.8 us (8%)
  matrix products  11.1 us (6%)
    pallas_call x3, Pallas kernels, stage(): pl.pallas_call(stage_kernel(scale_level, scale_step, rows_block), grid=(r...  79.1 us
    ppermute x4, starting transfers between devices, extended_2(): lax.ppermute(lax.slice_in_dim(block, block.shape[dim] - width, None, axis...  13.9 us
    concatenate x4, other arithmetic, extended_2(): block = jnp.concatenate([low, block, high], axis=dim)  11.4 us
    ppermute x2, waiting for transfers between devices, shifted(): return lax.ppermute(block, axis, route)  10.5 us
    ppermute x4, waiting for transfers between devices, extended_2(): lax.ppermute(lax.slice_in_dim(block, 0, width, axis=dim), axis, backward)  9.46 us
    ppermute x4, starting transfers between devices, extended_2(): lax.ppermute(lax.slice_in_dim(block, 0, width, axis=dim), axis, backward)  8.18 us
    ppermute x2, starting transfers between devices, shifted(): return lax.ppermute(block, axis, route)  6.43 us
    dot_general x1, matrix products, shards(): jnp.dot(band(rows, extended.shape[0], needed), extended.reshape(extended....  6.35 us
  transfers between devices with their start and end apart: 10, of which 5 were waited for; matrix products, arithmetic and copies ran while one was open for 11% of the time, Pallas kernels for 0%

profile of v1, /device:TPU:1, one launch (start us, length us, event | category | flops | bytes accessed | tf_op | source)
XLA Modules:
  0.0 177.4 jit_solution(14127976559421926612)
XLA Ops:
  2.2 2.8 %fusion.33 = f32[128,32,128]{2,0,1:T(8,128)S(1)} fusion(f32[128,128,1]{1,0,2:T(8,128)} %constant.40, f32[32,128,128]{2,1,0:T(8,128)S(1)} %copy-done), kind=kOutput, calls=%fused_computation.59 | convolution fusion | flops 805306368 | bytes 4259840 | tf_op jit(solution)/shard_map/dot_general | solution.py:212
  9.6 4.5 %collective-permute-start = (f32[12,128,128]{1,2,0:T(8,128)}, f32[12,128,128]{1,2,0:T(8,128)S(1)}, u32[]{:S(2)}, u32[]{:S(2)}) collective-permute-start(f32[12,128,128]{1,2,0:T(8,128)} %get-tuple-element.14), channel_id=1, source_target_pairs={{0,1},{1,2},{2,3},{3,4},{4,5},{5,6},{6,7},{7,8},{8,9},{9,10},{10,1... | collective-permute-start | bytes 2359304 | tf_op jit(solution)/shard_map/ppermute | solution.py:18
  14.1 1.9 %collective-permute-start.1 = (f32[12,128,128]{1,2,0:T(8,128)}, f32[12,128,128]{1,2,0:T(8,128)}, u32[]{:S(2)}, u32[]{:S(2)}) collective-permute-start(f32[12,128,128]{1,2,0:T(8,128)} %get-tuple-element.15), channel_id=1, source_target_pairs={{1,0},{2,1},{3,2},{4,3},{5,4},{6,5},{7,6},{8,7},{9,8},{10,9},{11,1... | collective-permute-start | bytes 2359304 | tf_op jit(solution)/shard_map/ppermute | solution.py:18
  17.7 3.6 %collective-permute-start.4 = (f32[3,128,128]{2,1,0:T(8,128)}, f32[3,128,128]{2,1,0:T(8,128)S(1)}, u32[]{:S(2)}, u32[]{:S(2)}) collective-permute-start(f32[3,128,128]{2,1,0:T(8,128)} %get-tuple-element.10), channel_id=1, source_target_pairs={{0,1},{1,2},{2,3},{3,4},{4,5},{5,6},{6,7},{7,8},{8,9},{9,10},{10,1... | collective-permute-start | bytes 589832 | tf_op jit(solution)/shard_map/ppermute | solution.py:26
  21.4 1.9 %collective-permute-start.5 = (f32[3,128,128]{2,1,0:T(8,128)S(1)}, f32[3,128,128]{2,1,0:T(8,128)S(1)}, u32[]{:S(2)}, u32[]{:S(2)}) collective-permute-start(f32[3,128,128]{2,1,0:T(8,128)S(1)} %get-tuple-element.11), channel_id=1, source_target_pairs={{1,0},{2,1},{3,2},{4,3},{5,4},{6,5},{7,6},{8,7},{9,8},{10,9},{11,1... | collective-permute-start | bytes 589832 | tf_op jit(solution)/shard_map/ppermute | solution.py:29
  23.3 10.5 %collective-permute-done = f32[12,128,128]{1,2,0:T(8,128)S(1)} collective-permute-done((f32[12,128,128]{1,2,0:T(8,128)}, f32[12,128,128]{1,2,0:T(8,128)S(1)}, u32[]{:S(2)}, u32[]{:S(2)}) %collective-permute-start) | collective-permute-done | bytes 786464 | tf_op jit(solution)/shard_map/ppermute | solution.py:18
  33.9 4.1 %pad_maximum_fusion = f32[56,128,128]{1,2,0:T(8,128)} fusion(f32[12,128,128]{1,2,0:T(8,128)} %collective-permute-done.1, f32[32,128,128]{1,2,0:T(8,128)} %copy-done.3, f32[12,128,128]{1,2,0:T(8,128)S(1)} %collective-permute-done), kind=kLoop, calls=%fused_computation.18 | loop fusion | flops 1835008 | bytes 7340032 | tf_op jit(solution)/shard_map/concatenate | solution.py:224
  37.9 5.3 %copy.7 = f32[56,128,128]{2,1,0:T(8,128)} copy(f32[56,128,128]{1,2,0:T(8,128)} %pad_maximum_fusion) | data formatting | bytes 7340032 | tf_op jit(solution)/shard_map/concatenate | solution.py:224
  43.2 6.3 %fusion.3 = f32[32,16384]{1,0:T(8,128)S(1)} fusion(f32[32,56]{1,0:T(8,128)S(1)} %copy-done.5, f32[7,8,128,128]{3,2,1,0:T(8,128)} %bitcast.30), kind=kOutput, calls=%fused_computation.15 | convolution fusion | flops 352321536 | bytes 5774336 | tf_op jit(solution)/shard_map/dot_general | solution.py:225
  49.7 1.9 %collective-permute-start.2 = (f32[2,128,128]{2,1,0:T(8,128)S(1)}, f32[2,128,128]{2,1,0:T(8,128)S(1)}, u32[]{:S(2)}, u32[]{:S(2)}) collective-permute-start(f32[2,128,128]{2,1,0:T(8,128)S(1)} %bitcast.33), channel_id=1, source_target_pairs={{1,0},{2,1},{3,2},{4,3},{5,4},{6,5},{7,6},{8,7},{9,8},{10,9},{11,1... | collective-permute-start | bytes 393224 | tf_op jit(solution)/shard_map/ppermute | solution.py:29
  51.6 4.5 %collective-permute-start.3 = (f32[2,128,128]{2,1,0:T(8,128)S(1)}, f32[2,128,128]{2,1,0:T(8,128)S(1)}, u32[]{:S(2)}, u32[]{:S(2)}) collective-permute-start(f32[2,128,128]{2,1,0:T(8,128)S(1)} %bitcast.32), channel_id=1, source_target_pairs={{0,1},{1,2},{2,3},{3,4},{4,5},{5,6},{6,7},{7,8},{8,9},{9,10},{10,1... | collective-permute-start | bytes 393224 | tf_op jit(solution)/shard_map/ppermute | solution.py:26
  58.3 2.9 %select_maximum_fusion = f32[34,130,130]{2,1,0:T(8,128)S(1)} fusion(f32[2,128,128]{2,1,0:T(8,128)S(1)} %collective-permute-done.2, f32[32,128,128]{2,1,0:T(8,128)S(1)} %bitcast.28, f32[2,128,128]{2,1,0:T(8,128)S(1)} %collective-permute-done.3), kind=kLoop, calls=%fused_computation.8 | loop fusion | flops 8619000 | bytes 4657696 | tf_op jit(solution)/shard_map/concatenate | solution.py:30
  61.2 2.6 %fusion.18 = f32[34,128,128]{2,1,0:T(8,128)S(1)} fusion(f32[34,130,130]{2,1,0:T(8,128)S(1)} %select_maximum_fusion, f32[32,128,128]{2,1,0:T(8,128)S(1)} %bitcast.29, f32[2,128,128]{2,1,0:T(8,128)S(1)} %collective-permute-done.3, f32[2,128,128]{2,1,0:T(8,128)S(1)} %collective-permute-done.2, pred[34]{0:T(512)(128)(4,1)S(1)} %compare_and_fusion), kind=kLoop, calls=%fused_computation.40 | loop fusion | flops 9469952 | bytes 13500450 | tf_op jit(solution)/shard_map/jit(_where)/select_n | solution.py:234
  65.6 3.4 %fusion.22 = (f32[32,128,128]{2,1,0:T(8,128)}, f32[32,128,128]{2,1,0:T(8,128)}) fusion(f32[32,128,128]{2,1,0:T(8,128)S(1)} %get-tuple-element.3.edge_ref), kind=kLoop, calls=%fused_computation.44 | loop fusion | flops 2097152 | bytes 6291456 | tf_op jit(solution)/shard_map/mul | solution.py:70
  69.1 26.2 %shard_map.68 = f32[32,128,128]{2,1,0:T(8,128)} custom-call(f32[38,144,128]{2,1,0:T(8,128)} %select_maximum_fusion.6.p_ref, f32[32,128,128]{2,1,0:T(8,128)} %copy-done.1, f32[32,128,128]{2,1,0:T(8,128)} %get-tuple-element.2.sx_ref, f32[32,128,128]{2,1,0:T(8,128)} %get-tuple-element.9.sy_ref, f32[32,128,128]{2,1,0:T(8,128)} %get-tuple-element.8.sz_ref, ...), custom_call_target="tpu_custom_call" | custom-call | tf_op jit(solution)/shard_map/pallas_call | solution.py:200
  96.4 3.9 %collective-permute-start.6 = (f32[3,128,128]{2,1,0:T(8,128)S(1)}, f32[3,128,128]{2,1,0:T(8,128)S(1)}, u32[]{:S(2)}, u32[]{:S(2)}) collective-permute-start(f32[3,128,128]{2,1,0:T(8,128)S(1)} %get-tuple-element.6), channel_id=1, source_target_pairs={{0,1},{1,2},{2,3},{3,4},{4,5},{5,6},{6,7},{7,8},{8,9},{9,10},{10,1... | collective-permute-start | bytes 589832 | tf_op jit(solution)/shard_map/ppermute | solution.py:26
  100.2 1.9 %collective-permute-start.7 = (f32[3,128,128]{2,1,0:T(8,128)S(1)}, f32[3,128,128]{2,1,0:T(8,128)S(1)}, u32[]{:S(2)}, u32[]{:S(2)}) collective-permute-start(f32[3,128,128]{2,1,0:T(8,128)S(1)} %get-tuple-element.7), channel_id=1, source_target_pairs={{1,0},{2,1},{3,2},{4,3},{5,4},{6,5},{7,6},{8,7},{9,8},{10,9},{11,1... | collective-permute-start | bytes 589832 | tf_op jit(solution)/shard_map/ppermute | solution.py:29
  102.8 4.4 %collective-permute-done.7 = f32[3,128,128]{2,1,0:T(8,128)S(1)} collective-permute-done((f32[3,128,128]{2,1,0:T(8,128)S(1)}, f32[3,128,128]{2,1,0:T(8,128)S(1)}, u32[]{:S(2)}, u32[]{:S(2)}) %collective-permute-start.7) | collective-permute-done | bytes 196640 | tf_op jit(solution)/shard_map/ppermute | solution.py:29
  107.2 3.3 %select_maximum_fusion.4.p_ref = f32[38,144,128]{2,1,0:T(8,128)} fusion(f32[3,128,128]{2,1,0:T(8,128)S(1)} %collective-permute-done.7, f32[32,128,128]{2,1,0:T(8,128)} %shard_map.68, f32[3,128,128]{2,1,0:T(8,128)S(1)} %collective-permute-done.6), kind=kLoop, calls=%fused_computation.21 | loop fusion | flops 5603328 | bytes 5292032 | tf_op jit(solution)/shard_map/concatenate | solution.py:30
  110.6 26.5 %shard_map.69 = f32[32,128,128]{2,1,0:T(8,128)} custom-call(f32[38,144,128]{2,1,0:T(8,128)} %select_maximum_fusion.4.p_ref, f32[32,128,128]{2,1,0:T(8,128)} %copy-done.1, f32[32,128,128]{2,1,0:T(8,128)} %get-tuple-element.2.sx_ref, f32[32,128,128]{2,1,0:T(8,128)} %get-tuple-element.9.sy_ref, f32[32,128,128]{2,1,0:T(8,128)} %get-tuple-element.8.sz_ref, ...), custom_call_target="tpu_custom_call" | custom-call | tf_op jit(solution)/shard_map/pallas_call | solution.py:200
  140.0 2.4 %collective-permute-start.9 = (f32[3,128,128]{2,1,0:T(8,128)S(1)}, f32[3,128,128]{2,1,0:T(8,128)S(1)}, u32[]{:S(2)}, u32[]{:S(2)}) collective-permute-start(f32[3,128,128]{2,1,0:T(8,128)S(1)} %get-tuple-element.5), channel_id=1, source_target_pairs={{1,0},{2,1},{3,2},{4,3},{5,4},{6,5},{7,6},{8,7},{9,8},{10,9},{11,1... | collective-permute-start | bytes 589832 | tf_op jit(solution)/shard_map/ppermute | solution.py:29
  142.6 5.1 %collective-permute-done.9 = f32[3,128,128]{2,1,0:T(8,128)S(1)} collective-permute-done((f32[3,128,128]{2,1,0:T(8,128)S(1)}, f32[3,128,128]{2,1,0:T(8,128)S(1)}, u32[]{:S(2)}, u32[]{:S(2)}) %collective-permute-start.9) | collective-permute-done | bytes 196640 | tf_op jit(solution)/shard_map/ppermute | solution.py:29
  147.6 3.3 %select_maximum_fusion.2.p_ref = f32[38,144,128]{2,1,0:T(8,128)} fusion(f32[3,128,128]{2,1,0:T(8,128)S(1)} %collective-permute-done.9, f32[32,128,128]{2,1,0:T(8,128)} %shard_map.69, f32[3,128,128]{2,1,0:T(8,128)S(1)} %collective-permute-done.8), kind=kLoop, calls=%fused_computation.19 | loop fusion | flops 5603328 | bytes 5292032 | tf_op jit(solution)/shard_map/concatenate | solution.py:30
  151.0 26.5 %shard_map.70 = f32[32,128,128]{2,1,0:T(8,128)} custom-call(f32[38,144,128]{2,1,0:T(8,128)} %select_maximum_fusion.2.p_ref, f32[32,128,128]{2,1,0:T(8,128)} %copy-done.1, f32[32,128,128]{2,1,0:T(8,128)} %get-tuple-element.2.sx_ref, f32[32,128,128]{2,1,0:T(8,128)} %get-tuple-element.9.sy_ref, f32[32,128,128]{2,1,0:T(8,128)} %get-tuple-element.8.sz_ref, ...), custom_call_target="tpu_custom_call" | custom-call | tf_op jit(solution)/shard_map/pallas_call | solution.py:200
  (32 shorter events, 16.8 us)
Async XLA Ops:
  0.6 1.6 copy-start
  0.6 4.4 %copy-start.4 = (f32[128,128,1]{1,0,2:T(8,128)S(1)}, f32[128,128,1]{1,0,2:T(8,128)}, u32[]{:S(2)}) copy-start(f32[128,128,1]{1,0,2:T(8,128)} %constant.40) | copy-start | bytes 196612
  7.0 1.3 copy-start.3
  9.6 24.3 %collective-permute-start = (f32[12,128,128]{1,2,0:T(8,128)}, f32[12,128,128]{1,2,0:T(8,128)S(1)}, u32[]{:S(2)}, u32[]{:S(2)}) collective-permute-start(f32[12,128,128]{1,2,0:T(8,128)} %get-tuple-element.14), channel_id=1, source_target_pairs={{0,1},{1,2},{2,3},{3,4},{4,5},{5,6},{6,7},{7,8},{8,9},{9,10},{10,1... | collective-permute-start | bytes 2359304 | tf_op jit(solution)/shard_map/ppermute | solution.py:18
  14.1 19.8 %collective-permute-start.1 = (f32[12,128,128]{1,2,0:T(8,128)}, f32[12,128,128]{1,2,0:T(8,128)}, u32[]{:S(2)}, u32[]{:S(2)}) collective-permute-start(f32[12,128,128]{1,2,0:T(8,128)} %get-tuple-element.15), channel_id=1, source_target_pairs={{1,0},{2,1},{3,2},{4,3},{5,4},{6,5},{7,6},{8,7},{9,8},{10,9},{11,1... | collective-permute-start | bytes 2359304 | tf_op jit(solution)/shard_map/ppermute | solution.py:18
  17.7 38.3 %collective-permute-start.4 = (f32[3,128,128]{2,1,0:T(8,128)}, f32[3,128,128]{2,1,0:T(8,128)S(1)}, u32[]{:S(2)}, u32[]{:S(2)}) collective-permute-start(f32[3,128,128]{2,1,0:T(8,128)} %get-tuple-element.10), channel_id=1, source_target_pairs={{0,1},{1,2},{2,3},{3,4},{4,5},{5,6},{6,7},{7,8},{8,9},{9,10},{10,1... | collective-permute-start | bytes 589832 | tf_op jit(solution)/shard_map/ppermute | solution.py:26
  21.4 34.7 %collective-permute-start.5 = (f32[3,128,128]{2,1,0:T(8,128)S(1)}, f32[3,128,128]{2,1,0:T(8,128)S(1)}, u32[]{:S(2)}, u32[]{:S(2)}) collective-permute-start(f32[3,128,128]{2,1,0:T(8,128)S(1)} %get-tuple-element.11), channel_id=1, source_target_pairs={{1,0},{2,1},{3,2},{4,3},{5,4},{6,5},{7,6},{8,7},{9,8},{10,9},{11,1... | collective-permute-start | bytes 589832 | tf_op jit(solution)/shard_map/ppermute | solution.py:29
  37.9 5.3 %copy-start.5 = (f32[32,56]{1,0:T(8,128)S(1)}, f32[32,56]{1,0:T(8,128)}, u32[]{:S(2)}) copy-start(f32[32,56]{1,0:T(8,128)} %constant.29.clone) | copy-start | bytes 21508
  43.2 12.9 %copy-start.2 = (f32[32,128,128]{2,1,0:T(8,128)S(1)}, f32[32,128,128]{2,1,0:T(8,128)}, u32[]{:S(2)}) copy-start(f32[32,128,128]{2,1,0:T(8,128)} %ls_ref.5) | copy-start | bytes 6291460
  49.7 8.6 %collective-permute-start.2 = (f32[2,128,128]{2,1,0:T(8,128)S(1)}, f32[2,128,128]{2,1,0:T(8,128)S(1)}, u32[]{:S(2)}, u32[]{:S(2)}) collective-permute-start(f32[2,128,128]{2,1,0:T(8,128)S(1)} %bitcast.33), channel_id=1, source_target_pairs={{1,0},{2,1},{3,2},{4,3},{5,4},{6,5},{7,6},{8,7},{9,8},{10,9},{11,1... | collective-permute-start | bytes 393224 | tf_op jit(solution)/shard_map/ppermute | solution.py:29
  51.6 6.7 %collective-permute-start.3 = (f32[2,128,128]{2,1,0:T(8,128)S(1)}, f32[2,128,128]{2,1,0:T(8,128)S(1)}, u32[]{:S(2)}, u32[]{:S(2)}) collective-permute-start(f32[2,128,128]{2,1,0:T(8,128)S(1)} %bitcast.32), channel_id=1, source_target_pairs={{0,1},{1,2},{2,3},{3,4},{4,5},{5,6},{6,7},{7,8},{8,9},{9,10},{10,1... | collective-permute-start | bytes 393224 | tf_op jit(solution)/shard_map/ppermute | solution.py:26
  65.6 3.5 %copy-start.1 = (f32[32,128,128]{2,1,0:T(8,128)}, f32[32,128,128]{2,1,0:T(8,128)S(1)}, u32[]{:S(2)}) copy-start(f32[32,128,128]{2,1,0:T(8,128)S(1)} %get-tuple-element.3.edge_ref) | copy-start | bytes 6291460
  96.4 6.5 %collective-permute-start.6 = (f32[3,128,128]{2,1,0:T(8,128)S(1)}, f32[3,128,128]{2,1,0:T(8,128)S(1)}, u32[]{:S(2)}, u32[]{:S(2)}) collective-permute-start(f32[3,128,128]{2,1,0:T(8,128)S(1)} %get-tuple-element.6), channel_id=1, source_target_pairs={{0,1},{1,2},{2,3},{3,4},{4,5},{5,6},{6,7},{7,8},{8,9},{9,10},{10,1... | collective-permute-start | bytes 589832 | tf_op jit(solution)/shard_map/ppermute | solution.py:26
  100.2 7.0 %collective-permute-start.7 = (f32[3,128,128]{2,1,0:T(8,128)S(1)}, f32[3,128,128]{2,1,0:T(8,128)S(1)}, u32[]{:S(2)}, u32[]{:S(2)}) collective-permute-start(f32[3,128,128]{2,1,0:T(8,128)S(1)} %get-tuple-element.7), channel_id=1, source_target_pairs={{1,0},{2,1},{3,2},{4,3},{5,4},{6,5},{7,6},{8,7},{9,8},{10,9},{11,1... | collective-permute-start | bytes 589832 | tf_op jit(solution)/shard_map/ppermute | solution.py:29
  138.1 4.5 %collective-permute-start.8 = (f32[3,128,128]{2,1,0:T(8,128)S(1)}, f32[3,128,128]{2,1,0:T(8,128)S(1)}, u32[]{:S(2)}, u32[]{:S(2)}) collective-permute-start(f32[3,128,128]{2,1,0:T(8,128)S(1)} %get-tuple-element.4), channel_id=1, source_target_pairs={{0,1},{1,2},{2,3},{3,4},{4,5},{5,6},{6,7},{7,8},{8,9},{9,10},{10,1... | collective-permute-start | bytes 589832 | tf_op jit(solution)/shard_map/ppermute | solution.py:26
  140.0 7.7 %collective-permute-start.9 = (f32[3,128,128]{2,1,0:T(8,128)S(1)}, f32[3,128,128]{2,1,0:T(8,128)S(1)}, u32[]{:S(2)}, u32[]{:S(2)}) collective-permute-start(f32[3,128,128]{2,1,0:T(8,128)S(1)} %get-tuple-element.5), channel_id=1, source_target_pairs={{1,0},{2,1},{3,2},{4,3},{5,4},{6,5},{7,6},{8,7},{9,8},{10,9},{11,1... | collective-permute-start | bytes 589832 | tf_op jit(solution)/shard_map/ppermute | solution.py:29

commit v2 on v1

--- a/solution.py
+++ b/solution.py
@@ -209,29 +209,25 @@
 def shards(volume, level_set):
     rows, rows_y, rows_z = volume.shape
     exact = lax.Precision.HIGHEST
+    halo = min(rows, RADIUS + 2)
+    low = shifted(volume[rows - halo :], "gx", 1)
+    high = shifted(volume[:halo], "gx", -1)
+    extended = jnp.concatenate([low, volume, high], axis=0)
+    wide = rows + 4
     blurred = jnp.dot(
-        volume.reshape(rows * rows_y, rows_z), band(rows_z, rows_z, 0).T, precision=exact
-    ).reshape(rows, rows_y, rows_z)
-    blurred = jnp.einsum("yv,xvz->xyz", band(rows_y, rows_y, 0), blurred, precision=exact)
-    reach = -(-RADIUS // rows)
-    jobs = []
-    needed = min(rows, RADIUS)
-    jobs.append((1, blurred[rows - needed :]))
-    jobs.append((-1, blurred[:needed]))
-    moved = [shifted(piece, "gx", signed_hops) for signed_hops, piece in jobs]
-    below = [moved[2 * (reach - 1)]]
-    above = [moved[1]]
-    extended = jnp.concatenate(below + [blurred] + above, axis=0)
-    blurred = jnp.dot(
-        band(rows, extended.shape[0], needed),
+        band(wide, extended.shape[0], halo - 2),
         extended.reshape(extended.shape[0], rows_y * rows_z),
         precision=exact,
-    ).reshape(rows, rows_y, rows_z)
-    wider = extended_2(blurred, (("gx", 0),), 2)
-    edge_wide = edge_from(wider)
-    positions = lax.axis_index("gx") * rows - 1 + jnp.arange(rows + 2, dtype=jnp.int32)
+    )
+    blurred = jnp.dot(
+        blurred.reshape(wide * rows_y, rows_z), band(rows_z, rows_z, 0).T, precision=exact
+    ).reshape(wide, rows_y, rows_z)
+    blurred = jnp.einsum("yv,xvz->xyz", band(rows_y, rows_y, 0), blurred, precision=exact)
+    positions = lax.axis_index("gx") * rows - 2 + jnp.arange(wide, dtype=jnp.int32)
     inside = (positions >= 0) & (positions < rows * lax.axis_size("gx"))
-    edge_wide = jnp.where(inside[:, None, None], edge_wide, 0.0)
+    blurred = jnp.where(inside[:, None, None], blurred, 0.0)
+    edge_wide = edge_from(blurred)
+    edge_wide = jnp.where(inside[1:-1, None, None], edge_wide, 0.0)
     edge = edge_wide[1:-1]
     slope = central_grads(edge_wide)
 

time: 178 us -> 163 us (0.916)
  starting transfers between devices: 28.5 us -> 22.5 us
  other arithmetic: 23.3 us -> 17.7 us
  waiting for transfers between devices: 20.8 us -> 25.9 us
  local copies, waits for them, and re-layouts: 13.8 us -> 9.61 us
  matrix products: 11.1 us -> 7.06 us
    ppermute x4 -> x3, waiting for transfers between devices: 0.84 us -> 17.1 us  [extended_2(): lax.ppermute(lax.slice_in_dim(block, block.shape[dim] - width, None, axis...]
    ppermute x2, waiting for transfers between devices: 10.5 us -> 0.01 us  [shifted(): return lax.ppermute(block, axis, route)]
    concatenate x1 -> x0, local copies, waits for them, and re-layouts: 5.26 us -> none  [shards(): extended = jnp.concatenate(below + [blurred] + above, axis=0)]
    dot_general x2, matrix products: 9.15 us -> 4.81 us  [the longest x1 2.55 us: shards(): jnp.dot(band(wide, extended.shape[0], halo - 2), extended.reshape(extende...]
    ppermute x4 -> x3, starting transfers between devices: 13.9 us -> 9.83 us  [extended_2(): lax.ppermute(lax.slice_in_dim(block, block.shape[dim] - width, None, axis...]
    concatenate x4 -> x3, other arithmetic: 11.4 us -> 8.54 us  [extended_2(): block = jnp.concatenate([low, block, high], axis=dim)]
    concatenate x1, other arithmetic: 4.06 us -> 1.84 us  [shards(): extended = jnp.concatenate([low, volume, high], axis=0)]
    ppermute x4 -> x3, starting transfers between devices: 8.18 us -> 6.25 us  [extended_2(): lax.ppermute(lax.slice_in_dim(block, 0, width, axis=dim), axis, backward)]
  transfers between devices with their start and end apart: 10 -> 8, of which waited for: 5 -> 5; matrix products, arithmetic and copies ran while one was open for 11% -> 2% of each run, Pallas kernels for 0% -> 0%
where the time goes in v2:
time: 163 us
  Pallas kernels  79.1 us (49%)
  waiting for transfers between devices  25.9 us (16%)
  starting transfers between devices  22.5 us (14%)
  other arithmetic  17.7 us (11%)
  local copies, waits for them, and re-layouts  9.61 us (6%)
  matrix products  7.06 us (4%)
    pallas_call x3, Pallas kernels, stage(): pl.pallas_call(stage_kernel(scale_level, scale_step, rows_block), grid=(r...  79.1 us
    ppermute x3, waiting for transfers between devices, extended_2(): lax.ppermute(lax.slice_in_dim(block, block.shape[dim] - width, None, axis...  17.1 us
    ppermute x3, starting transfers between devices, extended_2(): lax.ppermute(lax.slice_in_dim(block, block.shape[dim] - width, None, axis...  9.83 us
    ppermute x3, waiting for transfers between devices, extended_2(): lax.ppermute(lax.slice_in_dim(block, 0, width, axis=dim), axis, backward)  8.79 us
    concatenate x3, other arithmetic, extended_2(): block = jnp.concatenate([low, block, high], axis=dim)  8.54 us
    ppermute x2, starting transfers between devices, shifted(): return lax.ppermute(block, axis, route)  6.44 us
    ppermute x3, starting transfers between devices, extended_2(): lax.ppermute(lax.slice_in_dim(block, 0, width, axis=dim), axis, backward)  6.25 us
    unnamed x13, local copies, waits for them, and re-layouts  3.73 us
  transfers between devices with their start and end apart: 8, of which 5 were waited for; matrix products, arithmetic and copies ran while one was open for 2% of the time, Pallas kernels for 0%

profile of v2, /device:TPU:1, one launch (start us, length us, event | category | flops | bytes accessed | tf_op | source)
XLA Modules:
  0.0 162.8 jit_solution(18227586904184481282)
XLA Ops:
  0.6 2.7 %fusion.25 = (f32[14,128,128]{2,1,0:T(8,128)}, f32[14,128,128]{2,1,0:T(8,128)S(1)}) fusion(f32[32,128,128]{2,1,0:T(8,128)} %param.5), kind=kLoop, calls=%fused_computation.46 | loop fusion | bytes 3670016 | tf_op jit(solution)/shard_map/slice | solution.py:213
  3.3 4.5 %collective-permute-start = (f32[14,128,128]{2,1,0:T(8,128)}, f32[14,128,128]{2,1,0:T(8,128)}, u32[]{:S(2)}, u32[]{:S(2)}) collective-permute-start(f32[14,128,128]{2,1,0:T(8,128)} %get-tuple-element.12), channel_id=1, source_target_pairs={{0,1},{1,2},{2,3},{3,4},{4,5},{5,6},{6,7},{7,8},{8,9},{9,10},{10,1... | collective-permute-start | bytes 2752520 | tf_op jit(solution)/shard_map/ppermute | solution.py:18
  7.9 1.9 %collective-permute-start.1 = (f32[14,128,128]{2,1,0:T(8,128)S(1)}, f32[14,128,128]{2,1,0:T(8,128)}, u32[]{:S(2)}, u32[]{:S(2)}) collective-permute-start(f32[14,128,128]{2,1,0:T(8,128)S(1)} %get-tuple-element.13), channel_id=1, source_target_pairs={{1,0},{2,1},{3,2},{4,3},{5,4},{6,5},{7,6},{8,7},{9,8},{10,9},{11,1... | collective-permute-start | bytes 2752520 | tf_op jit(solution)/shard_map/ppermute | solution.py:18
  10.6 3.6 %collective-permute-start.2 = (f32[3,128,128]{2,1,0:T(8,128)}, f32[3,128,128]{2,1,0:T(8,128)S(1)}, u32[]{:S(2)}, u32[]{:S(2)}) collective-permute-start(f32[3,128,128]{2,1,0:T(8,128)} %get-tuple-element.10), channel_id=1, source_target_pairs={{0,1},{1,2},{2,3},{3,4},{4,5},{5,6},{6,7},{7,8},{8,9},{9,10},{10,1... | collective-permute-start | bytes 589832 | tf_op jit(solution)/shard_map/ppermute | solution.py:26
  14.2 1.9 %collective-permute-start.3 = (f32[3,128,128]{2,1,0:T(8,128)}, f32[3,128,128]{2,1,0:T(8,128)S(1)}, u32[]{:S(2)}, u32[]{:S(2)}) collective-permute-start(f32[3,128,128]{2,1,0:T(8,128)} %get-tuple-element.11), channel_id=1, source_target_pairs={{1,0},{2,1},{3,2},{4,3},{5,4},{6,5},{7,6},{8,7},{9,8},{10,9},{11,1... | collective-permute-start | bytes 589832 | tf_op jit(solution)/shard_map/ppermute | solution.py:29
  16.2 16.3 %collective-permute-done.2 = f32[3,128,128]{2,1,0:T(8,128)S(1)} collective-permute-done((f32[3,128,128]{2,1,0:T(8,128)}, f32[3,128,128]{2,1,0:T(8,128)S(1)}, u32[]{:S(2)}, u32[]{:S(2)}) %collective-permute-start.2) | collective-permute-done | bytes 196640 | tf_op jit(solution)/shard_map/ppermute | solution.py:26
  34.4 1.8 %pad_maximum_fusion = f32[60,128,128]{2,1,0:T(8,128)S(1)} fusion(f32[14,128,128]{2,1,0:T(8,128)} %collective-permute-done.1, f32[32,128,128]{2,1,0:T(8,128)S(1)} %copy-done.2, f32[14,128,128]{2,1,0:T(8,128)} %collective-permute-done), kind=kLoop, calls=%fused_computation.10 | loop fusion | flops 1966080 | bytes 7864320 | tf_op jit(solution)/shard_map/concatenate | solution.py:215
  36.7 2.4 %copy.9 = f32[8,8,128,128]{3,1,2,0:T(8,128)S(1)} copy(f32[8,8,128,128]{3,2,1,0:T(8,128)S(1)} %bitcast.14) | data formatting | bytes 8388608
  39.1 2.5 %fusion.26 = f32[36,16384]{1,0:T(8,128)S(1)} fusion(f32[36,60]{1,0:T(8,128)S(1)} %copy-done.4, f32[60,16384]{1,0:T(8,128)S(1)} %bitcast.15), kind=kOutput, calls=%fused_computation.47 | convolution fusion | flops 424673280 | bytes 6300096 | tf_op jit(solution)/shard_map/dot_general | solution.py:217
  42.5 2.3 %fusion.1 = f32[36,128,128]{1,2,0:T(8,128)S(1)} fusion(f32[128,128,1]{1,0,2:T(8,128)S(1)} %copy-done.3, f32[40,128,128]{2,1,0:T(8,128)S(1)} %bitcast.17), kind=kOutput, calls=%fused_computation.18 | convolution fusion | flops 905969664 | bytes 4784128 | tf_op jit(solution)/shard_map/dot_general | solution.py:222
  44.8 2.2 %select_bitcast_fusion = f32[36,128,128]{2,1,0:T(8,128)S(1)} fusion(f32[36,128,128]{1,2,0:T(8,128)S(1)} %fusion.1, f32[128,128,1]{1,0,2:T(8,128)S(1)} %copy-done.3, pred[36]{0:T(512)(128)(4,1)S(1)} %compare_and_fusion), kind=kOutput, calls=%fused_computation.20 | convolution fusion | flops 906559488 | bytes 4784164 | tf_op jit(solution)/shard_map/yv,xvz->xyz/dot_general | solution.py:225
  47.3 2.1 %fusion.16 = f32[34,128,128]{2,1,0:T(8,128)S(1)} fusion(f32[34,128,128]{2,1,0:T(8,128)S(1)} %slice.95, f32[36,128,128]{2,1,0:T(8,128)S(1)} %select_bitcast_fusion, pred[34]{0:T(512)(128)(4,1)S(1)} %slice.70), kind=kLoop, calls=%fused_computation.35 | loop fusion | flops 8355840 | bytes 8912930 | tf_op jit(solution)/shard_map/jit(_where)/select_n | solution.py:230
  51.2 3.4 %fusion.20 = (f32[32,128,128]{2,1,0:T(8,128)}, f32[32,128,128]{2,1,0:T(8,128)}) fusion(f32[32,128,128]{2,1,0:T(8,128)S(1)} %get-tuple-element.3.edge_ref), kind=kLoop, calls=%fused_computation.39 | loop fusion | flops 2097152 | bytes 6291456 | tf_op jit(solution)/shard_map/mul | solution.py:70
  54.6 26.2 %shard_map.68 = f32[32,128,128]{2,1,0:T(8,128)} custom-call(f32[38,144,128]{2,1,0:T(8,128)} %select_maximum_fusion.4.p_ref, f32[32,128,128]{2,1,0:T(8,128)} %copy-done, f32[32,128,128]{2,1,0:T(8,128)} %get-tuple-element.2.sx_ref, f32[32,128,128]{2,1,0:T(8,128)} %get-tuple-element.9.sy_ref, f32[32,128,128]{2,1,0:T(8,128)} %get-tuple-element.8.sz_ref, ...), custom_call_target="tpu_custom_call" | custom-call | tf_op jit(solution)/shard_map/pallas_call | solution.py:200
  81.9 4.3 %collective-permute-start.4 = (f32[3,128,128]{2,1,0:T(8,128)S(1)}, f32[3,128,128]{2,1,0:T(8,128)S(1)}, u32[]{:S(2)}, u32[]{:S(2)}) collective-permute-start(f32[3,128,128]{2,1,0:T(8,128)S(1)} %get-tuple-element.6), channel_id=1, source_target_pairs={{0,1},{1,2},{2,3},{3,4},{4,5},{5,6},{6,7},{7,8},{8,9},{9,10},{10,1... | collective-permute-start | bytes 589832 | tf_op jit(solution)/shard_map/ppermute | solution.py:26
  86.2 1.9 %collective-permute-start.5 = (f32[3,128,128]{2,1,0:T(8,128)S(1)}, f32[3,128,128]{2,1,0:T(8,128)S(1)}, u32[]{:S(2)}, u32[]{:S(2)}) collective-permute-start(f32[3,128,128]{2,1,0:T(8,128)S(1)} %get-tuple-element.7), channel_id=1, source_target_pairs={{1,0},{2,1},{3,2},{4,3},{5,4},{6,5},{7,6},{8,7},{9,8},{10,9},{11,1... | collective-permute-start | bytes 589832 | tf_op jit(solution)/shard_map/ppermute | solution.py:29
  88.8 4.4 %collective-permute-done.5 = f32[3,128,128]{2,1,0:T(8,128)S(1)} collective-permute-done((f32[3,128,128]{2,1,0:T(8,128)S(1)}, f32[3,128,128]{2,1,0:T(8,128)S(1)}, u32[]{:S(2)}, u32[]{:S(2)}) %collective-permute-start.5) | collective-permute-done | bytes 196640 | tf_op jit(solution)/shard_map/ppermute | solution.py:29
  93.2 3.4 %select_maximum_fusion.2.p_ref = f32[38,144,128]{2,1,0:T(8,128)} fusion(f32[3,128,128]{2,1,0:T(8,128)S(1)} %collective-permute-done.5, f32[32,128,128]{2,1,0:T(8,128)} %shard_map.68, f32[3,128,128]{2,1,0:T(8,128)S(1)} %collective-permute-done.4), kind=kLoop, calls=%fused_computation.13 | loop fusion | flops 5603328 | bytes 5292032 | tf_op jit(solution)/shard_map/concatenate | solution.py:30
  96.6 26.5 %shard_map.69 = f32[32,128,128]{2,1,0:T(8,128)} custom-call(f32[38,144,128]{2,1,0:T(8,128)} %select_maximum_fusion.2.p_ref, f32[32,128,128]{2,1,0:T(8,128)} %copy-done, f32[32,128,128]{2,1,0:T(8,128)} %get-tuple-element.2.sx_ref, f32[32,128,128]{2,1,0:T(8,128)} %get-tuple-element.9.sy_ref, f32[32,128,128]{2,1,0:T(8,128)} %get-tuple-element.8.sz_ref, ...), custom_call_target="tpu_custom_call" | custom-call | tf_op jit(solution)/shard_map/pallas_call | solution.py:200
  124.1 1.9 %collective-permute-start.6 = (f32[3,128,128]{2,1,0:T(8,128)S(1)}, f32[3,128,128]{2,1,0:T(8,128)S(1)}, u32[]{:S(2)}, u32[]{:S(2)}) collective-permute-start(f32[3,128,128]{2,1,0:T(8,128)S(1)} %get-tuple-element.4), channel_id=1, source_target_pairs={{0,1},{1,2},{2,3},{3,4},{4,5},{5,6},{6,7},{7,8},{8,9},{9,10},{10,1... | collective-permute-start | bytes 589832 | tf_op jit(solution)/shard_map/ppermute | solution.py:26
  126.0 2.4 %collective-permute-start.7 = (f32[3,128,128]{2,1,0:T(8,128)S(1)}, f32[3,128,128]{2,1,0:T(8,128)S(1)}, u32[]{:S(2)}, u32[]{:S(2)}) collective-permute-start(f32[3,128,128]{2,1,0:T(8,128)S(1)} %get-tuple-element.5), channel_id=1, source_target_pairs={{1,0},{2,1},{3,2},{4,3},{5,4},{6,5},{7,6},{8,7},{9,8},{10,9},{11,1... | collective-permute-start | bytes 589832 | tf_op jit(solution)/shard_map/ppermute | solution.py:29
  128.6 4.4 %collective-permute-done.7 = f32[3,128,128]{2,1,0:T(8,128)S(1)} collective-permute-done((f32[3,128,128]{2,1,0:T(8,128)S(1)}, f32[3,128,128]{2,1,0:T(8,128)S(1)}, u32[]{:S(2)}, u32[]{:S(2)}) %collective-permute-start.7) | collective-permute-done | bytes 196640 | tf_op jit(solution)/shard_map/ppermute | solution.py:29
  133.0 3.4 %select_maximum_fusion.p_ref = f32[38,144,128]{2,1,0:T(8,128)} fusion(f32[3,128,128]{2,1,0:T(8,128)S(1)} %collective-permute-done.7, f32[32,128,128]{2,1,0:T(8,128)} %shard_map.69, f32[3,128,128]{2,1,0:T(8,128)S(1)} %collective-permute-done.6), kind=kLoop, calls=%fused_computation.11 | loop fusion | flops 5603328 | bytes 5292032 | tf_op jit(solution)/shard_map/concatenate | solution.py:30
  136.4 26.5 %shard_map.70 = f32[32,128,128]{2,1,0:T(8,128)} custom-call(f32[38,144,128]{2,1,0:T(8,128)} %select_maximum_fusion.p_ref, f32[32,128,128]{2,1,0:T(8,128)} %copy-done, f32[32,128,128]{2,1,0:T(8,128)} %get-tuple-element.2.sx_ref, f32[32,128,128]{2,1,0:T(8,128)} %get-tuple-element.9.sy_ref, f32[32,128,128]{2,1,0:T(8,128)} %get-tuple-element.8.sz_ref, ...), custom_call_target="tpu_custom_call" | custom-call | tf_op jit(solution)/shard_map/pallas_call | solution.py:200
  (25 shorter events, 9.0 us)
Async XLA Ops:
  0.6 9.2 %copy-start.1 = (f32[32,128,128]{2,1,0:T(8,128)S(1)}, f32[32,128,128]{2,1,0:T(8,128)}, u32[]{:S(2)}) copy-start(f32[32,128,128]{2,1,0:T(8,128)} %ls_ref.5) | copy-start | bytes 6291460
  3.3 31.0 %collective-permute-start = (f32[14,128,128]{2,1,0:T(8,128)}, f32[14,128,128]{2,1,0:T(8,128)}, u32[]{:S(2)}, u32[]{:S(2)}) collective-permute-start(f32[14,128,128]{2,1,0:T(8,128)} %get-tuple-element.12), channel_id=1, source_target_pairs={{0,1},{1,2},{2,3},{3,4},{4,5},{5,6},{6,7},{7,8},{8,9},{9,10},{10,1... | collective-permute-start | bytes 2752520 | tf_op jit(solution)/shard_map/ppermute | solution.py:18
  7.9 26.5 %collective-permute-start.1 = (f32[14,128,128]{2,1,0:T(8,128)S(1)}, f32[14,128,128]{2,1,0:T(8,128)}, u32[]{:S(2)}, u32[]{:S(2)}) collective-permute-start(f32[14,128,128]{2,1,0:T(8,128)S(1)} %get-tuple-element.13), channel_id=1, source_target_pairs={{1,0},{2,1},{3,2},{4,3},{5,4},{6,5},{7,6},{8,7},{9,8},{10,9},{11,1... | collective-permute-start | bytes 2752520 | tf_op jit(solution)/shard_map/ppermute | solution.py:18
  10.6 22.0 %collective-permute-start.2 = (f32[3,128,128]{2,1,0:T(8,128)}, f32[3,128,128]{2,1,0:T(8,128)S(1)}, u32[]{:S(2)}, u32[]{:S(2)}) collective-permute-start(f32[3,128,128]{2,1,0:T(8,128)} %get-tuple-element.10), channel_id=1, source_target_pairs={{0,1},{1,2},{2,3},{3,4},{4,5},{5,6},{6,7},{7,8},{8,9},{9,10},{10,1... | collective-permute-start | bytes 589832 | tf_op jit(solution)/shard_map/ppermute | solution.py:26
  14.2 18.3 %collective-permute-start.3 = (f32[3,128,128]{2,1,0:T(8,128)}, f32[3,128,128]{2,1,0:T(8,128)S(1)}, u32[]{:S(2)}, u32[]{:S(2)}) collective-permute-start(f32[3,128,128]{2,1,0:T(8,128)} %get-tuple-element.11), channel_id=1, source_target_pairs={{1,0},{2,1},{3,2},{4,3},{5,4},{6,5},{7,6},{8,7},{9,8},{10,9},{11,1... | collective-permute-start | bytes 589832 | tf_op jit(solution)/shard_map/ppermute | solution.py:29
  16.2 18.1 %copy-start.2 = (f32[32,128,128]{2,1,0:T(8,128)S(1)}, f32[32,128,128]{2,1,0:T(8,128)}, u32[]{:S(2)}) copy-start(f32[32,128,128]{2,1,0:T(8,128)} %param.5) | copy-start | bytes 6291460
  36.7 2.4 %copy-start.4 = (f32[36,60]{1,0:T(8,128)S(1)}, f32[36,60]{1,0:T(8,128)}, u32[]{:S(2)}) copy-start(f32[36,60]{1,0:T(8,128)} %constant.28.clone) | copy-start | bytes 25924
  41.7 0.8 copy-start.3
  51.2 3.5 %copy-start = (f32[32,128,128]{2,1,0:T(8,128)}, f32[32,128,128]{2,1,0:T(8,128)S(1)}, u32[]{:S(2)}) copy-start(f32[32,128,128]{2,1,0:T(8,128)S(1)} %get-tuple-element.3.edge_ref) | copy-start | bytes 6291460
  81.9 6.9 %collective-permute-start.4 = (f32[3,128,128]{2,1,0:T(8,128)S(1)}, f32[3,128,128]{2,1,0:T(8,128)S(1)}, u32[]{:S(2)}, u32[]{:S(2)}) collective-permute-start(f32[3,128,128]{2,1,0:T(8,128)S(1)} %get-tuple-element.6), channel_id=1, source_target_pairs={{0,1},{1,2},{2,3},{3,4},{4,5},{5,6},{6,7},{7,8},{8,9},{9,10},{10,1... | collective-permute-start | bytes 589832 | tf_op jit(solution)/shard_map/ppermute | solution.py:26
  86.2 7.0 %collective-permute-start.5 = (f32[3,128,128]{2,1,0:T(8,128)S(1)}, f32[3,128,128]{2,1,0:T(8,128)S(1)}, u32[]{:S(2)}, u32[]{:S(2)}) collective-permute-start(f32[3,128,128]{2,1,0:T(8,128)S(1)} %get-tuple-element.7), channel_id=1, source_target_pairs={{1,0},{2,1},{3,2},{4,3},{5,4},{6,5},{7,6},{8,7},{9,8},{10,9},{11,1... | collective-permute-start | bytes 589832 | tf_op jit(solution)/shard_map/ppermute | solution.py:29
  124.1 4.5 %collective-permute-start.6 = (f32[3,128,128]{2,1,0:T(8,128)S(1)}, f32[3,128,128]{2,1,0:T(8,128)S(1)}, u32[]{:S(2)}, u32[]{:S(2)}) collective-permute-start(f32[3,128,128]{2,1,0:T(8,128)S(1)} %get-tuple-element.4), channel_id=1, source_target_pairs={{0,1},{1,2},{2,3},{3,4},{4,5},{5,6},{6,7},{7,8},{8,9},{9,10},{10,1... | collective-permute-start | bytes 589832 | tf_op jit(solution)/shard_map/ppermute | solution.py:26
  126.0 7.0 %collective-permute-start.7 = (f32[3,128,128]{2,1,0:T(8,128)S(1)}, f32[3,128,128]{2,1,0:T(8,128)S(1)}, u32[]{:S(2)}, u32[]{:S(2)}) collective-permute-start(f32[3,128,128]{2,1,0:T(8,128)S(1)} %get-tuple-element.5), channel_id=1, source_target_pairs={{1,0},{2,1},{3,2},{4,3},{5,4},{6,5},{7,6},{8,7},{9,8},{10,9},{11,1... | collective-permute-start | bytes 589832 | tf_op jit(solution)/shard_map/ppermute | solution.py:29

commit v3 on v2

--- a/solution.py
+++ b/solution.py
@@ -120,11 +120,16 @@
         rows_z = out_ref.shape[2]
         block = pl.program_id(0)
         lane = lax.broadcasted_iota(jnp.int32, (SUB, rows_z), 1)
+        keeps = {
+            step: (lane + step >= 0) & (lane + step < rows_z)
+            for step in range(-HALO, HALO + 1)
+            if step != 0
+        }
 
         def along_z(tile, step):
-            moved = pltpu.roll(tile, (-step) % rows_z, 1)
-            keep = (lane + step >= 0) & (lane + step < rows_z)
-            return jnp.where(keep, moved, 0.0)
+            if step == 0:
+                return tile
+            return jnp.where(keeps[step], pltpu.roll(tile, (-step) % rows_z, 1), 0.0)
 
         def row(r, carry):
             centre_row = block * rows_block + r + HALO
@@ -212,17 +217,24 @@
     halo = min(rows, RADIUS + 2)
     low = shifted(volume[rows - halo :], "gx", 1)
     high = shifted(volume[:halo], "gx", -1)
-    extended = jnp.concatenate([low, volume, high], axis=0)
+
+    def across(block):
+        count = block.shape[0]
+        flat = jnp.dot(
+            block.reshape(count * rows_y, rows_z), band(rows_z, rows_z, 0).T, precision=exact
+        ).reshape(count, rows_y, rows_z)
+        return jnp.einsum("yv,xvz->xyz", band(rows_y, rows_y, 0), flat, precision=exact)
+
     wide = rows + 4
-    blurred = jnp.dot(
-        band(wide, extended.shape[0], halo - 2),
-        extended.reshape(extended.shape[0], rows_y * rows_z),
-        precision=exact,
-    )
-    blurred = jnp.dot(
-        blurred.reshape(wide * rows_y, rows_z), band(rows_z, rows_z, 0).T, precision=exact
-    ).reshape(wide, rows_y, rows_z)
-    blurred = jnp.einsum("yv,xvz->xyz", band(rows_y, rows_y, 0), blurred, precision=exact)
+
+    def along_x(block, shift):
+        count = block.shape[0]
+        return jnp.dot(
+            band(wide, count, shift), block.reshape(count, rows_y * rows_z), precision=exact
+        ).reshape(wide, rows_y, rows_z)
+
+    blurred = along_x(across(volume), -2)
+    blurred = blurred + along_x(across(low), halo - 2) + along_x(across(high), -(rows + 2))
     positions = lax.axis_index("gx") * rows - 2 + jnp.arange(wide, dtype=jnp.int32)
     inside = (positions >= 0) & (positions < rows * lax.axis_size("gx"))
     blurred = jnp.where(inside[:, None, None], blurred, 0.0)

time: 163 us -> 165 us (1.012)
  matrix products: 7.06 us -> 21.4 us
  waiting for transfers between devices: 25.9 us -> 11.8 us
  local copies, waits for them, and re-layouts: 9.61 us -> 11.8 us
  other arithmetic: 17.7 us -> 15.9 us
    ppermute x3, waiting for transfers between devices: 17.1 us -> 0.84 us  [extended_2(): lax.ppermute(lax.slice_in_dim(block, block.shape[dim] - width, None, axis...]
    dot_general x3 -> x9, matrix products: 7.06 us -> 21.4 us  [the longest x3 11.7 us: along_x(): jnp.dot(band(wide, count, shift), block.reshape(count, rows_y * rows_z),...]
    transpose x0 -> x3, local copies, waits for them, and re-layouts: none -> 2.41 us  [across(): jnp.einsum('yv,xvz->xyz', band(rows_y, rows_y, 0), flat, precision=exact)]
    concatenate x1 -> x0, other arithmetic: 1.84 us -> none  [shards(): extended = jnp.concatenate([low, volume, high], axis=0)]
    unnamed x13 -> x21, local copies, waits for them, and re-layouts: 3.73 us -> 2.94 us
  transfers between devices with their start and end apart: 8 -> 8, of which waited for: 5 -> 5; matrix products, arithmetic and copies ran while one was open for 2% -> 13% of each run, Pallas kernels for 0% -> 0%
where the time goes in v3:
time: 165 us
  Pallas kernels  80.2 us (49%)
  starting transfers between devices  22.6 us (14%)
  matrix products  21.4 us (13%)
  other arithmetic  15.9 us (10%)
  local copies, waits for them, and re-layouts  11.8 us (7%)
  waiting for transfers between devices  11.8 us (7%)
    pallas_call x3, Pallas kernels, stage(): pl.pallas_call(stage_kernel(scale_level, scale_step, rows_block), grid=(r...  80.2 us
    dot_general x3, matrix products, along_x(): jnp.dot(band(wide, count, shift), block.reshape(count, rows_y * rows_z),...  11.7 us
    ppermute x3, starting transfers between devices, extended_2(): lax.ppermute(lax.slice_in_dim(block, block.shape[dim] - width, None, axis...  10.8 us
    ppermute x3, waiting for transfers between devices, extended_2(): lax.ppermute(lax.slice_in_dim(block, 0, width, axis=dim), axis, backward)  9.89 us
    concatenate x3, other arithmetic, extended_2(): block = jnp.concatenate([low, block, high], axis=dim)  8.49 us
    ppermute x3, starting transfers between devices, extended_2(): lax.ppermute(lax.slice_in_dim(block, 0, width, axis=dim), axis, backward)  6.25 us
    dot_general x3, matrix products, across(): jnp.dot(block.reshape(count * rows_y, rows_z), band(rows_z, rows_z, 0).T,...  6.11 us
    ppermute x2, starting transfers between devices, shifted(): return lax.ppermute(block, axis, route)  5.55 us
  transfers between devices with their start and end apart: 8, of which 5 were waited for; matrix products, arithmetic and copies ran while one was open for 13% of the time, Pallas kernels for 0%

profile of v3, /device:TPU:1, one launch (start us, length us, event | category | flops | bytes accessed | tf_op | source)
XLA Modules:
  0.0 164.7 jit_solution(15802278470714115410)
XLA Ops:
  1.9 4.5 %collective-permute-start.2 = (f32[3,128,128]{2,1,0:T(8,128)S(1)}, f32[3,128,128]{2,1,0:T(8,128)S(1)}, u32[]{:S(2)}, u32[]{:S(2)}) collective-permute-start(f32[3,128,128]{2,1,0:T(8,128)S(1)} %get-tuple-element.10), channel_id=1, source_target_pairs={{0,1},{1,2},{2,3},{3,4},{4,5},{5,6},{6,7},{7,8},{8,9},{9,10},{10,1... | collective-permute-start | bytes 589832 | tf_op jit(solution)/shard_map/ppermute | solution.py:26
  6.4 1.9 %collective-permute-start.3 = (f32[3,128,128]{2,1,0:T(8,128)S(1)}, f32[3,128,128]{2,1,0:T(8,128)S(1)}, u32[]{:S(2)}, u32[]{:S(2)}) collective-permute-start(f32[3,128,128]{2,1,0:T(8,128)S(1)} %get-tuple-element.11), channel_id=1, source_target_pairs={{1,0},{2,1},{3,2},{4,3},{5,4},{6,5},{7,6},{8,7},{9,8},{10,9},{11,1... | collective-permute-start | bytes 589832 | tf_op jit(solution)/shard_map/ppermute | solution.py:29
  8.3 2.9 %fusion.31 = (f32[14,128,128]{2,1,0:T(8,128)}, f32[14,128,128]{2,1,0:T(8,128)}) fusion(f32[32,128,128]{2,1,0:T(8,128)} %param.11), kind=kLoop, calls=%fused_computation.55 | loop fusion | bytes 3670016 | tf_op jit(solution)/shard_map/slice | solution.py:219
  11.2 1.9 %collective-permute-start.1 = (f32[14,128,128]{2,1,0:T(8,128)}, f32[14,128,128]{2,1,0:T(8,128)}, u32[]{:S(2)}, u32[]{:S(2)}) collective-permute-start(f32[14,128,128]{2,1,0:T(8,128)} %get-tuple-element.12), channel_id=1, source_target_pairs={{1,0},{2,1},{3,2},{4,3},{5,4},{6,5},{7,6},{8,7},{9,8},{10,9},{11,1... | collective-permute-start | bytes 2752520 | tf_op jit(solution)/shard_map/ppermute | solution.py:18
  13.1 3.6 %collective-permute-start = (f32[14,128,128]{2,1,0:T(8,128)}, f32[14,128,128]{2,1,0:T(8,128)}, u32[]{:S(2)}, u32[]{:S(2)}) collective-permute-start(f32[14,128,128]{2,1,0:T(8,128)} %get-tuple-element.13), channel_id=1, source_target_pairs={{0,1},{1,2},{2,3},{3,4},{4,5},{5,6},{6,7},{7,8},{8,9},{9,10},{10,1... | collective-permute-start | bytes 2752520 | tf_op jit(solution)/shard_map/ppermute | solution.py:18
  16.8 2.0 %fusion.32 = f32[128,32,128]{2,0,1:T(8,128)S(1)} fusion(f32[128,128,1]{1,0,2:T(8,128)S(1)} %copy-done.4, f32[32,128,128]{2,1,0:T(8,128)S(1)} %copy-done.3), kind=kOutput, calls=%fused_computation.56 | convolution fusion | flops 805306368 | bytes 4259840 | tf_op jit(solution)/shard_map/dot_general | solution.py:223
  22.4 6.9 %fusion.19 = f32[16384,36]{0,1:T(8,128)} fusion(f32[36,32]{1,0:T(8,128)S(1)} %copy-done.7, f32[4,8,128,128]{3,2,1,0:T(8,128)} %bitcast.48), kind=kOutput, calls=%fused_computation.39 | convolution fusion | flops 226492416 | bytes 4461056 | tf_op jit(solution)/shard_map/dot_general | solution.py:232
  31.2 2.1 %convolution_bitcast_fusion.1 = f32[14,128,128]{1,2,0:T(8,128)S(1)} fusion(f32[128,128,1]{1,0,2:T(8,128)S(1)} %copy-done.4, f32[14,128,128]{2,1,0:T(8,128)} %collective-permute-done.1), kind=kOutput, calls=%fused_computation.48 | convolution fusion | flops 352321536 | bytes 1900544 | tf_op jit(solution)/shard_map/dot_general | solution.py:223
  36.3 2.1 %convolution_bitcast_fusion.3 = f32[14,128,128]{1,2,0:T(8,128)S(1)} fusion(f32[128,128,1]{1,0,2:T(8,128)S(1)} %copy-done.4, f32[14,128,128]{2,1,0:T(8,128)} %collective-permute-done), kind=kOutput, calls=%fused_computation.50 | convolution fusion | flops 352321536 | bytes 1900544 | tf_op jit(solution)/shard_map/dot_general | solution.py:223
  41.3 2.3 %convolution_add_fusion.1 = f32[16384,36]{0,1:T(8,128)S(1)} fusion(f32[16384,36]{0,1:T(8,128)S(1)} %copy-done.2, f32[14,16384]{1,0:T(8,128)S(1)} %bitcast.52, f32[36,14]{1,0:T(8,128)S(1)} %copy-done.6), kind=kOutput, calls=%fused_computation.1 | convolution fusion | flops 99680256 | bytes 5638112 | tf_op jit(solution)/shard_map/dot_general | solution.py:232
  43.6 2.5 %convolution_add_fusion = f32[16384,36]{0,1:T(8,128)S(1)} fusion(f32[16384,36]{0,1:T(8,128)S(1)} %convolution_add_fusion.1, f32[14,16384]{1,0:T(8,128)S(1)} %bitcast.51, f32[36,14]{1,0:T(8,128)S(1)} %copy-done.5), kind=kOutput, calls=%fused_computation | convolution fusion | flops 99680256 | bytes 5638112 | tf_op jit(solution)/shard_map/dot_general | solution.py:232
  47.1 1.9 %fusion.14 = f32[34,128,128]{2,1,0:T(8,128)S(1)} fusion(f32[34,128,128]{2,1,0:T(8,128)S(1)} %slice.95, f32[36,128,128]{2,1,0:T(8,128)S(1)} %slice_select_fusion, pred[34]{0:T(512)(128)(4,1)S(1)} %slice.70), kind=kLoop, calls=%fused_computation.34 | loop fusion | flops 8355840 | bytes 8912930 | tf_op jit(solution)/shard_map/jit(_where)/select_n | solution.py:242
  50.8 3.5 %fusion.18 = (f32[32,128,128]{2,1,0:T(8,128)}, f32[32,128,128]{2,1,0:T(8,128)}) fusion(f32[32,128,128]{2,1,0:T(8,128)S(1)} %get-tuple-element.3.edge_ref), kind=kLoop, calls=%fused_computation.38 | loop fusion | flops 2097152 | bytes 6291456 | tf_op jit(solution)/shard_map/mul | solution.py:70
  54.3 26.6 %shard_map.122 = f32[32,128,128]{2,1,0:T(8,128)} custom-call(f32[38,144,128]{2,1,0:T(8,128)} %select_maximum_fusion.4.p_ref, f32[32,128,128]{2,1,0:T(8,128)} %copy-done, f32[32,128,128]{2,1,0:T(8,128)} %get-tuple-element.2.sx_ref, f32[32,128,128]{2,1,0:T(8,128)} %get-tuple-element.9.sy_ref, f32[32,128,128]{2,1,0:T(8,128)} %get-tuple-element.8.sz_ref, ...), custom_call_target="tpu_custom_call" | custom-call | tf_op jit(solution)/shard_map/pallas_call | solution.py:205
  82.0 4.4 %collective-permute-start.4 = (f32[3,128,128]{2,1,0:T(8,128)S(1)}, f32[3,128,128]{2,1,0:T(8,128)S(1)}, u32[]{:S(2)}, u32[]{:S(2)}) collective-permute-start(f32[3,128,128]{2,1,0:T(8,128)S(1)} %get-tuple-element.6), channel_id=1, source_target_pairs={{0,1},{1,2},{2,3},{3,4},{4,5},{5,6},{6,7},{7,8},{8,9},{9,10},{10,1... | collective-permute-start | bytes 589832 | tf_op jit(solution)/shard_map/ppermute | solution.py:26
  86.4 1.9 %collective-permute-start.5 = (f32[3,128,128]{2,1,0:T(8,128)S(1)}, f32[3,128,128]{2,1,0:T(8,128)S(1)}, u32[]{:S(2)}, u32[]{:S(2)}) collective-permute-start(f32[3,128,128]{2,1,0:T(8,128)S(1)} %get-tuple-element.7), channel_id=1, source_target_pairs={{1,0},{2,1},{3,2},{4,3},{5,4},{6,5},{7,6},{8,7},{9,8},{10,9},{11,1... | collective-permute-start | bytes 589832 | tf_op jit(solution)/shard_map/ppermute | solution.py:29
  89.0 4.4 %collective-permute-done.5 = f32[3,128,128]{2,1,0:T(8,128)S(1)} collective-permute-done((f32[3,128,128]{2,1,0:T(8,128)S(1)}, f32[3,128,128]{2,1,0:T(8,128)S(1)}, u32[]{:S(2)}, u32[]{:S(2)}) %collective-permute-start.5) | collective-permute-done | bytes 196640 | tf_op jit(solution)/shard_map/ppermute | solution.py:29
  93.4 3.3 %select_maximum_fusion.2.p_ref = f32[38,144,128]{2,1,0:T(8,128)} fusion(f32[3,128,128]{2,1,0:T(8,128)S(1)} %collective-permute-done.5, f32[32,128,128]{2,1,0:T(8,128)} %shard_map.122, f32[3,128,128]{2,1,0:T(8,128)S(1)} %collective-permute-done.4), kind=kLoop, calls=%fused_computation.14 | loop fusion | flops 5603328 | bytes 5292032 | tf_op jit(solution)/shard_map/concatenate | solution.py:30
  96.7 26.8 %shard_map.123 = f32[32,128,128]{2,1,0:T(8,128)} custom-call(f32[38,144,128]{2,1,0:T(8,128)} %select_maximum_fusion.2.p_ref, f32[32,128,128]{2,1,0:T(8,128)} %copy-done, f32[32,128,128]{2,1,0:T(8,128)} %get-tuple-element.2.sx_ref, f32[32,128,128]{2,1,0:T(8,128)} %get-tuple-element.9.sy_ref, f32[32,128,128]{2,1,0:T(8,128)} %get-tuple-element.8.sz_ref, ...), custom_call_target="tpu_custom_call" | custom-call | tf_op jit(solution)/shard_map/pallas_call | solution.py:205
  124.6 1.9 %collective-permute-start.6 = (f32[3,128,128]{2,1,0:T(8,128)S(1)}, f32[3,128,128]{2,1,0:T(8,128)S(1)}, u32[]{:S(2)}, u32[]{:S(2)}) collective-permute-start(f32[3,128,128]{2,1,0:T(8,128)S(1)} %get-tuple-element.4), channel_id=1, source_target_pairs={{0,1},{1,2},{2,3},{3,4},{4,5},{5,6},{6,7},{7,8},{8,9},{9,10},{10,1... | collective-permute-start | bytes 589832 | tf_op jit(solution)/shard_map/ppermute | solution.py:26
  126.5 2.4 %collective-permute-start.7 = (f32[3,128,128]{2,1,0:T(8,128)S(1)}, f32[3,128,128]{2,1,0:T(8,128)S(1)}, u32[]{:S(2)}, u32[]{:S(2)}) collective-permute-start(f32[3,128,128]{2,1,0:T(8,128)S(1)} %get-tuple-element.5), channel_id=1, source_target_pairs={{1,0},{2,1},{3,2},{4,3},{5,4},{6,5},{7,6},{8,7},{9,8},{10,9},{11,1... | collective-permute-start | bytes 589832 | tf_op jit(solution)/shard_map/ppermute | solution.py:29
  129.1 5.5 %collective-permute-done.7 = f32[3,128,128]{2,1,0:T(8,128)S(1)} collective-permute-done((f32[3,128,128]{2,1,0:T(8,128)S(1)}, f32[3,128,128]{2,1,0:T(8,128)S(1)}, u32[]{:S(2)}, u32[]{:S(2)}) %collective-permute-start.7) | collective-permute-done | bytes 196640 | tf_op jit(solution)/shard_map/ppermute | solution.py:29
  134.6 3.3 %select_maximum_fusion.p_ref = f32[38,144,128]{2,1,0:T(8,128)} fusion(f32[3,128,128]{2,1,0:T(8,128)S(1)} %collective-permute-done.7, f32[32,128,128]{2,1,0:T(8,128)} %shard_map.123, f32[3,128,128]{2,1,0:T(8,128)S(1)} %collective-permute-done.6), kind=kLoop, calls=%fused_computation.12 | loop fusion | flops 5603328 | bytes 5292032 | tf_op jit(solution)/shard_map/concatenate | solution.py:30
  137.9 26.8 %shard_map.124 = f32[32,128,128]{2,1,0:T(8,128)} custom-call(f32[38,144,128]{2,1,0:T(8,128)} %select_maximum_fusion.p_ref, f32[32,128,128]{2,1,0:T(8,128)} %copy-done, f32[32,128,128]{2,1,0:T(8,128)} %get-tuple-element.2.sx_ref, f32[32,128,128]{2,1,0:T(8,128)} %get-tuple-element.9.sy_ref, f32[32,128,128]{2,1,0:T(8,128)} %get-tuple-element.8.sz_ref, ...), custom_call_target="tpu_custom_call" | custom-call | tf_op jit(solution)/shard_map/pallas_call | solution.py:205
  (42 shorter events, 18.3 us)
Async XLA Ops:
  0.6 16.2 %copy-start.4 = (f32[128,128,1]{1,0,2:T(8,128)S(1)}, f32[128,128,1]{1,0,2:T(8,128)}, u32[]{:S(2)}) copy-start(f32[128,128,1]{1,0,2:T(8,128)} %constant.46) | copy-start | bytes 196612
  0.6 16.2 %copy-start.3 = (f32[32,128,128]{2,1,0:T(8,128)S(1)}, f32[32,128,128]{2,1,0:T(8,128)}, u32[]{:S(2)}) copy-start(f32[32,128,128]{2,1,0:T(8,128)} %param.11) | copy-start | bytes 6291460
  1.9 27.5 %collective-permute-start.2 = (f32[3,128,128]{2,1,0:T(8,128)S(1)}, f32[3,128,128]{2,1,0:T(8,128)S(1)}, u32[]{:S(2)}, u32[]{:S(2)}) collective-permute-start(f32[3,128,128]{2,1,0:T(8,128)S(1)} %get-tuple-element.10), channel_id=1, source_target_pairs={{0,1},{1,2},{2,3},{3,4},{4,5},{5,6},{6,7},{7,8},{8,9},{9,10},{10,1... | collective-permute-start | bytes 589832 | tf_op jit(solution)/shard_map/ppermute | solution.py:26
  6.4 23.0 %collective-permute-start.3 = (f32[3,128,128]{2,1,0:T(8,128)S(1)}, f32[3,128,128]{2,1,0:T(8,128)S(1)}, u32[]{:S(2)}, u32[]{:S(2)}) collective-permute-start(f32[3,128,128]{2,1,0:T(8,128)S(1)} %get-tuple-element.11), channel_id=1, source_target_pairs={{1,0},{2,1},{3,2},{4,3},{5,4},{6,5},{7,6},{8,7},{9,8},{10,9},{11,1... | collective-permute-start | bytes 589832 | tf_op jit(solution)/shard_map/ppermute | solution.py:29
  11.2 20.0 %collective-permute-start.1 = (f32[14,128,128]{2,1,0:T(8,128)}, f32[14,128,128]{2,1,0:T(8,128)}, u32[]{:S(2)}, u32[]{:S(2)}) collective-permute-start(f32[14,128,128]{2,1,0:T(8,128)} %get-tuple-element.12), channel_id=1, source_target_pairs={{1,0},{2,1},{3,2},{4,3},{5,4},{6,5},{7,6},{8,7},{9,8},{10,9},{11,1... | collective-permute-start | bytes 2752520 | tf_op jit(solution)/shard_map/ppermute | solution.py:18
  13.1 23.2 %collective-permute-start = (f32[14,128,128]{2,1,0:T(8,128)}, f32[14,128,128]{2,1,0:T(8,128)}, u32[]{:S(2)}, u32[]{:S(2)}) collective-permute-start(f32[14,128,128]{2,1,0:T(8,128)} %get-tuple-element.13), channel_id=1, source_target_pairs={{0,1},{1,2},{2,3},{3,4},{4,5},{5,6},{6,7},{7,8},{8,9},{9,10},{10,1... | collective-permute-start | bytes 2752520 | tf_op jit(solution)/shard_map/ppermute | solution.py:18
  20.6 1.8 %copy-start.7 = (f32[36,32]{1,0:T(8,128)S(1)}, f32[36,32]{1,0:T(8,128)}, u32[]{:S(2)}) copy-start(f32[36,32]{1,0:T(8,128)} %constant.33.clone) | copy-start | bytes 13828
  22.4 7.0 %copy-start.1 = (f32[32,128,128]{2,1,0:T(8,128)S(1)}, f32[32,128,128]{2,1,0:T(8,128)}, u32[]{:S(2)}) copy-start(f32[32,128,128]{2,1,0:T(8,128)} %ls_ref.5) | copy-start | bytes 6291460
  39.6 1.7 %copy-start.2 = (f32[16384,36]{0,1:T(8,128)S(1)}, f32[16384,36]{0,1:T(8,128)}, u32[]{:S(2)}) copy-start(f32[16384,36]{0,1:T(8,128)} %fusion.19) | copy-start | bytes 7077892
  39.6 1.7 %copy-start.6 = (f32[36,14]{1,0:T(8,128)S(1)}, f32[36,14]{1,0:T(8,128)}, u32[]{:S(2)}) copy-start(f32[36,14]{1,0:T(8,128)} %constant.34.clone) | copy-start | bytes 6052
  41.3 2.3 %copy-start.5 = (f32[36,14]{1,0:T(8,128)S(1)}, f32[36,14]{1,0:T(8,128)}, u32[]{:S(2)}) copy-start(f32[36,14]{1,0:T(8,128)} %constant.35.clone) | copy-start | bytes 6052
  50.8 3.5 %copy-start = (f32[32,128,128]{2,1,0:T(8,128)}, f32[32,128,128]{2,1,0:T(8,128)S(1)}, u32[]{:S(2)}) copy-start(f32[32,128,128]{2,1,0:T(8,128)S(1)} %get-tuple-element.3.edge_ref) | copy-start | bytes 6291460
  82.0 7.0 %collective-permute-start.4 = (f32[3,128,128]{2,1,0:T(8,128)S(1)}, f32[3,128,128]{2,1,0:T(8,128)S(1)}, u32[]{:S(2)}, u32[]{:S(2)}) collective-permute-start(f32[3,128,128]{2,1,0:T(8,128)S(1)} %get-tuple-element.6), channel_id=1, source_target_pairs={{0,1},{1,2},{2,3},{3,4},{4,5},{5,6},{6,7},{7,8},{8,9},{9,10},{10,1... | collective-permute-start | bytes 589832 | tf_op jit(solution)/shard_map/ppermute | solution.py:26
  86.4 7.0 %collective-permute-start.5 = (f32[3,128,128]{2,1,0:T(8,128)S(1)}, f32[3,128,128]{2,1,0:T(8,128)S(1)}, u32[]{:S(2)}, u32[]{:S(2)}) collective-permute-start(f32[3,128,128]{2,1,0:T(8,128)S(1)} %get-tuple-element.7), channel_id=1, source_target_pairs={{1,0},{2,1},{3,2},{4,3},{5,4},{6,5},{7,6},{8,7},{9,8},{10,9},{11,1... | collective-permute-start | bytes 589832 | tf_op jit(solution)/shard_map/ppermute | solution.py:29
  124.6 4.5 %collective-permute-start.6 = (f32[3,128,128]{2,1,0:T(8,128)S(1)}, f32[3,128,128]{2,1,0:T(8,128)S(1)}, u32[]{:S(2)}, u32[]{:S(2)}) collective-permute-start(f32[3,128,128]{2,1,0:T(8,128)S(1)} %get-tuple-element.4), channel_id=1, source_target_pairs={{0,1},{1,2},{2,3},{3,4},{4,5},{5,6},{6,7},{7,8},{8,9},{9,10},{10,1... | collective-permute-start | bytes 589832 | tf_op jit(solution)/shard_map/ppermute | solution.py:26
  126.5 8.1 %collective-permute-start.7 = (f32[3,128,128]{2,1,0:T(8,128)S(1)}, f32[3,128,128]{2,1,0:T(8,128)S(1)}, u32[]{:S(2)}, u32[]{:S(2)}) collective-permute-start(f32[3,128,128]{2,1,0:T(8,128)S(1)} %get-tuple-element.5), channel_id=1, source_target_pairs={{1,0},{2,1},{3,2},{4,3},{5,4},{6,5},{7,6},{8,7},{9,8},{10,9},{11,1... | collective-permute-start | bytes 589832 | tf_op jit(solution)/shard_map/ppermute | solution.py:29

commit v4 on v2

--- a/solution.py
+++ b/solution.py
@@ -115,10 +115,36 @@
 
 
 def stage_kernel(scale_level, scale_step, rows_block):
-    def kernel(p_ref, edge_ref, sx_ref, sy_ref, sz_ref, ls_ref, out_ref):
+    def kernel(
+        low_ref, main_ref, high_ref, edge_ref, sx_ref, sy_ref, sz_ref, ls_ref, out_ref, p_ref, sems
+    ):
+        rows = main_ref.shape[0]
         rows_y = out_ref.shape[1]
         rows_z = out_ref.shape[2]
         block = pl.program_id(0)
+
+        @pl.when(block == 0)
+        def _():
+            inner = pl.ds(SUB, rows_y)
+            copies = [
+                pltpu.make_async_copy(low_ref, p_ref.at[pl.ds(0, HALO), inner, :], sems.at[0]),
+                pltpu.make_async_copy(main_ref, p_ref.at[pl.ds(HALO, rows), inner, :], sems.at[1]),
+                pltpu.make_async_copy(
+                    high_ref, p_ref.at[pl.ds(HALO + rows, HALO), inner, :], sems.at[2]
+                ),
+            ]
+            for copy in copies:
+                copy.start()
+            zeros = jnp.zeros((SUB, rows_z), jnp.float32)
+
+            def clear(x, carry):
+                p_ref[x, pl.ds(0, SUB), :] = zeros
+                p_ref[x, pl.ds(SUB + rows_y, SUB), :] = zeros
+                return carry
+
+            lax.fori_loop(0, rows + 2 * HALO, clear, 0)
+            for copy in copies:
+                copy.wait()
         lane = lax.broadcasted_iota(jnp.int32, (SUB, rows_z), 1)
 
         def along_z(tile, step):
@@ -192,18 +218,23 @@
     return kernel
 
 
-def stage(padded, edge, slope, level_set, scale_level, scale_step):
+def stage(low, field, high, edge, slope, level_set, scale_level, scale_step):
     rows, rows_y, rows_z = level_set.shape
     rows_block = SUB if rows % SUB == 0 else rows
-    whole = pl.BlockSpec(padded.shape, lambda i: (0, 0, 0))
+    raw = pl.BlockSpec(memory_space=pl.ANY)
     part = pl.BlockSpec((rows_block, rows_y, rows_z), lambda i: (i, 0, 0))
     return pl.pallas_call(
         stage_kernel(scale_level, scale_step, rows_block),
         grid=(rows // rows_block,),
-        in_specs=[whole, part, part, part, part, part],
+        in_specs=[raw, raw, raw, part, part, part, part, part],
         out_specs=part,
         out_shape=jax.ShapeDtypeStruct(level_set.shape, level_set.dtype),
-    )(padded, edge, slope[0], slope[1], slope[2], level_set)
+        scratch_shapes=[
+            pltpu.VMEM((rows + 2 * HALO, rows_y + 2 * SUB, rows_z), jnp.float32),
+            pltpu.SemaphoreType.DMA((3,)),
+        ],
+        compiler_params=pltpu.CompilerParams(dimension_semantics=("arbitrary",)),
+    )(low, field, high, edge, slope[0], slope[1], slope[2], level_set)
 
 
 def shards(volume, level_set):
@@ -232,9 +263,9 @@
     slope = central_grads(edge_wide)
 
     def step(field, scale_level, scale_step):
-        padded = extended_2(field, (("gx", 0),), HALO)
-        padded = jnp.pad(padded, ((0, 0), (SUB, SUB), (0, 0)))
-        return stage(padded, edge, slope, level_set, scale_level, scale_step)
+        low = shifted(field[rows - HALO :], "gx", 1)
+        high = shifted(field[:HALO], "gx", -1)
+        return stage(low, field, high, edge, slope, level_set, scale_level, scale_step)
 
     section_one = step(level_set, None, None)
     section_two = step(section_one, 0.75, 0.25)

time: 163 us -> 157 us (0.963); the launches traced: 163 us -> 154 us
  other arithmetic: 17.7 us -> 9.03 us
  waiting for transfers between devices: 25.9 us -> 18.5 us
  local copies, waits for them, and re-layouts: 9.61 us -> 12.7 us
  Pallas kernels: 79.1 us -> 81.6 us
  starting transfers between devices: 22.5 us -> 24.6 us
    ppermute x6 -> x0, waiting for transfers between devices: 25.9 us -> none  [the longest x3 17.1 us: extended_2(): lax.ppermute(lax.slice_in_dim(block, block.shape[dim] - width, None, axis...]
    ppermute x2 -> x8, waiting for transfers between devices: 0.01 us -> 18.5 us  [shifted(): return lax.ppermute(block, axis, route)]
    ppermute x2 -> x8, starting transfers between devices: 6.44 us -> 24.6 us  [shifted(): return lax.ppermute(block, axis, route)]
    ppermute x6 -> x0, starting transfers between devices: 16.1 us -> none  [the longest x3 9.83 us: extended_2(): lax.ppermute(lax.slice_in_dim(block, block.shape[dim] - width, None, axis...]
    concatenate x3 -> x0, other arithmetic: 8.54 us -> none  [extended_2(): block = jnp.concatenate([low, block, high], axis=dim)]
    pallas_call x3, Pallas kernels: 79.1 us -> 81.6 us  [stage(): pl.pallas_call(stage_kernel(scale_level, scale_step, rows_block), grid=(r...]
    unnamed x13 -> x23, local copies, waits for them, and re-layouts: 3.73 us -> 5.8 us
  transfers between devices with their start and end apart: 8 -> 8, of which waited for: 5 -> 5; matrix products, arithmetic and copies ran while one was open for 2% -> 14% of each run, Pallas kernels for 0% -> 0%
where the time goes in v4:
time: 157 us; the launch traced here: 154 us
  Pallas kernels  81.6 us (52%)
  starting transfers between devices  24.6 us (16%)
  waiting for transfers between devices  18.5 us (12%)
  local copies, waits for them, and re-layouts  12.7 us (8%)
  other arithmetic  9.03 us (6%)
  matrix products  7.06 us (4%)
    pallas_call x3, Pallas kernels, stage(): pl.pallas_call(stage_kernel(scale_level, scale_step, rows_block), grid=(r...  81.6 us
    ppermute x8, starting transfers between devices, shifted(): return lax.ppermute(block, axis, route)  24.6 us
    ppermute x8, waiting for transfers between devices, shifted(): return lax.ppermute(block, axis, route)  18.5 us
    unnamed x23, local copies, waits for them, and re-layouts  5.8 us
    slice x3, local copies, waits for them, and re-layouts, step(): high = shifted(field[:HALO], 'gx', -1)  3.89 us
    mul x1, other arithmetic, central_grads(): grad_z = (side[:, 1:-1, 2:] - side[:, 1:-1, :-2]) * 0.5  3.47 us
  transfers between devices with their start and end apart: 8, of which 5 were waited for; matrix products, arithmetic and copies ran while one was open for 14% of the time, Pallas kernels for 0%

profile of v4, /device:TPU:1, one launch (start us, length us, event | category | flops | bytes accessed | tf_op | source)
XLA Modules:
  0.0 154.5 jit_solution(10588384237941077162)
XLA Ops:
  0.6 2.7 %fusion.24 = (f32[14,128,128]{2,1,0:T(8,128)}, f32[14,128,128]{2,1,0:T(8,128)S(1)}) fusion(f32[32,128,128]{2,1,0:T(8,128)} %param.5), kind=kLoop, calls=%fused_computation.37 | loop fusion | bytes 3670016 | tf_op jit(solution)/shard_map/slice | solution.py:244
  3.3 4.5 %collective-permute-start = (f32[14,128,128]{2,1,0:T(8,128)}, f32[14,128,128]{2,1,0:T(8,128)}, u32[]{:S(2)}, u32[]{:S(2)}) collective-permute-start(f32[14,128,128]{2,1,0:T(8,128)} %get-tuple-element.12), channel_id=1, source_target_pairs={{0,1},{1,2},{2,3},{3,4},{4,5},{5,6},{6,7},{7,8},{8,9},{9,10},{10,1... | collective-permute-start | bytes 2752520 | tf_op jit(solution)/shard_map/ppermute | solution.py:18
  7.9 1.9 %collective-permute-start.1 = (f32[14,128,128]{2,1,0:T(8,128)S(1)}, f32[14,128,128]{2,1,0:T(8,128)}, u32[]{:S(2)}, u32[]{:S(2)}) collective-permute-start(f32[14,128,128]{2,1,0:T(8,128)S(1)} %get-tuple-element.13), channel_id=1, source_target_pairs={{1,0},{2,1},{3,2},{4,3},{5,4},{6,5},{7,6},{8,7},{9,8},{10,9},{11,1... | collective-permute-start | bytes 2752520 | tf_op jit(solution)/shard_map/ppermute | solution.py:18
  9.8 1.8 %fusion.23 = (f32[3,128,128]{2,1,0:T(8,128)}, f32[3,128,128]{2,1,0:T(8,128)}) fusion(f32[32,128,128]{2,1,0:T(8,128)} %ls_ref.5), kind=kLoop, calls=%fused_computation.36 | loop fusion | bytes 786432 | tf_op jit(solution)/shard_map/slice | solution.py:267
  11.6 1.9 %collective-permute-start.3 = (f32[3,128,128]{2,1,0:T(8,128)}, f32[3,128,128]{2,1,0:T(8,128)S(1)}, u32[]{:S(2)}, u32[]{:S(2)}) collective-permute-start(f32[3,128,128]{2,1,0:T(8,128)} %get-tuple-element.10), channel_id=1, source_target_pairs={{1,0},{2,1},{3,2},{4,3},{5,4},{6,5},{7,6},{8,7},{9,8},{10,9},{11,1... | collective-permute-start | bytes 589832 | tf_op jit(solution)/shard_map/ppermute | solution.py:18
  13.5 3.6 %collective-permute-start.2 = (f32[3,128,128]{2,1,0:T(8,128)}, f32[3,128,128]{2,1,0:T(8,128)S(1)}, u32[]{:S(2)}, u32[]{:S(2)}) collective-permute-start(f32[3,128,128]{2,1,0:T(8,128)} %get-tuple-element.11), channel_id=1, source_target_pairs={{0,1},{1,2},{2,3},{3,4},{4,5},{5,6},{6,7},{7,8},{8,9},{9,10},{10,1... | collective-permute-start | bytes 589832 | tf_op jit(solution)/shard_map/ppermute | solution.py:18
  17.2 13.2 %collective-permute-done = f32[14,128,128]{2,1,0:T(8,128)} collective-permute-done((f32[14,128,128]{2,1,0:T(8,128)}, f32[14,128,128]{2,1,0:T(8,128)}, u32[]{:S(2)}, u32[]{:S(2)}) %collective-permute-start) | collective-permute-done | bytes 917536 | tf_op jit(solution)/shard_map/ppermute | solution.py:18
  30.4 1.7 %pad_maximum_fusion = f32[60,128,128]{2,1,0:T(8,128)S(1)} fusion(f32[14,128,128]{2,1,0:T(8,128)} %collective-permute-done.1, f32[32,128,128]{2,1,0:T(8,128)S(1)} %copy-done.1, f32[14,128,128]{2,1,0:T(8,128)} %collective-permute-done), kind=kLoop, calls=%fused_computation.8 | loop fusion | flops 1966080 | bytes 7864320 | tf_op jit(solution)/shard_map/concatenate | solution.py:246
  32.7 2.4 %copy.9 = f32[8,8,128,128]{3,1,2,0:T(8,128)S(1)} copy(f32[8,8,128,128]{3,2,1,0:T(8,128)S(1)} %bitcast.14) | data formatting | bytes 8388608
  35.1 2.5 %fusion.25 = f32[36,16384]{1,0:T(8,128)S(1)} fusion(f32[36,60]{1,0:T(8,128)S(1)} %copy-done.9, f32[60,16384]{1,0:T(8,128)S(1)} %bitcast.15), kind=kOutput, calls=%fused_computation.38 | convolution fusion | flops 424673280 | bytes 6300096 | tf_op jit(solution)/shard_map/dot_general | solution.py:248
  38.5 2.3 %fusion = f32[36,128,128]{1,2,0:T(8,128)S(1)} fusion(f32[128,128,1]{1,0,2:T(8,128)S(1)} %copy-done.2, f32[40,128,128]{2,1,0:T(8,128)S(1)} %bitcast.17), kind=kOutput, calls=%fused_computation.9 | convolution fusion | flops 905969664 | bytes 4784128 | tf_op jit(solution)/shard_map/dot_general | solution.py:253
  40.7 2.2 %select_bitcast_fusion = f32[36,128,128]{2,1,0:T(8,128)S(1)} fusion(f32[36,128,128]{1,2,0:T(8,128)S(1)} %fusion, f32[128,128,1]{1,0,2:T(8,128)S(1)} %copy-done.2, pred[36]{0:T(512)(128)(4,1)S(1)} %compare_and_fusion), kind=kOutput, calls=%fused_computation.11 | convolution fusion | flops 906559488 | bytes 4784164 | tf_op jit(solution)/shard_map/yv,xvz->xyz/dot_general | solution.py:256
  43.2 2.1 %fusion.15 = f32[34,128,128]{2,1,0:T(8,128)S(1)} fusion(f32[34,128,128]{2,1,0:T(8,128)S(1)} %slice.95, f32[36,128,128]{2,1,0:T(8,128)S(1)} %select_bitcast_fusion, pred[34]{0:T(512)(128)(4,1)S(1)} %slice.70), kind=kLoop, calls=%fused_computation.26 | loop fusion | flops 8355840 | bytes 8912930 | tf_op jit(solution)/shard_map/jit(_where)/select_n | solution.py:261
  45.3 1.8 %fusion.20 = (f32[32,128,128]{2,1,0:T(8,128)}, f32[32,128,128]{2,1,0:T(8,128)S(1)}) fusion(f32[34,128,128]{2,1,0:T(8,128)S(1)} %fusion.15), kind=kLoop, calls=%fused_computation.32 | loop fusion | flops 1048576 | bytes 10485760 | tf_op jit(solution)/shard_map/mul | solution.py:68
  47.1 3.5 %fusion.19 = (f32[32,128,128]{2,1,0:T(8,128)}, f32[32,128,128]{2,1,0:T(8,128)}) fusion(f32[32,128,128]{2,1,0:T(8,128)S(1)} %get-tuple-element.3.edge_ref), kind=kLoop, calls=%fused_computation.30 | loop fusion | flops 2097152 | bytes 6291456 | tf_op jit(solution)/shard_map/mul | solution.py:70
  51.3 27.0 %shard_map.68.main_ref = f32[32,128,128]{2,1,0:T(8,128)} custom-call(f32[3,128,128]{2,1,0:T(8,128)} %copy-done.4, f32[32,128,128]{2,1,0:T(8,128)} %ls_ref.5, f32[3,128,128]{2,1,0:T(8,128)} %copy-done.3, f32[32,128,128]{2,1,0:T(8,128)} %copy-done, f32[32,128,128]{2,1,0:T(8,128)} %get-tuple-element.2.sx_ref, f32[32,128,128]{2,1,0:T(8,128)} %get-tuple-element.9.sy_ref, ...), custom_call_target="tpu_custom_call" | custom-call | tf_op jit(solution)/shard_map/pallas_call | solution.py:226
  79.3 1.9 %collective-permute-start.5 = (f32[3,128,128]{2,1,0:T(8,128)S(1)}, f32[3,128,128]{2,1,0:T(8,128)S(1)}, u32[]{:S(2)}, u32[]{:S(2)}) collective-permute-start(f32[3,128,128]{2,1,0:T(8,128)S(1)} %get-tuple-element.6), channel_id=1, source_target_pairs={{1,0},{2,1},{3,2},{4,3},{5,4},{6,5},{7,6},{8,7},{9,8},{10,9},{11,1... | collective-permute-start | bytes 589832 | tf_op jit(solution)/shard_map/ppermute | solution.py:18
  81.3 4.4 %collective-permute-start.4 = (f32[3,128,128]{2,1,0:T(8,128)S(1)}, f32[3,128,128]{2,1,0:T(8,128)S(1)}, u32[]{:S(2)}, u32[]{:S(2)}) collective-permute-start(f32[3,128,128]{2,1,0:T(8,128)S(1)} %get-tuple-element.7), channel_id=1, source_target_pairs={{0,1},{1,2},{2,3},{3,4},{4,5},{5,6},{6,7},{7,8},{8,9},{9,10},{10,1... | collective-permute-start | bytes 589832 | tf_op jit(solution)/shard_map/ppermute | solution.py:18
  85.7 1.4 collective-permute-done.5.high_ref
  88.9 27.3 %shard_map.69.main_ref = f32[32,128,128]{2,1,0:T(8,128)} custom-call(f32[3,128,128]{2,1,0:T(8,128)} %copy-done.8, f32[32,128,128]{2,1,0:T(8,128)} %shard_map.68.main_ref, f32[3,128,128]{2,1,0:T(8,128)} %copy-done.6, f32[32,128,128]{2,1,0:T(8,128)} %copy-done, f32[32,128,128]{2,1,0:T(8,128)} %get-tuple-element.2.sx_ref, ...), custom_call_target="tpu_custom_call" | custom-call | tf_op jit(solution)/shard_map/pallas_call | solution.py:226
  117.3 1.9 %collective-permute-start.7 = (f32[3,128,128]{2,1,0:T(8,128)S(1)}, f32[3,128,128]{2,1,0:T(8,128)S(1)}, u32[]{:S(2)}, u32[]{:S(2)}) collective-permute-start(f32[3,128,128]{2,1,0:T(8,128)S(1)} %get-tuple-element.4), channel_id=1, source_target_pairs={{1,0},{2,1},{3,2},{4,3},{5,4},{6,5},{7,6},{8,7},{9,8},{10,9},{11,1... | collective-permute-start | bytes 589832 | tf_op jit(solution)/shard_map/ppermute | solution.py:18
  119.2 4.4 %collective-permute-start.6 = (f32[3,128,128]{2,1,0:T(8,128)S(1)}, f32[3,128,128]{2,1,0:T(8,128)S(1)}, u32[]{:S(2)}, u32[]{:S(2)}) collective-permute-start(f32[3,128,128]{2,1,0:T(8,128)S(1)} %get-tuple-element.5), channel_id=1, source_target_pairs={{0,1},{1,2},{2,3},{3,4},{4,5},{5,6},{6,7},{7,8},{8,9},{9,10},{10,1... | collective-permute-start | bytes 589832 | tf_op jit(solution)/shard_map/ppermute | solution.py:18
  123.6 1.4 collective-permute-done.7.high_ref
  127.0 27.3 %shard_map.70 = f32[32,128,128]{2,1,0:T(8,128)} custom-call(f32[3,128,128]{2,1,0:T(8,128)} %copy-done.7, f32[32,128,128]{2,1,0:T(8,128)} %shard_map.69.main_ref, f32[3,128,128]{2,1,0:T(8,128)} %copy-done.5, f32[32,128,128]{2,1,0:T(8,128)} %copy-done, f32[32,128,128]{2,1,0:T(8,128)} %get-tuple-element.2.sx_ref, f32[32,128,128]{2,1,0:T(8,128)} %get-tuple-element.9.sy_ref, ...), custom_call_target="tpu_custom_call" | custom-call | tf_op jit(solution)/shard_map/pallas_call | solution.py:226
  (32 shorter events, 8.3 us)
Async XLA Ops:
  0.6 29.8 %copy-start.1 = (f32[32,128,128]{2,1,0:T(8,128)S(1)}, f32[32,128,128]{2,1,0:T(8,128)}, u32[]{:S(2)}) copy-start(f32[32,128,128]{2,1,0:T(8,128)} %param.5) | copy-start | bytes 6291460
  3.3 27.1 %collective-permute-start = (f32[14,128,128]{2,1,0:T(8,128)}, f32[14,128,128]{2,1,0:T(8,128)}, u32[]{:S(2)}, u32[]{:S(2)}) collective-permute-start(f32[14,128,128]{2,1,0:T(8,128)} %get-tuple-element.12), channel_id=1, source_target_pairs={{0,1},{1,2},{2,3},{3,4},{4,5},{5,6},{6,7},{7,8},{8,9},{9,10},{10,1... | collective-permute-start | bytes 2752520 | tf_op jit(solution)/shard_map/ppermute | solution.py:18
  7.9 22.6 %collective-permute-start.1 = (f32[14,128,128]{2,1,0:T(8,128)S(1)}, f32[14,128,128]{2,1,0:T(8,128)}, u32[]{:S(2)}, u32[]{:S(2)}) collective-permute-start(f32[14,128,128]{2,1,0:T(8,128)S(1)} %get-tuple-element.13), channel_id=1, source_target_pairs={{1,0},{2,1},{3,2},{4,3},{5,4},{6,5},{7,6},{8,7},{9,8},{10,9},{11,1... | collective-permute-start | bytes 2752520 | tf_op jit(solution)/shard_map/ppermute | solution.py:18
  11.6 39.0 %collective-permute-start.3 = (f32[3,128,128]{2,1,0:T(8,128)}, f32[3,128,128]{2,1,0:T(8,128)S(1)}, u32[]{:S(2)}, u32[]{:S(2)}) collective-permute-start(f32[3,128,128]{2,1,0:T(8,128)} %get-tuple-element.10), channel_id=1, source_target_pairs={{1,0},{2,1},{3,2},{4,3},{5,4},{6,5},{7,6},{8,7},{9,8},{10,9},{11,1... | collective-permute-start | bytes 589832 | tf_op jit(solution)/shard_map/ppermute | solution.py:18
  13.5 37.1 %collective-permute-start.2 = (f32[3,128,128]{2,1,0:T(8,128)}, f32[3,128,128]{2,1,0:T(8,128)S(1)}, u32[]{:S(2)}, u32[]{:S(2)}) collective-permute-start(f32[3,128,128]{2,1,0:T(8,128)} %get-tuple-element.11), channel_id=1, source_target_pairs={{0,1},{1,2},{2,3},{3,4},{4,5},{5,6},{6,7},{7,8},{8,9},{9,10},{10,1... | collective-permute-start | bytes 589832 | tf_op jit(solution)/shard_map/ppermute | solution.py:18
  32.7 2.4 %copy-start.9 = (f32[36,60]{1,0:T(8,128)S(1)}, f32[36,60]{1,0:T(8,128)}, u32[]{:S(2)}) copy-start(f32[36,60]{1,0:T(8,128)} %constant.28.clone) | copy-start | bytes 25924
  37.6 0.8 copy-start.2
  47.1 3.5 %copy-start = (f32[32,128,128]{2,1,0:T(8,128)}, f32[32,128,128]{2,1,0:T(8,128)S(1)}, u32[]{:S(2)}) copy-start(f32[32,128,128]{2,1,0:T(8,128)S(1)} %get-tuple-element.3.edge_ref) | copy-start | bytes 6291460
  50.6 0.7 copy-start.3
  50.6 0.7 copy-start.4
  79.3 7.7 %collective-permute-start.5 = (f32[3,128,128]{2,1,0:T(8,128)S(1)}, f32[3,128,128]{2,1,0:T(8,128)S(1)}, u32[]{:S(2)}, u32[]{:S(2)}) collective-permute-start(f32[3,128,128]{2,1,0:T(8,128)S(1)} %get-tuple-element.6), channel_id=1, source_target_pairs={{1,0},{2,1},{3,2},{4,3},{5,4},{6,5},{7,6},{8,7},{9,8},{10,9},{11,1... | collective-permute-start | bytes 589832 | tf_op jit(solution)/shard_map/ppermute | solution.py:18
  81.3 7.0 %collective-permute-start.4 = (f32[3,128,128]{2,1,0:T(8,128)S(1)}, f32[3,128,128]{2,1,0:T(8,128)S(1)}, u32[]{:S(2)}, u32[]{:S(2)}) collective-permute-start(f32[3,128,128]{2,1,0:T(8,128)S(1)} %get-tuple-element.7), channel_id=1, source_target_pairs={{0,1},{1,2},{2,3},{3,4},{4,5},{5,6},{6,7},{7,8},{8,9},{9,10},{10,1... | collective-permute-start | bytes 589832 | tf_op jit(solution)/shard_map/ppermute | solution.py:18
  87.1 1.2 copy-start.6
  88.3 0.7 copy-start.8
  117.3 7.7 %collective-permute-start.7 = (f32[3,128,128]{2,1,0:T(8,128)S(1)}, f32[3,128,128]{2,1,0:T(8,128)S(1)}, u32[]{:S(2)}, u32[]{:S(2)}) collective-permute-start(f32[3,128,128]{2,1,0:T(8,128)S(1)} %get-tuple-element.4), channel_id=1, source_target_pairs={{1,0},{2,1},{3,2},{4,3},{5,4},{6,5},{7,6},{8,7},{9,8},{10,9},{11,1... | collective-permute-start | bytes 589832 | tf_op jit(solution)/shard_map/ppermute | solution.py:18
  119.2 7.1 %collective-permute-start.6 = (f32[3,128,128]{2,1,0:T(8,128)S(1)}, f32[3,128,128]{2,1,0:T(8,128)S(1)}, u32[]{:S(2)}, u32[]{:S(2)}) collective-permute-start(f32[3,128,128]{2,1,0:T(8,128)S(1)} %get-tuple-element.5), channel_id=1, source_target_pairs={{0,1},{1,2},{2,3},{3,4},{4,5},{5,6},{6,7},{7,8},{8,9},{9,10},{10,1... | collective-permute-start | bytes 589832 | tf_op jit(solution)/shard_map/ppermute | solution.py:18
  125.1 1.3 copy-start.5
  126.4 0.7 copy-start.7

commit v5 on v4

--- a/solution.py
+++ b/solution.py
@@ -114,10 +114,16 @@
 HALO = 3
 
 
-def stage_kernel(scale_level, scale_step, rows_block):
-    def kernel(
-        low_ref, main_ref, high_ref, edge_ref, sx_ref, sy_ref, sz_ref, ls_ref, out_ref, p_ref, sems
-    ):
+def stage_kernel(scale_level, scale_step, rows_block, block_of, edges):
+    def kernel(*refs):
+        if edges:
+            low_ref, main_ref, high_ref = refs[:3]
+            rest = refs[3:]
+        else:
+            main_ref = refs[0]
+            rest = refs[1:]
+        edge_ref, sx_ref, sy_ref, sz_ref, ls_ref = rest[:5]
+        out_ref, p_ref, sems = rest[-3:]
         rows = main_ref.shape[0]
         rows_y = out_ref.shape[1]
         rows_z = out_ref.shape[2]
@@ -127,12 +133,17 @@
         def _():
             inner = pl.ds(SUB, rows_y)
             copies = [
-                pltpu.make_async_copy(low_ref, p_ref.at[pl.ds(0, HALO), inner, :], sems.at[0]),
-                pltpu.make_async_copy(main_ref, p_ref.at[pl.ds(HALO, rows), inner, :], sems.at[1]),
-                pltpu.make_async_copy(
-                    high_ref, p_ref.at[pl.ds(HALO + rows, HALO), inner, :], sems.at[2]
-                ),
+                pltpu.make_async_copy(main_ref, p_ref.at[pl.ds(HALO, rows), inner, :], sems.at[1])
             ]
+            if edges:
+                copies.append(
+                    pltpu.make_async_copy(low_ref, p_ref.at[pl.ds(0, HALO), inner, :], sems.at[0])
+                )
+                copies.append(
+                    pltpu.make_async_copy(
+                        high_ref, p_ref.at[pl.ds(HALO + rows, HALO), inner, :], sems.at[2]
+                    )
+                )
             for copy in copies:
                 copy.start()
             zeros = jnp.zeros((SUB, rows_z), jnp.float32)
@@ -145,6 +156,7 @@
             lax.fori_loop(0, rows + 2 * HALO, clear, 0)
             for copy in copies:
                 copy.wait()
+
         lane = lax.broadcasted_iota(jnp.int32, (SUB, rows_z), 1)
 
         def along_z(tile, step):
@@ -153,7 +165,7 @@
             return jnp.where(keep, moved, 0.0)
 
         def row(r, carry):
-            centre_row = block * rows_block + r + HALO
+            centre_row = block_of(block) * rows_block + r + HALO
             for chunk in range(rows_y // SUB):
                 top = SUB + chunk * SUB
 
@@ -218,23 +230,57 @@
     return kernel
 
 
-def stage(low, field, high, edge, slope, level_set, scale_level, scale_step):
+def stage_call(inputs, prior, level_set, scale_level, scale_step, blocks, block_of, edges):
     rows, rows_y, rows_z = level_set.shape
     rows_block = SUB if rows % SUB == 0 else rows
     raw = pl.BlockSpec(memory_space=pl.ANY)
-    part = pl.BlockSpec((rows_block, rows_y, rows_z), lambda i: (i, 0, 0))
+    part = pl.BlockSpec((rows_block, rows_y, rows_z), lambda i: (block_of(i), 0, 0))
+    count = len(inputs)
+    specs = [raw] * count + [part] * 5
+    operands = list(inputs)
+    aliases = {}
+    if prior is not None:
+        specs.append(raw)
+        aliases = {count + 5: 0}
     return pl.pallas_call(
-        stage_kernel(scale_level, scale_step, rows_block),
-        grid=(rows // rows_block,),
-        in_specs=[raw, raw, raw, part, part, part, part, part],
+        stage_kernel(scale_level, scale_step, rows_block, block_of, edges),
+        grid=(blocks,),
+        in_specs=specs,
         out_specs=part,
         out_shape=jax.ShapeDtypeStruct(level_set.shape, level_set.dtype),
         scratch_shapes=[
             pltpu.VMEM((rows + 2 * HALO, rows_y + 2 * SUB, rows_z), jnp.float32),
             pltpu.SemaphoreType.DMA((3,)),
         ],
+        input_output_aliases=aliases,
         compiler_params=pltpu.CompilerParams(dimension_semantics=("arbitrary",)),
-    )(low, field, high, edge, slope[0], slope[1], slope[2], level_set)
+    ), operands
+
+
+def stage(low, field, high, edge, slope, level_set, scale_level, scale_step):
+    rows = level_set.shape[0]
+    blocks = rows // SUB
+    extras = (edge, slope[0], slope[1], slope[2], level_set)
+    if rows % SUB != 0 or blocks < 3 or HALO > SUB:
+        call, operands = stage_call(
+            (low, field, high), None, level_set, scale_level, scale_step, 1, lambda i: 0, True
+        )
+        return call(*operands, *extras)
+    call, operands = stage_call(
+        (field,), None, level_set, scale_level, scale_step, blocks - 2, lambda i: i + 1, False
+    )
+    middle = call(*operands, *extras)
+    call, operands = stage_call(
+        (low, field, high),
+        middle,
+        level_set,
+        scale_level,
+        scale_step,
+        2,
+        lambda i: i * (blocks - 1),
+        True,
+    )
+    return call(*operands, *extras, middle)
 
 
 def shards(volume, level_set):

time: 157 us -> 164 us (1.045); the launches traced: 154 us -> 163 us
  Pallas kernels: 81.6 us -> 94.3 us
  waiting for transfers between devices: 18.5 us -> 13.2 us
  local copies, waits for them, and re-layouts: 12.7 us -> 14.6 us
    pallas_call x3 -> x6, Pallas kernels: 81.6 us -> 94.3 us  [the longest x3 47.2 us: stage(): return call(*operands, *extras, middle)]
    ppermute x8, waiting for transfers between devices: 18.5 us -> 13.2 us  [shifted(): return lax.ppermute(block, axis, route)]
    unnamed x23, local copies, waits for them, and re-layouts: 5.8 us -> 7.74 us
  transfers between devices with their start and end apart: 8 -> 8, of which waited for: 5 -> 1; matrix products, arithmetic and copies ran while one was open for 14% -> 13% of each run, Pallas kernels for 0% -> 29%
where the time goes in v5:
time: 164 us; the launch traced here: 163 us
  Pallas kernels  94.3 us (58%)
  starting transfers between devices  23.9 us (15%)
  local copies, waits for them, and re-layouts  14.6 us (9%)
  waiting for transfers between devices  13.2 us (8%)
  other arithmetic  9.03 us (6%)
  matrix products  7.06 us (4%)
    pallas_call x3, Pallas kernels, stage(): return call(*operands, *extras, middle)  47.2 us
    pallas_call x3, Pallas kernels, stage(): middle = call(*operands, *extras)  47.1 us
    ppermute x8, starting transfers between devices, shifted(): return lax.ppermute(block, axis, route)  23.9 us
    ppermute x8, waiting for transfers between devices, shifted(): return lax.ppermute(block, axis, route)  13.2 us
    unnamed x23, local copies, waits for them, and re-layouts  7.74 us
    slice x3, local copies, waits for them, and re-layouts, step(): high = shifted(field[:HALO], 'gx', -1)  3.89 us
    mul x1, other arithmetic, central_grads(): grad_z = (side[:, 1:-1, 2:] - side[:, 1:-1, :-2]) * 0.5  3.47 us
  transfers between devices with their start and end apart: 8, of which 1 were waited for; matrix products, arithmetic and copies ran while one was open for 13% of the time, Pallas kernels for 29%

profile of v5, /device:TPU:1, one launch (start us, length us, event | category | flops | bytes accessed | tf_op | source)
XLA Modules:
  0.0 163.1 jit_solution(2328444272647808227)
XLA Ops:
  0.6 2.7 %fusion.24 = (f32[14,128,128]{2,1,0:T(8,128)}, f32[14,128,128]{2,1,0:T(8,128)S(1)}) fusion(f32[32,128,128]{2,1,0:T(8,128)} %param.5), kind=kLoop, calls=%fused_computation.37 | loop fusion | bytes 3670016 | tf_op jit(solution)/shard_map/slice | solution.py:290
  3.3 4.5 %collective-permute-start = (f32[14,128,128]{2,1,0:T(8,128)}, f32[14,128,128]{2,1,0:T(8,128)}, u32[]{:S(2)}, u32[]{:S(2)}) collective-permute-start(f32[14,128,128]{2,1,0:T(8,128)} %get-tuple-element.12), channel_id=1, source_target_pairs={{0,1},{1,2},{2,3},{3,4},{4,5},{5,6},{6,7},{7,8},{8,9},{9,10},{10,1... | collective-permute-start | bytes 2752520 | tf_op jit(solution)/shard_map/ppermute | solution.py:18
  7.9 1.9 %collective-permute-start.1 = (f32[14,128,128]{2,1,0:T(8,128)S(1)}, f32[14,128,128]{2,1,0:T(8,128)}, u32[]{:S(2)}, u32[]{:S(2)}) collective-permute-start(f32[14,128,128]{2,1,0:T(8,128)S(1)} %get-tuple-element.13), channel_id=1, source_target_pairs={{1,0},{2,1},{3,2},{4,3},{5,4},{6,5},{7,6},{8,7},{9,8},{10,9},{11,1... | collective-permute-start | bytes 2752520 | tf_op jit(solution)/shard_map/ppermute | solution.py:18
  9.8 1.8 %fusion.23 = (f32[3,128,128]{2,1,0:T(8,128)}, f32[3,128,128]{2,1,0:T(8,128)}) fusion(f32[32,128,128]{2,1,0:T(8,128)} %refs_7_.5), kind=kLoop, calls=%fused_computation.36 | loop fusion | bytes 786432 | tf_op jit(solution)/shard_map/slice | solution.py:313
  11.6 1.9 %collective-permute-start.3 = (f32[3,128,128]{2,1,0:T(8,128)}, f32[3,128,128]{2,1,0:T(8,128)S(1)}, u32[]{:S(2)}, u32[]{:S(2)}) collective-permute-start(f32[3,128,128]{2,1,0:T(8,128)} %get-tuple-element.10), channel_id=1, source_target_pairs={{1,0},{2,1},{3,2},{4,3},{5,4},{6,5},{7,6},{8,7},{9,8},{10,9},{11,1... | collective-permute-start | bytes 589832 | tf_op jit(solution)/shard_map/ppermute | solution.py:18
  13.5 3.6 %collective-permute-start.2 = (f32[3,128,128]{2,1,0:T(8,128)}, f32[3,128,128]{2,1,0:T(8,128)S(1)}, u32[]{:S(2)}, u32[]{:S(2)}) collective-permute-start(f32[3,128,128]{2,1,0:T(8,128)} %get-tuple-element.11), channel_id=1, source_target_pairs={{0,1},{1,2},{2,3},{3,4},{4,5},{5,6},{6,7},{7,8},{8,9},{9,10},{10,1... | collective-permute-start | bytes 589832 | tf_op jit(solution)/shard_map/ppermute | solution.py:18
  17.2 13.2 %collective-permute-done = f32[14,128,128]{2,1,0:T(8,128)} collective-permute-done((f32[14,128,128]{2,1,0:T(8,128)}, f32[14,128,128]{2,1,0:T(8,128)}, u32[]{:S(2)}, u32[]{:S(2)}) %collective-permute-start) | collective-permute-done | bytes 917536 | tf_op jit(solution)/shard_map/ppermute | solution.py:18
  32.7 2.4 %copy.12 = f32[8,8,128,128]{3,1,2,0:T(8,128)S(1)} copy(f32[8,8,128,128]{3,2,1,0:T(8,128)S(1)} %bitcast.14) | data formatting | bytes 8388608
  35.1 2.5 %fusion.25 = f32[36,16384]{1,0:T(8,128)S(1)} fusion(f32[36,60]{1,0:T(8,128)S(1)} %copy-done.9, f32[60,16384]{1,0:T(8,128)S(1)} %bitcast.15), kind=kOutput, calls=%fused_computation.38 | convolution fusion | flops 424673280 | bytes 6300096 | tf_op jit(solution)/shard_map/dot_general | solution.py:294
  38.5 2.3 %fusion = f32[36,128,128]{1,2,0:T(8,128)S(1)} fusion(f32[128,128,1]{1,0,2:T(8,128)S(1)} %copy-done.2, f32[40,128,128]{2,1,0:T(8,128)S(1)} %bitcast.17), kind=kOutput, calls=%fused_computation.9 | convolution fusion | flops 905969664 | bytes 4784128 | tf_op jit(solution)/shard_map/dot_general | solution.py:299
  40.7 2.2 %select_bitcast_fusion = f32[36,128,128]{2,1,0:T(8,128)S(1)} fusion(f32[36,128,128]{1,2,0:T(8,128)S(1)} %fusion, f32[128,128,1]{1,0,2:T(8,128)S(1)} %copy-done.2, pred[36]{0:T(512)(128)(4,1)S(1)} %compare_and_fusion), kind=kOutput, calls=%fused_computation.11 | convolution fusion | flops 906559488 | bytes 4784164 | tf_op jit(solution)/shard_map/yv,xvz->xyz/dot_general | solution.py:302
  43.2 2.1 %fusion.15 = f32[34,128,128]{2,1,0:T(8,128)S(1)} fusion(f32[34,128,128]{2,1,0:T(8,128)S(1)} %slice.95, f32[36,128,128]{2,1,0:T(8,128)S(1)} %select_bitcast_fusion, pred[34]{0:T(512)(128)(4,1)S(1)} %slice.70), kind=kLoop, calls=%fused_computation.26 | loop fusion | flops 8355840 | bytes 8912930 | tf_op jit(solution)/shard_map/jit(_where)/select_n | solution.py:307
  45.3 1.8 %fusion.20 = (f32[32,128,128]{2,1,0:T(8,128)}, f32[32,128,128]{2,1,0:T(8,128)S(1)}) fusion(f32[34,128,128]{2,1,0:T(8,128)S(1)} %fusion.15), kind=kLoop, calls=%fused_computation.32 | loop fusion | flops 1048576 | bytes 10485760 | tf_op jit(solution)/shard_map/mul | solution.py:68
  47.1 3.5 %fusion.19 = (f32[32,128,128]{2,1,0:T(8,128)}, f32[32,128,128]{2,1,0:T(8,128)}) fusion(f32[32,128,128]{2,1,0:T(8,128)S(1)} %get-tuple-element.3.refs_1_.refs_3_), kind=kLoop, calls=%fused_computation.30 | loop fusion | flops 2097152 | bytes 6291456 | tf_op jit(solution)/shard_map/mul | solution.py:70
  50.6 15.6 %shard_map.68.refs_8_ = f32[32,128,128]{2,1,0:T(8,128)} custom-call(f32[32,128,128]{2,1,0:T(8,128)} %refs_7_.5, f32[32,128,128]{2,1,0:T(8,128)} %copy-done, f32[32,128,128]{2,1,0:T(8,128)} %get-tuple-element.2.refs_2_.refs_4_, f32[32,128,128]{2,1,0:T(8,128)} %get-tuple-element.9.refs_3_.refs_5_, f32[32,128,128]{2,1,0:T(8,128)} %get-tuple-element.8.refs_4_.refs_6_, ...), custom_call_target="tpu_custom_call" | custom-call | tf_op jit(solution)/shard_map/pallas_call | solution.py:272
  67.5 15.6 %shard_map.69.refs_0_.refs_1_ = f32[32,128,128]{2,1,0:T(8,128)} custom-call(f32[3,128,128]{2,1,0:T(8,128)} %copy-done.4, f32[32,128,128]{2,1,0:T(8,128)} %refs_7_.5, f32[3,128,128]{2,1,0:T(8,128)} %copy-done.3, f32[32,128,128]{2,1,0:T(8,128)} %copy-done, f32[32,128,128]{2,1,0:T(8,128)} %get-tuple-element.2.refs_2_.refs_4_, ...), custom_call_target="tpu_custom_call", output_to_operand_aliasing={{}: (8, {})} | custom-call | tf_op jit(solution)/shard_map/pallas_call | solution.py:283
  84.2 1.9 %collective-permute-start.5 = (f32[3,128,128]{2,1,0:T(8,128)S(1)}, f32[3,128,128]{2,1,0:T(8,128)S(1)}, u32[]{:S(2)}, u32[]{:S(2)}) collective-permute-start(f32[3,128,128]{2,1,0:T(8,128)S(1)} %get-tuple-element.6), channel_id=1, source_target_pairs={{1,0},{2,1},{3,2},{4,3},{5,4},{6,5},{7,6},{8,7},{9,8},{10,9},{11,1... | collective-permute-start | bytes 589832 | tf_op jit(solution)/shard_map/ppermute | solution.py:18
  86.1 4.4 %collective-permute-start.4 = (f32[3,128,128]{2,1,0:T(8,128)S(1)}, f32[3,128,128]{2,1,0:T(8,128)S(1)}, u32[]{:S(2)}, u32[]{:S(2)}) collective-permute-start(f32[3,128,128]{2,1,0:T(8,128)S(1)} %get-tuple-element.7), channel_id=1, source_target_pairs={{0,1},{1,2},{2,3},{3,4},{4,5},{5,6},{6,7},{7,8},{8,9},{9,10},{10,1... | collective-permute-start | bytes 589832 | tf_op jit(solution)/shard_map/ppermute | solution.py:18
  90.5 15.7 %shard_map.70.refs_8_ = f32[32,128,128]{2,1,0:T(8,128)} custom-call(f32[32,128,128]{2,1,0:T(8,128)} %shard_map.69.refs_0_.refs_1_, f32[32,128,128]{2,1,0:T(8,128)} %copy-done, f32[32,128,128]{2,1,0:T(8,128)} %get-tuple-element.2.refs_2_.refs_4_, f32[32,128,128]{2,1,0:T(8,128)} %get-tuple-element.9.refs_3_.refs_5_, ...), custom_call_target="tpu_custom_call" | custom-call | tf_op jit(solution)/shard_map/pallas_call | solution.py:272
  107.6 15.8 %shard_map.71.refs_0_.refs_1_ = f32[32,128,128]{2,1,0:T(8,128)} custom-call(f32[3,128,128]{2,1,0:T(8,128)} %copy-done.8, f32[32,128,128]{2,1,0:T(8,128)} %shard_map.69.refs_0_.refs_1_, f32[3,128,128]{2,1,0:T(8,128)} %copy-done.6, f32[32,128,128]{2,1,0:T(8,128)} %copy-done, ...), custom_call_target="tpu_custom_call", output_to_operand_aliasing={{}: (8, {})} | custom-call | tf_op jit(solution)/shard_map/pallas_call | solution.py:283
  124.5 1.9 %collective-permute-start.7 = (f32[3,128,128]{2,1,0:T(8,128)S(1)}, f32[3,128,128]{2,1,0:T(8,128)S(1)}, u32[]{:S(2)}, u32[]{:S(2)}) collective-permute-start(f32[3,128,128]{2,1,0:T(8,128)S(1)} %get-tuple-element.4), channel_id=1, source_target_pairs={{1,0},{2,1},{3,2},{4,3},{5,4},{6,5},{7,6},{8,7},{9,8},{10,9},{11,1... | collective-permute-start | bytes 589832 | tf_op jit(solution)/shard_map/ppermute | solution.py:18
  126.4 3.6 %collective-permute-start.6 = (f32[3,128,128]{2,1,0:T(8,128)S(1)}, f32[3,128,128]{2,1,0:T(8,128)S(1)}, u32[]{:S(2)}, u32[]{:S(2)}) collective-permute-start(f32[3,128,128]{2,1,0:T(8,128)S(1)} %get-tuple-element.5), channel_id=1, source_target_pairs={{0,1},{1,2},{2,3},{3,4},{4,5},{5,6},{6,7},{7,8},{8,9},{9,10},{10,1... | collective-permute-start | bytes 589832 | tf_op jit(solution)/shard_map/ppermute | solution.py:18
  130.1 15.7 %shard_map.72.refs_8_ = f32[32,128,128]{2,1,0:T(8,128)} custom-call(f32[32,128,128]{2,1,0:T(8,128)} %shard_map.71.refs_0_.refs_1_, f32[32,128,128]{2,1,0:T(8,128)} %copy-done, f32[32,128,128]{2,1,0:T(8,128)} %get-tuple-element.2.refs_2_.refs_4_, f32[32,128,128]{2,1,0:T(8,128)} %get-tuple-element.9.refs_3_.refs_5_, ...), custom_call_target="tpu_custom_call" | custom-call | tf_op jit(solution)/shard_map/pallas_call | solution.py:272
  147.2 15.8 %shard_map.73 = f32[32,128,128]{2,1,0:T(8,128)} custom-call(f32[3,128,128]{2,1,0:T(8,128)} %copy-done.7, f32[32,128,128]{2,1,0:T(8,128)} %shard_map.71.refs_0_.refs_1_, f32[3,128,128]{2,1,0:T(8,128)} %copy-done.5, f32[32,128,128]{2,1,0:T(8,128)} %copy-done, f32[32,128,128]{2,1,0:T(8,128)} %get-tuple-element.2.refs_2_.refs_4_, ...), custom_call_target="tpu_custom_call", output_to_operand_aliasing={{}: (8, {})} | custom-call | tf_op jit(solution)/shard_map/pallas_call | solution.py:283
  (35 shorter events, 9.5 us)
Async XLA Ops:
  0.6 29.8 %copy-start.1 = (f32[32,128,128]{2,1,0:T(8,128)S(1)}, f32[32,128,128]{2,1,0:T(8,128)}, u32[]{:S(2)}) copy-start(f32[32,128,128]{2,1,0:T(8,128)} %param.5) | copy-start | bytes 6291460
  3.3 27.1 %collective-permute-start = (f32[14,128,128]{2,1,0:T(8,128)}, f32[14,128,128]{2,1,0:T(8,128)}, u32[]{:S(2)}, u32[]{:S(2)}) collective-permute-start(f32[14,128,128]{2,1,0:T(8,128)} %get-tuple-element.12), channel_id=1, source_target_pairs={{0,1},{1,2},{2,3},{3,4},{4,5},{5,6},{6,7},{7,8},{8,9},{9,10},{10,1... | collective-permute-start | bytes 2752520 | tf_op jit(solution)/shard_map/ppermute | solution.py:18
  7.9 22.6 %collective-permute-start.1 = (f32[14,128,128]{2,1,0:T(8,128)S(1)}, f32[14,128,128]{2,1,0:T(8,128)}, u32[]{:S(2)}, u32[]{:S(2)}) collective-permute-start(f32[14,128,128]{2,1,0:T(8,128)S(1)} %get-tuple-element.13), channel_id=1, source_target_pairs={{1,0},{2,1},{3,2},{4,3},{5,4},{6,5},{7,6},{8,7},{9,8},{10,9},{11,1... | collective-permute-start | bytes 2752520 | tf_op jit(solution)/shard_map/ppermute | solution.py:18
  11.6 54.6 %collective-permute-start.3 = (f32[3,128,128]{2,1,0:T(8,128)}, f32[3,128,128]{2,1,0:T(8,128)S(1)}, u32[]{:S(2)}, u32[]{:S(2)}) collective-permute-start(f32[3,128,128]{2,1,0:T(8,128)} %get-tuple-element.10), channel_id=1, source_target_pairs={{1,0},{2,1},{3,2},{4,3},{5,4},{6,5},{7,6},{8,7},{9,8},{10,9},{11,1... | collective-permute-start | bytes 589832 | tf_op jit(solution)/shard_map/ppermute | solution.py:18
  13.5 52.7 %collective-permute-start.2 = (f32[3,128,128]{2,1,0:T(8,128)}, f32[3,128,128]{2,1,0:T(8,128)S(1)}, u32[]{:S(2)}, u32[]{:S(2)}) collective-permute-start(f32[3,128,128]{2,1,0:T(8,128)} %get-tuple-element.11), channel_id=1, source_target_pairs={{0,1},{1,2},{2,3},{3,4},{4,5},{5,6},{6,7},{7,8},{8,9},{9,10},{10,1... | collective-permute-start | bytes 589832 | tf_op jit(solution)/shard_map/ppermute | solution.py:18
  32.7 2.4 %copy-start.9 = (f32[36,60]{1,0:T(8,128)S(1)}, f32[36,60]{1,0:T(8,128)}, u32[]{:S(2)}) copy-start(f32[36,60]{1,0:T(8,128)} %constant.28.clone) | copy-start | bytes 25924
  37.6 0.8 copy-start.2
  47.1 3.5 %copy-start = (f32[32,128,128]{2,1,0:T(8,128)}, f32[32,128,128]{2,1,0:T(8,128)S(1)}, u32[]{:S(2)}) copy-start(f32[32,128,128]{2,1,0:T(8,128)S(1)} %get-tuple-element.3.refs_1_.refs_3_) | copy-start | bytes 6291460
  66.2 0.7 copy-start.3
  66.9 0.7 copy-start.4
  84.2 22.1 %collective-permute-start.5 = (f32[3,128,128]{2,1,0:T(8,128)S(1)}, f32[3,128,128]{2,1,0:T(8,128)S(1)}, u32[]{:S(2)}, u32[]{:S(2)}) collective-permute-start(f32[3,128,128]{2,1,0:T(8,128)S(1)} %get-tuple-element.6), channel_id=1, source_target_pairs={{1,0},{2,1},{3,2},{4,3},{5,4},{6,5},{7,6},{8,7},{9,8},{10,9},{11,1... | collective-permute-start | bytes 589832 | tf_op jit(solution)/shard_map/ppermute | solution.py:18
  86.1 20.2 %collective-permute-start.4 = (f32[3,128,128]{2,1,0:T(8,128)S(1)}, f32[3,128,128]{2,1,0:T(8,128)S(1)}, u32[]{:S(2)}, u32[]{:S(2)}) collective-permute-start(f32[3,128,128]{2,1,0:T(8,128)S(1)} %get-tuple-element.7), channel_id=1, source_target_pairs={{0,1},{1,2},{2,3},{3,4},{4,5},{5,6},{6,7},{7,8},{8,9},{9,10},{10,1... | collective-permute-start | bytes 589832 | tf_op jit(solution)/shard_map/ppermute | solution.py:18
  106.3 0.7 copy-start.6
  107.0 0.7 copy-start.8
  124.5 21.3 %collective-permute-start.7 = (f32[3,128,128]{2,1,0:T(8,128)S(1)}, f32[3,128,128]{2,1,0:T(8,128)S(1)}, u32[]{:S(2)}, u32[]{:S(2)}) collective-permute-start(f32[3,128,128]{2,1,0:T(8,128)S(1)} %get-tuple-element.4), channel_id=1, source_target_pairs={{1,0},{2,1},{3,2},{4,3},{5,4},{6,5},{7,6},{8,7},{9,8},{10,9},{11,1... | collective-permute-start | bytes 589832 | tf_op jit(solution)/shard_map/ppermute | solution.py:18
  126.4 19.4 %collective-permute-start.6 = (f32[3,128,128]{2,1,0:T(8,128)S(1)}, f32[3,128,128]{2,1,0:T(8,128)S(1)}, u32[]{:S(2)}, u32[]{:S(2)}) collective-permute-start(f32[3,128,128]{2,1,0:T(8,128)S(1)} %get-tuple-element.5), channel_id=1, source_target_pairs={{0,1},{1,2},{2,3},{3,4},{4,5},{5,6},{6,7},{7,8},{8,9},{9,10},{10,1... | collective-permute-start | bytes 589832 | tf_op jit(solution)/shard_map/ppermute | solution.py:18
  145.9 0.7 copy-start.5
  146.5 0.7 copy-start.7

commit v6 on v4

--- a/solution.py
+++ b/solution.py
@@ -77,17 +77,21 @@
 
 
 def weno(first, second, third, fourth, fifth):
+    step_one = second - first
+    step_two = third - second
+    step_three = fourth - third
+    step_four = fifth - fourth
     cand_one = 2.0 * first - 7.0 * second + 11.0 * third
     cand_two = -second + 5.0 * third + 2.0 * fourth
     cand_three = 2.0 * third + 5.0 * fourth - fifth
-    part_a = first - 2.0 * second + third
-    part_b = first - 4.0 * second + 3.0 * third
+    part_a = step_two - step_one
+    part_b = 3.0 * step_two - step_one
     smooth_one = 13.0 / 12.0 * part_a * part_a + 0.25 * part_b * part_b
-    part_a = second - 2.0 * third + fourth
-    part_b = second - fourth
+    part_a = step_three - step_two
+    part_b = step_two + step_three
     smooth_two = 13.0 / 12.0 * part_a * part_a + 0.25 * part_b * part_b
-    part_a = third - 2.0 * fourth + fifth
-    part_b = 3.0 * third - 4.0 * fourth + fifth
+    part_a = step_four - step_three
+    part_b = step_four - 3.0 * step_three
     smooth_three = 13.0 / 12.0 * part_a * part_a + 0.25 * part_b * part_b
     denom_one = 1e-06 + smooth_one
     denom_two = 1e-06 + smooth_two
@@ -103,11 +107,11 @@
     )
 
 
-def upwind(values, speed):
+def upwind(values, slope):
     diffs = [values[k + 1] - values[k] for k in range(6)]
-    ahead = speed > 0.0
+    ahead = slope < 0.0
     chosen = [jnp.where(ahead, diffs[k], diffs[5 - k]) for k in range(5)]
-    return speed * weno(*chosen)
+    return slope * weno(*chosen)
 
 
 SUB = 8
@@ -149,7 +153,7 @@
 
         def along_z(tile, step):
             moved = pltpu.roll(tile, (-step) % rows_z, 1)
-            keep = (lane + step >= 0) & (lane + step < rows_z)
+            keep = lane < rows_z - step if step > 0 else lane >= -step
             return jnp.where(keep, moved, 0.0)
 
         def row(r, carry):
@@ -165,12 +169,9 @@
                 line_y = [at(0, k) for k in range(-HALO, HALO + 1)]
                 line_z = [along_z(centre, k) for k in range(-HALO, HALO + 1)]
                 here = pl.ds(chunk * SUB, SUB)
-                speed_x = -sx_ref[r, here, :]
-                speed_y = -sy_ref[r, here, :]
-                speed_z = -sz_ref[r, here, :]
-                flow_x = upwind(line_x, speed_x)
-                flow_y = upwind(line_y, speed_y)
-                flow_z = upwind(line_z, speed_z)
+                flow_x = upwind(line_x, sx_ref[r, here, :])
+                flow_y = upwind(line_y, sy_ref[r, here, :])
+                flow_z = upwind(line_z, sz_ref[r, here, :])
                 up_x = line_x[HALO + 1]
                 down_x = line_x[HALO - 1]
                 up_y = line_y[HALO + 1]
@@ -184,12 +185,10 @@
                 second_yy = up_y - 2.0 * centre + down_y
                 second_zz = up_z - 2.0 * centre + down_z
                 mixed_xy = (at(1, 1) - at(1, -1) - at(-1, 1) + at(-1, -1)) * 0.25
-                mixed_xz = (
-                    along_z(up_x, 1) - along_z(up_x, -1) - along_z(down_x, 1) + along_z(down_x, -1)
-                ) * 0.25
-                mixed_yz = (
-                    along_z(up_y, 1) - along_z(up_y, -1) - along_z(down_y, 1) + along_z(down_y, -1)
-                ) * 0.25
+                across_x = up_x - down_x
+                across_y = up_y - down_y
+                mixed_xz = (along_z(across_x, 1) - along_z(across_x, -1)) * 0.25
+                mixed_yz = (along_z(across_y, 1) - along_z(across_y, -1)) * 0.25
                 square_x = first_x * first_x
                 square_y = first_y * first_y
                 square_z = first_z * first_z
@@ -204,8 +203,7 @@
                     + first_y * first_z * mixed_yz
                 )
                 curvature = numerator / (square_x + square_y + square_z + 1.0)
-                transport = flow_x + flow_y + flow_z
-                rate = edge_ref[r, here, :] * curvature - transport
+                rate = edge_ref[r, here, :] * curvature + (flow_x + flow_y + flow_z)
                 moved = centre + 0.1 * rate
                 if scale_level is None:
                     out_ref[r, here, :] = moved

time: 157 us -> 151 us (0.962)
  Pallas kernels: 81.6 us -> 75.2 us
    pallas_call x3, Pallas kernels: 81.6 us -> 75.2 us  [stage(): pl.pallas_call(stage_kernel(scale_level, scale_step, rows_block), grid=(r...]
  transfers between devices with their start and end apart: 8 -> 8, of which waited for: 5 -> 5; matrix products, arithmetic and copies ran while one was open for 14% -> 15% of each run, Pallas kernels for 0% -> 0%
where the time goes in v6:
time: 151 us; the launch traced here: 148 us
  Pallas kernels  75.2 us (50%)
  starting transfers between devices  24.6 us (16%)
  waiting for transfers between devices  18.5 us (12%)
  local copies, waits for them, and re-layouts  12.7 us (8%)
  other arithmetic  9.03 us (6%)
  matrix products  7.06 us (5%)
    pallas_call x3, Pallas kernels, stage(): pl.pallas_call(stage_kernel(scale_level, scale_step, rows_block), grid=(r...  75.2 us
    ppermute x8, starting transfers between devices, shifted(): return lax.ppermute(block, axis, route)  24.6 us
    ppermute x8, waiting for transfers between devices, shifted(): return lax.ppermute(block, axis, route)  18.5 us
    unnamed x23, local copies, waits for them, and re-layouts  5.8 us
    slice x3, local copies, waits for them, and re-layouts, step(): high = shifted(field[:HALO], 'gx', -1)  3.89 us
    mul x1, other arithmetic, central_grads(): grad_z = (side[:, 1:-1, 2:] - side[:, 1:-1, :-2]) * 0.5  3.47 us
  transfers between devices with their start and end apart: 8, of which 5 were waited for; matrix products, arithmetic and copies ran while one was open for 15% of the time, Pallas kernels for 0%

profile of v6, /device:TPU:1, one launch (start us, length us, event | category | flops | bytes accessed | tf_op | source)
XLA Modules:
  0.0 148.1 jit_solution(13699064362003491225)
XLA Ops:
  0.6 2.7 %fusion.24 = (f32[14,128,128]{2,1,0:T(8,128)}, f32[14,128,128]{2,1,0:T(8,128)S(1)}) fusion(f32[32,128,128]{2,1,0:T(8,128)} %param.5), kind=kLoop, calls=%fused_computation.37 | loop fusion | bytes 3670016 | tf_op jit(solution)/shard_map/slice | solution.py:242
  3.3 4.5 %collective-permute-start = (f32[14,128,128]{2,1,0:T(8,128)}, f32[14,128,128]{2,1,0:T(8,128)}, u32[]{:S(2)}, u32[]{:S(2)}) collective-permute-start(f32[14,128,128]{2,1,0:T(8,128)} %get-tuple-element.12), channel_id=1, source_target_pairs={{0,1},{1,2},{2,3},{3,4},{4,5},{5,6},{6,7},{7,8},{8,9},{9,10},{10,1... | collective-permute-start | bytes 2752520 | tf_op jit(solution)/shard_map/ppermute | solution.py:18
  7.9 1.9 %collective-permute-start.1 = (f32[14,128,128]{2,1,0:T(8,128)S(1)}, f32[14,128,128]{2,1,0:T(8,128)}, u32[]{:S(2)}, u32[]{:S(2)}) collective-permute-start(f32[14,128,128]{2,1,0:T(8,128)S(1)} %get-tuple-element.13), channel_id=1, source_target_pairs={{1,0},{2,1},{3,2},{4,3},{5,4},{6,5},{7,6},{8,7},{9,8},{10,9},{11,1... | collective-permute-start | bytes 2752520 | tf_op jit(solution)/shard_map/ppermute | solution.py:18
  9.8 1.8 %fusion.23 = (f32[3,128,128]{2,1,0:T(8,128)}, f32[3,128,128]{2,1,0:T(8,128)}) fusion(f32[32,128,128]{2,1,0:T(8,128)} %ls_ref.5), kind=kLoop, calls=%fused_computation.36 | loop fusion | bytes 786432 | tf_op jit(solution)/shard_map/slice | solution.py:265
  11.6 1.9 %collective-permute-start.3 = (f32[3,128,128]{2,1,0:T(8,128)}, f32[3,128,128]{2,1,0:T(8,128)S(1)}, u32[]{:S(2)}, u32[]{:S(2)}) collective-permute-start(f32[3,128,128]{2,1,0:T(8,128)} %get-tuple-element.10), channel_id=1, source_target_pairs={{1,0},{2,1},{3,2},{4,3},{5,4},{6,5},{7,6},{8,7},{9,8},{10,9},{11,1... | collective-permute-start | bytes 589832 | tf_op jit(solution)/shard_map/ppermute | solution.py:18
  13.5 3.6 %collective-permute-start.2 = (f32[3,128,128]{2,1,0:T(8,128)}, f32[3,128,128]{2,1,0:T(8,128)S(1)}, u32[]{:S(2)}, u32[]{:S(2)}) collective-permute-start(f32[3,128,128]{2,1,0:T(8,128)} %get-tuple-element.11), channel_id=1, source_target_pairs={{0,1},{1,2},{2,3},{3,4},{4,5},{5,6},{6,7},{7,8},{8,9},{9,10},{10,1... | collective-permute-start | bytes 589832 | tf_op jit(solution)/shard_map/ppermute | solution.py:18
  17.2 13.2 %collective-permute-done = f32[14,128,128]{2,1,0:T(8,128)} collective-permute-done((f32[14,128,128]{2,1,0:T(8,128)}, f32[14,128,128]{2,1,0:T(8,128)}, u32[]{:S(2)}, u32[]{:S(2)}) %collective-permute-start) | collective-permute-done | bytes 917536 | tf_op jit(solution)/shard_map/ppermute | solution.py:18
  30.4 1.7 %pad_maximum_fusion = f32[60,128,128]{2,1,0:T(8,128)S(1)} fusion(f32[14,128,128]{2,1,0:T(8,128)} %collective-permute-done.1, f32[32,128,128]{2,1,0:T(8,128)S(1)} %copy-done.1, f32[14,128,128]{2,1,0:T(8,128)} %collective-permute-done), kind=kLoop, calls=%fused_computation.8 | loop fusion | flops 1966080 | bytes 7864320 | tf_op jit(solution)/shard_map/concatenate | solution.py:244
  32.7 2.4 %copy.9 = f32[8,8,128,128]{3,1,2,0:T(8,128)S(1)} copy(f32[8,8,128,128]{3,2,1,0:T(8,128)S(1)} %bitcast.14) | data formatting | bytes 8388608
  35.1 2.5 %fusion.25 = f32[36,16384]{1,0:T(8,128)S(1)} fusion(f32[36,60]{1,0:T(8,128)S(1)} %copy-done.9, f32[60,16384]{1,0:T(8,128)S(1)} %bitcast.15), kind=kOutput, calls=%fused_computation.38 | convolution fusion | flops 424673280 | bytes 6300096 | tf_op jit(solution)/shard_map/dot_general | solution.py:246
  38.5 2.3 %fusion = f32[36,128,128]{1,2,0:T(8,128)S(1)} fusion(f32[128,128,1]{1,0,2:T(8,128)S(1)} %copy-done.2, f32[40,128,128]{2,1,0:T(8,128)S(1)} %bitcast.17), kind=kOutput, calls=%fused_computation.9 | convolution fusion | flops 905969664 | bytes 4784128 | tf_op jit(solution)/shard_map/dot_general | solution.py:251
  40.7 2.2 %select_bitcast_fusion = f32[36,128,128]{2,1,0:T(8,128)S(1)} fusion(f32[36,128,128]{1,2,0:T(8,128)S(1)} %fusion, f32[128,128,1]{1,0,2:T(8,128)S(1)} %copy-done.2, pred[36]{0:T(512)(128)(4,1)S(1)} %compare_and_fusion), kind=kOutput, calls=%fused_computation.11 | convolution fusion | flops 906559488 | bytes 4784164 | tf_op jit(solution)/shard_map/yv,xvz->xyz/dot_general | solution.py:254
  43.2 2.1 %fusion.15 = f32[34,128,128]{2,1,0:T(8,128)S(1)} fusion(f32[34,128,128]{2,1,0:T(8,128)S(1)} %slice.95, f32[36,128,128]{2,1,0:T(8,128)S(1)} %select_bitcast_fusion, pred[34]{0:T(512)(128)(4,1)S(1)} %slice.70), kind=kLoop, calls=%fused_computation.26 | loop fusion | flops 8355840 | bytes 8912930 | tf_op jit(solution)/shard_map/jit(_where)/select_n | solution.py:259
  45.3 1.8 %fusion.20 = (f32[32,128,128]{2,1,0:T(8,128)}, f32[32,128,128]{2,1,0:T(8,128)S(1)}) fusion(f32[34,128,128]{2,1,0:T(8,128)S(1)} %fusion.15), kind=kLoop, calls=%fused_computation.32 | loop fusion | flops 1048576 | bytes 10485760 | tf_op jit(solution)/shard_map/mul | solution.py:68
  47.1 3.5 %fusion.19 = (f32[32,128,128]{2,1,0:T(8,128)}, f32[32,128,128]{2,1,0:T(8,128)}) fusion(f32[32,128,128]{2,1,0:T(8,128)S(1)} %get-tuple-element.3.edge_ref), kind=kLoop, calls=%fused_computation.30 | loop fusion | flops 2097152 | bytes 6291456 | tf_op jit(solution)/shard_map/mul | solution.py:70
  51.3 24.9 %shard_map.68.main_ref = f32[32,128,128]{2,1,0:T(8,128)} custom-call(f32[3,128,128]{2,1,0:T(8,128)} %copy-done.4, f32[32,128,128]{2,1,0:T(8,128)} %ls_ref.5, f32[3,128,128]{2,1,0:T(8,128)} %copy-done.3, f32[32,128,128]{2,1,0:T(8,128)} %copy-done, f32[32,128,128]{2,1,0:T(8,128)} %get-tuple-element.2.sx_ref, f32[32,128,128]{2,1,0:T(8,128)} %get-tuple-element.9.sy_ref, ...), custom_call_target="tpu_custom_call" | custom-call | tf_op jit(solution)/shard_map/pallas_call | solution.py:224
  77.3 1.9 %collective-permute-start.5 = (f32[3,128,128]{2,1,0:T(8,128)S(1)}, f32[3,128,128]{2,1,0:T(8,128)S(1)}, u32[]{:S(2)}, u32[]{:S(2)}) collective-permute-start(f32[3,128,128]{2,1,0:T(8,128)S(1)} %get-tuple-element.6), channel_id=1, source_target_pairs={{1,0},{2,1},{3,2},{4,3},{5,4},{6,5},{7,6},{8,7},{9,8},{10,9},{11,1... | collective-permute-start | bytes 589832 | tf_op jit(solution)/shard_map/ppermute | solution.py:18
  79.2 4.4 %collective-permute-start.4 = (f32[3,128,128]{2,1,0:T(8,128)S(1)}, f32[3,128,128]{2,1,0:T(8,128)S(1)}, u32[]{:S(2)}, u32[]{:S(2)}) collective-permute-start(f32[3,128,128]{2,1,0:T(8,128)S(1)} %get-tuple-element.7), channel_id=1, source_target_pairs={{0,1},{1,2},{2,3},{3,4},{4,5},{5,6},{6,7},{7,8},{8,9},{9,10},{10,1... | collective-permute-start | bytes 589832 | tf_op jit(solution)/shard_map/ppermute | solution.py:18
  83.6 1.4 collective-permute-done.5.high_ref
  86.9 25.2 %shard_map.69.main_ref = f32[32,128,128]{2,1,0:T(8,128)} custom-call(f32[3,128,128]{2,1,0:T(8,128)} %copy-done.8, f32[32,128,128]{2,1,0:T(8,128)} %shard_map.68.main_ref, f32[3,128,128]{2,1,0:T(8,128)} %copy-done.6, f32[32,128,128]{2,1,0:T(8,128)} %copy-done, f32[32,128,128]{2,1,0:T(8,128)} %get-tuple-element.2.sx_ref, ...), custom_call_target="tpu_custom_call" | custom-call | tf_op jit(solution)/shard_map/pallas_call | solution.py:224
  113.1 1.9 %collective-permute-start.7 = (f32[3,128,128]{2,1,0:T(8,128)S(1)}, f32[3,128,128]{2,1,0:T(8,128)S(1)}, u32[]{:S(2)}, u32[]{:S(2)}) collective-permute-start(f32[3,128,128]{2,1,0:T(8,128)S(1)} %get-tuple-element.4), channel_id=1, source_target_pairs={{1,0},{2,1},{3,2},{4,3},{5,4},{6,5},{7,6},{8,7},{9,8},{10,9},{11,1... | collective-permute-start | bytes 589832 | tf_op jit(solution)/shard_map/ppermute | solution.py:18
  115.0 4.4 %collective-permute-start.6 = (f32[3,128,128]{2,1,0:T(8,128)S(1)}, f32[3,128,128]{2,1,0:T(8,128)S(1)}, u32[]{:S(2)}, u32[]{:S(2)}) collective-permute-start(f32[3,128,128]{2,1,0:T(8,128)S(1)} %get-tuple-element.5), channel_id=1, source_target_pairs={{0,1},{1,2},{2,3},{3,4},{4,5},{5,6},{6,7},{7,8},{8,9},{9,10},{10,1... | collective-permute-start | bytes 589832 | tf_op jit(solution)/shard_map/ppermute | solution.py:18
  119.4 1.4 collective-permute-done.7.high_ref
  122.8 25.1 %shard_map.70 = f32[32,128,128]{2,1,0:T(8,128)} custom-call(f32[3,128,128]{2,1,0:T(8,128)} %copy-done.7, f32[32,128,128]{2,1,0:T(8,128)} %shard_map.69.main_ref, f32[3,128,128]{2,1,0:T(8,128)} %copy-done.5, f32[32,128,128]{2,1,0:T(8,128)} %copy-done, f32[32,128,128]{2,1,0:T(8,128)} %get-tuple-element.2.sx_ref, f32[32,128,128]{2,1,0:T(8,128)} %get-tuple-element.9.sy_ref, ...), custom_call_target="tpu_custom_call" | custom-call | tf_op jit(solution)/shard_map/pallas_call | solution.py:224
  (32 shorter events, 8.3 us)
Async XLA Ops:
  0.6 29.8 %copy-start.1 = (f32[32,128,128]{2,1,0:T(8,128)S(1)}, f32[32,128,128]{2,1,0:T(8,128)}, u32[]{:S(2)}) copy-start(f32[32,128,128]{2,1,0:T(8,128)} %param.5) | copy-start | bytes 6291460
  3.3 27.1 %collective-permute-start = (f32[14,128,128]{2,1,0:T(8,128)}, f32[14,128,128]{2,1,0:T(8,128)}, u32[]{:S(2)}, u32[]{:S(2)}) collective-permute-start(f32[14,128,128]{2,1,0:T(8,128)} %get-tuple-element.12), channel_id=1, source_target_pairs={{0,1},{1,2},{2,3},{3,4},{4,5},{5,6},{6,7},{7,8},{8,9},{9,10},{10,1... | collective-permute-start | bytes 2752520 | tf_op jit(solution)/shard_map/ppermute | solution.py:18
  7.9 22.6 %collective-permute-start.1 = (f32[14,128,128]{2,1,0:T(8,128)S(1)}, f32[14,128,128]{2,1,0:T(8,128)}, u32[]{:S(2)}, u32[]{:S(2)}) collective-permute-start(f32[14,128,128]{2,1,0:T(8,128)S(1)} %get-tuple-element.13), channel_id=1, source_target_pairs={{1,0},{2,1},{3,2},{4,3},{5,4},{6,5},{7,6},{8,7},{9,8},{10,9},{11,1... | collective-permute-start | bytes 2752520 | tf_op jit(solution)/shard_map/ppermute | solution.py:18
  11.6 39.0 %collective-permute-start.3 = (f32[3,128,128]{2,1,0:T(8,128)}, f32[3,128,128]{2,1,0:T(8,128)S(1)}, u32[]{:S(2)}, u32[]{:S(2)}) collective-permute-start(f32[3,128,128]{2,1,0:T(8,128)} %get-tuple-element.10), channel_id=1, source_target_pairs={{1,0},{2,1},{3,2},{4,3},{5,4},{6,5},{7,6},{8,7},{9,8},{10,9},{11,1... | collective-permute-start | bytes 589832 | tf_op jit(solution)/shard_map/ppermute | solution.py:18
  13.5 37.1 %collective-permute-start.2 = (f32[3,128,128]{2,1,0:T(8,128)}, f32[3,128,128]{2,1,0:T(8,128)S(1)}, u32[]{:S(2)}, u32[]{:S(2)}) collective-permute-start(f32[3,128,128]{2,1,0:T(8,128)} %get-tuple-element.11), channel_id=1, source_target_pairs={{0,1},{1,2},{2,3},{3,4},{4,5},{5,6},{6,7},{7,8},{8,9},{9,10},{10,1... | collective-permute-start | bytes 589832 | tf_op jit(solution)/shard_map/ppermute | solution.py:18
  32.7 2.4 %copy-start.9 = (f32[36,60]{1,0:T(8,128)S(1)}, f32[36,60]{1,0:T(8,128)}, u32[]{:S(2)}) copy-start(f32[36,60]{1,0:T(8,128)} %constant.28.clone) | copy-start | bytes 25924
  37.6 0.8 copy-start.2
  47.1 3.5 %copy-start = (f32[32,128,128]{2,1,0:T(8,128)}, f32[32,128,128]{2,1,0:T(8,128)S(1)}, u32[]{:S(2)}) copy-start(f32[32,128,128]{2,1,0:T(8,128)S(1)} %get-tuple-element.3.edge_ref) | copy-start | bytes 6291460
  50.6 0.7 copy-start.3
  50.6 0.7 copy-start.4
  77.3 7.7 %collective-permute-start.5 = (f32[3,128,128]{2,1,0:T(8,128)S(1)}, f32[3,128,128]{2,1,0:T(8,128)S(1)}, u32[]{:S(2)}, u32[]{:S(2)}) collective-permute-start(f32[3,128,128]{2,1,0:T(8,128)S(1)} %get-tuple-element.6), channel_id=1, source_target_pairs={{1,0},{2,1},{3,2},{4,3},{5,4},{6,5},{7,6},{8,7},{9,8},{10,9},{11,1... | collective-permute-start | bytes 589832 | tf_op jit(solution)/shard_map/ppermute | solution.py:18
  79.2 7.0 %collective-permute-start.4 = (f32[3,128,128]{2,1,0:T(8,128)S(1)}, f32[3,128,128]{2,1,0:T(8,128)S(1)}, u32[]{:S(2)}, u32[]{:S(2)}) collective-permute-start(f32[3,128,128]{2,1,0:T(8,128)S(1)} %get-tuple-element.7), channel_id=1, source_target_pairs={{0,1},{1,2},{2,3},{3,4},{4,5},{5,6},{6,7},{7,8},{8,9},{9,10},{10,1... | collective-permute-start | bytes 589832 | tf_op jit(solution)/shard_map/ppermute | solution.py:18
  85.0 1.2 copy-start.6
  86.2 0.7 copy-start.8
  113.1 7.7 %collective-permute-start.7 = (f32[3,128,128]{2,1,0:T(8,128)S(1)}, f32[3,128,128]{2,1,0:T(8,128)S(1)}, u32[]{:S(2)}, u32[]{:S(2)}) collective-permute-start(f32[3,128,128]{2,1,0:T(8,128)S(1)} %get-tuple-element.4), channel_id=1, source_target_pairs={{1,0},{2,1},{3,2},{4,3},{5,4},{6,5},{7,6},{8,7},{9,8},{10,9},{11,1... | collective-permute-start | bytes 589832 | tf_op jit(solution)/shard_map/ppermute | solution.py:18
  115.0 7.1 %collective-permute-start.6 = (f32[3,128,128]{2,1,0:T(8,128)S(1)}, f32[3,128,128]{2,1,0:T(8,128)S(1)}, u32[]{:S(2)}, u32[]{:S(2)}) collective-permute-start(f32[3,128,128]{2,1,0:T(8,128)S(1)} %get-tuple-element.5), channel_id=1, source_target_pairs={{0,1},{1,2},{2,3},{3,4},{4,5},{5,6},{6,7},{7,8},{8,9},{9,10},{10,1... | collective-permute-start | bytes 589832 | tf_op jit(solution)/shard_map/ppermute | solution.py:18
  120.8 1.3 copy-start.5
  122.2 0.7 copy-start.7

commit v7 on v6

--- a/solution.py
+++ b/solution.py
@@ -81,9 +81,9 @@
     step_two = third - second
     step_three = fourth - third
     step_four = fifth - fourth
-    cand_one = 2.0 * first - 7.0 * second + 11.0 * third
-    cand_two = -second + 5.0 * third + 2.0 * fourth
-    cand_three = 2.0 * third + 5.0 * fourth - fifth
+    cand_one = 5.0 * step_two - 2.0 * step_one
+    cand_two = step_two + 2.0 * step_three
+    cand_three = 4.0 * step_three - step_four
     part_a = step_two - step_one
     part_b = 3.0 * step_two - step_one
     smooth_one = 13.0 / 12.0 * part_a * part_a + 0.25 * part_b * part_b
@@ -102,7 +102,7 @@
     weight_one = 0.1 * (square_two * square_three)
     weight_two = 0.6 * (square_one * square_three)
     weight_three = 0.3 * (square_one * square_two)
-    return (weight_one * cand_one + weight_two * cand_two + weight_three * cand_three) / (
+    return third + (weight_one * cand_one + weight_two * cand_two + weight_three * cand_three) / (
         6.0 * (weight_one + weight_two + weight_three)
     )
 
@@ -178,17 +178,15 @@
                 down_y = line_y[HALO - 1]
                 up_z = line_z[HALO + 1]
                 down_z = line_z[HALO - 1]
-                first_x = (up_x - down_x) * 0.5
-                first_y = (up_y - down_y) * 0.5
-                first_z = (up_z - down_z) * 0.5
+                first_x = up_x - down_x
+                first_y = up_y - down_y
+                first_z = up_z - down_z
                 second_xx = up_x - 2.0 * centre + down_x
                 second_yy = up_y - 2.0 * centre + down_y
                 second_zz = up_z - 2.0 * centre + down_z
-                mixed_xy = (at(1, 1) - at(1, -1) - at(-1, 1) + at(-1, -1)) * 0.25
-                across_x = up_x - down_x
-                across_y = up_y - down_y
-                mixed_xz = (along_z(across_x, 1) - along_z(across_x, -1)) * 0.25
-                mixed_yz = (along_z(across_y, 1) - along_z(across_y, -1)) * 0.25
+                mixed_xy = at(1, 1) - at(1, -1) - at(-1, 1) + at(-1, -1)
+                mixed_xz = along_z(first_x, 1) - along_z(first_x, -1)
+                mixed_yz = along_z(first_y, 1) - along_z(first_y, -1)
                 square_x = first_x * first_x
                 square_y = first_y * first_y
                 square_z = first_z * first_z
@@ -197,12 +195,12 @@
                     + second_yy * (square_x + square_z)
                     + second_zz * (square_x + square_y)
                 )
-                numerator = numerator - 2.0 * (
+                numerator = numerator - 0.5 * (
                     first_x * first_y * mixed_xy
                     + first_x * first_z * mixed_xz
                     + first_y * first_z * mixed_yz
                 )
-                curvature = numerator / (square_x + square_y + square_z + 1.0)
+                curvature = numerator / (square_x + square_y + square_z + 4.0)
                 rate = edge_ref[r, here, :] * curvature + (flow_x + flow_y + flow_z)
                 moved = centre + 0.1 * rate
                 if scale_level is None:

time: 151 us -> 147 us (0.974)
  Pallas kernels: 75.2 us -> 71.2 us
    pallas_call x3, Pallas kernels: 75.2 us -> 71.2 us  [stage(): pl.pallas_call(stage_kernel(scale_level, scale_step, rows_block), grid=(r...]
where the time goes in v7:
time: 147 us; the launch traced here: 144 us
  Pallas kernels  71.2 us (48%)
  starting transfers between devices  24.6 us (17%)
  waiting for transfers between devices  18.5 us (13%)
  local copies, waits for them, and re-layouts  12.7 us (9%)
  other arithmetic  9.03 us (6%)
  matrix products  7.06 us (5%)
    pallas_call x3, Pallas kernels, stage(): pl.pallas_call(stage_kernel(scale_level, scale_step, rows_block), grid=(r...  71.2 us
    ppermute x8, starting transfers between devices, shifted(): return lax.ppermute(block, axis, route)  24.6 us
    ppermute x8, waiting for transfers between devices, shifted(): return lax.ppermute(block, axis, route)  18.5 us
    unnamed x23, local copies, waits for them, and re-layouts  5.8 us
    slice x3, local copies, waits for them, and re-layouts, step(): high = shifted(field[:HALO], 'gx', -1)  3.89 us
    mul x1, other arithmetic, central_grads(): grad_z = (side[:, 1:-1, 2:] - side[:, 1:-1, :-2]) * 0.5  3.47 us
  transfers between devices with their start and end apart: 8, of which 5 were waited for; matrix products, arithmetic and copies ran while one was open for 15% of the time, Pallas kernels for 0%

profile of v7, /device:TPU:1, one launch (start us, length us, event | category | flops | bytes accessed | tf_op | source)
XLA Modules:
  0.0 144.1 jit_solution(17090720448927894753)
XLA Ops:
  0.6 2.7 %fusion.24 = (f32[14,128,128]{2,1,0:T(8,128)}, f32[14,128,128]{2,1,0:T(8,128)S(1)}) fusion(f32[32,128,128]{2,1,0:T(8,128)} %param.5), kind=kLoop, calls=%fused_computation.37 | loop fusion | bytes 3670016 | tf_op jit(solution)/shard_map/slice | solution.py:240
  3.3 4.5 %collective-permute-start = (f32[14,128,128]{2,1,0:T(8,128)}, f32[14,128,128]{2,1,0:T(8,128)}, u32[]{:S(2)}, u32[]{:S(2)}) collective-permute-start(f32[14,128,128]{2,1,0:T(8,128)} %get-tuple-element.12), channel_id=1, source_target_pairs={{0,1},{1,2},{2,3},{3,4},{4,5},{5,6},{6,7},{7,8},{8,9},{9,10},{10,1... | collective-permute-start | bytes 2752520 | tf_op jit(solution)/shard_map/ppermute | solution.py:18
  7.9 1.9 %collective-permute-start.1 = (f32[14,128,128]{2,1,0:T(8,128)S(1)}, f32[14,128,128]{2,1,0:T(8,128)}, u32[]{:S(2)}, u32[]{:S(2)}) collective-permute-start(f32[14,128,128]{2,1,0:T(8,128)S(1)} %get-tuple-element.13), channel_id=1, source_target_pairs={{1,0},{2,1},{3,2},{4,3},{5,4},{6,5},{7,6},{8,7},{9,8},{10,9},{11,1... | collective-permute-start | bytes 2752520 | tf_op jit(solution)/shard_map/ppermute | solution.py:18
  9.8 1.8 %fusion.23 = (f32[3,128,128]{2,1,0:T(8,128)}, f32[3,128,128]{2,1,0:T(8,128)}) fusion(f32[32,128,128]{2,1,0:T(8,128)} %ls_ref.5), kind=kLoop, calls=%fused_computation.36 | loop fusion | bytes 786432 | tf_op jit(solution)/shard_map/slice | solution.py:263
  11.6 1.9 %collective-permute-start.3 = (f32[3,128,128]{2,1,0:T(8,128)}, f32[3,128,128]{2,1,0:T(8,128)S(1)}, u32[]{:S(2)}, u32[]{:S(2)}) collective-permute-start(f32[3,128,128]{2,1,0:T(8,128)} %get-tuple-element.10), channel_id=1, source_target_pairs={{1,0},{2,1},{3,2},{4,3},{5,4},{6,5},{7,6},{8,7},{9,8},{10,9},{11,1... | collective-permute-start | bytes 589832 | tf_op jit(solution)/shard_map/ppermute | solution.py:18
  13.5 3.6 %collective-permute-start.2 = (f32[3,128,128]{2,1,0:T(8,128)}, f32[3,128,128]{2,1,0:T(8,128)S(1)}, u32[]{:S(2)}, u32[]{:S(2)}) collective-permute-start(f32[3,128,128]{2,1,0:T(8,128)} %get-tuple-element.11), channel_id=1, source_target_pairs={{0,1},{1,2},{2,3},{3,4},{4,5},{5,6},{6,7},{7,8},{8,9},{9,10},{10,1... | collective-permute-start | bytes 589832 | tf_op jit(solution)/shard_map/ppermute | solution.py:18
  17.2 13.2 %collective-permute-done = f32[14,128,128]{2,1,0:T(8,128)} collective-permute-done((f32[14,128,128]{2,1,0:T(8,128)}, f32[14,128,128]{2,1,0:T(8,128)}, u32[]{:S(2)}, u32[]{:S(2)}) %collective-permute-start) | collective-permute-done | bytes 917536 | tf_op jit(solution)/shard_map/ppermute | solution.py:18
  30.4 1.7 %pad_maximum_fusion = f32[60,128,128]{2,1,0:T(8,128)S(1)} fusion(f32[14,128,128]{2,1,0:T(8,128)} %collective-permute-done.1, f32[32,128,128]{2,1,0:T(8,128)S(1)} %copy-done.1, f32[14,128,128]{2,1,0:T(8,128)} %collective-permute-done), kind=kLoop, calls=%fused_computation.8 | loop fusion | flops 1966080 | bytes 7864320 | tf_op jit(solution)/shard_map/concatenate | solution.py:242
  32.7 2.4 %copy.9 = f32[8,8,128,128]{3,1,2,0:T(8,128)S(1)} copy(f32[8,8,128,128]{3,2,1,0:T(8,128)S(1)} %bitcast.14) | data formatting | bytes 8388608
  35.1 2.5 %fusion.25 = f32[36,16384]{1,0:T(8,128)S(1)} fusion(f32[36,60]{1,0:T(8,128)S(1)} %copy-done.9, f32[60,16384]{1,0:T(8,128)S(1)} %bitcast.15), kind=kOutput, calls=%fused_computation.38 | convolution fusion | flops 424673280 | bytes 6300096 | tf_op jit(solution)/shard_map/dot_general | solution.py:244
  38.5 2.3 %fusion = f32[36,128,128]{1,2,0:T(8,128)S(1)} fusion(f32[128,128,1]{1,0,2:T(8,128)S(1)} %copy-done.2, f32[40,128,128]{2,1,0:T(8,128)S(1)} %bitcast.17), kind=kOutput, calls=%fused_computation.9 | convolution fusion | flops 905969664 | bytes 4784128 | tf_op jit(solution)/shard_map/dot_general | solution.py:249
  40.7 2.2 %select_bitcast_fusion = f32[36,128,128]{2,1,0:T(8,128)S(1)} fusion(f32[36,128,128]{1,2,0:T(8,128)S(1)} %fusion, f32[128,128,1]{1,0,2:T(8,128)S(1)} %copy-done.2, pred[36]{0:T(512)(128)(4,1)S(1)} %compare_and_fusion), kind=kOutput, calls=%fused_computation.11 | convolution fusion | flops 906559488 | bytes 4784164 | tf_op jit(solution)/shard_map/yv,xvz->xyz/dot_general | solution.py:252
  43.2 2.1 %fusion.15 = f32[34,128,128]{2,1,0:T(8,128)S(1)} fusion(f32[34,128,128]{2,1,0:T(8,128)S(1)} %slice.95, f32[36,128,128]{2,1,0:T(8,128)S(1)} %select_bitcast_fusion, pred[34]{0:T(512)(128)(4,1)S(1)} %slice.70), kind=kLoop, calls=%fused_computation.26 | loop fusion | flops 8355840 | bytes 8912930 | tf_op jit(solution)/shard_map/jit(_where)/select_n | solution.py:257
  45.3 1.8 %fusion.20 = (f32[32,128,128]{2,1,0:T(8,128)}, f32[32,128,128]{2,1,0:T(8,128)S(1)}) fusion(f32[34,128,128]{2,1,0:T(8,128)S(1)} %fusion.15), kind=kLoop, calls=%fused_computation.32 | loop fusion | flops 1048576 | bytes 10485760 | tf_op jit(solution)/shard_map/mul | solution.py:68
  47.1 3.5 %fusion.19 = (f32[32,128,128]{2,1,0:T(8,128)}, f32[32,128,128]{2,1,0:T(8,128)}) fusion(f32[32,128,128]{2,1,0:T(8,128)S(1)} %get-tuple-element.3.edge_ref), kind=kLoop, calls=%fused_computation.30 | loop fusion | flops 2097152 | bytes 6291456 | tf_op jit(solution)/shard_map/mul | solution.py:70
  51.3 23.6 %shard_map.68.main_ref = f32[32,128,128]{2,1,0:T(8,128)} custom-call(f32[3,128,128]{2,1,0:T(8,128)} %copy-done.4, f32[32,128,128]{2,1,0:T(8,128)} %ls_ref.5, f32[3,128,128]{2,1,0:T(8,128)} %copy-done.3, f32[32,128,128]{2,1,0:T(8,128)} %copy-done, f32[32,128,128]{2,1,0:T(8,128)} %get-tuple-element.2.sx_ref, f32[32,128,128]{2,1,0:T(8,128)} %get-tuple-element.9.sy_ref, ...), custom_call_target="tpu_custom_call" | custom-call | tf_op jit(solution)/shard_map/pallas_call | solution.py:222
  76.0 1.9 %collective-permute-start.5 = (f32[3,128,128]{2,1,0:T(8,128)S(1)}, f32[3,128,128]{2,1,0:T(8,128)S(1)}, u32[]{:S(2)}, u32[]{:S(2)}) collective-permute-start(f32[3,128,128]{2,1,0:T(8,128)S(1)} %get-tuple-element.6), channel_id=1, source_target_pairs={{1,0},{2,1},{3,2},{4,3},{5,4},{6,5},{7,6},{8,7},{9,8},{10,9},{11,1... | collective-permute-start | bytes 589832 | tf_op jit(solution)/shard_map/ppermute | solution.py:18
  77.9 4.4 %collective-permute-start.4 = (f32[3,128,128]{2,1,0:T(8,128)S(1)}, f32[3,128,128]{2,1,0:T(8,128)S(1)}, u32[]{:S(2)}, u32[]{:S(2)}) collective-permute-start(f32[3,128,128]{2,1,0:T(8,128)S(1)} %get-tuple-element.7), channel_id=1, source_target_pairs={{0,1},{1,2},{2,3},{3,4},{4,5},{5,6},{6,7},{7,8},{8,9},{9,10},{10,1... | collective-permute-start | bytes 589832 | tf_op jit(solution)/shard_map/ppermute | solution.py:18
  82.3 1.4 collective-permute-done.5.high_ref
  85.6 23.8 %shard_map.69.main_ref = f32[32,128,128]{2,1,0:T(8,128)} custom-call(f32[3,128,128]{2,1,0:T(8,128)} %copy-done.8, f32[32,128,128]{2,1,0:T(8,128)} %shard_map.68.main_ref, f32[3,128,128]{2,1,0:T(8,128)} %copy-done.6, f32[32,128,128]{2,1,0:T(8,128)} %copy-done, f32[32,128,128]{2,1,0:T(8,128)} %get-tuple-element.2.sx_ref, ...), custom_call_target="tpu_custom_call" | custom-call | tf_op jit(solution)/shard_map/pallas_call | solution.py:222
  110.5 1.9 %collective-permute-start.7 = (f32[3,128,128]{2,1,0:T(8,128)S(1)}, f32[3,128,128]{2,1,0:T(8,128)S(1)}, u32[]{:S(2)}, u32[]{:S(2)}) collective-permute-start(f32[3,128,128]{2,1,0:T(8,128)S(1)} %get-tuple-element.4), channel_id=1, source_target_pairs={{1,0},{2,1},{3,2},{4,3},{5,4},{6,5},{7,6},{8,7},{9,8},{10,9},{11,1... | collective-permute-start | bytes 589832 | tf_op jit(solution)/shard_map/ppermute | solution.py:18
  112.4 4.4 %collective-permute-start.6 = (f32[3,128,128]{2,1,0:T(8,128)S(1)}, f32[3,128,128]{2,1,0:T(8,128)S(1)}, u32[]{:S(2)}, u32[]{:S(2)}) collective-permute-start(f32[3,128,128]{2,1,0:T(8,128)S(1)} %get-tuple-element.5), channel_id=1, source_target_pairs={{0,1},{1,2},{2,3},{3,4},{4,5},{5,6},{6,7},{7,8},{8,9},{9,10},{10,1... | collective-permute-start | bytes 589832 | tf_op jit(solution)/shard_map/ppermute | solution.py:18
  116.8 1.4 collective-permute-done.7.high_ref
  120.2 23.7 %shard_map.70 = f32[32,128,128]{2,1,0:T(8,128)} custom-call(f32[3,128,128]{2,1,0:T(8,128)} %copy-done.7, f32[32,128,128]{2,1,0:T(8,128)} %shard_map.69.main_ref, f32[3,128,128]{2,1,0:T(8,128)} %copy-done.5, f32[32,128,128]{2,1,0:T(8,128)} %copy-done, f32[32,128,128]{2,1,0:T(8,128)} %get-tuple-element.2.sx_ref, f32[32,128,128]{2,1,0:T(8,128)} %get-tuple-element.9.sy_ref, ...), custom_call_target="tpu_custom_call" | custom-call | tf_op jit(solution)/shard_map/pallas_call | solution.py:222
  (32 shorter events, 8.3 us)
Async XLA Ops:
  0.6 29.8 %copy-start.1 = (f32[32,128,128]{2,1,0:T(8,128)S(1)}, f32[32,128,128]{2,1,0:T(8,128)}, u32[]{:S(2)}) copy-start(f32[32,128,128]{2,1,0:T(8,128)} %param.5) | copy-start | bytes 6291460
  3.3 27.1 %collective-permute-start = (f32[14,128,128]{2,1,0:T(8,128)}, f32[14,128,128]{2,1,0:T(8,128)}, u32[]{:S(2)}, u32[]{:S(2)}) collective-permute-start(f32[14,128,128]{2,1,0:T(8,128)} %get-tuple-element.12), channel_id=1, source_target_pairs={{0,1},{1,2},{2,3},{3,4},{4,5},{5,6},{6,7},{7,8},{8,9},{9,10},{10,1... | collective-permute-start | bytes 2752520 | tf_op jit(solution)/shard_map/ppermute | solution.py:18
  7.9 22.6 %collective-permute-start.1 = (f32[14,128,128]{2,1,0:T(8,128)S(1)}, f32[14,128,128]{2,1,0:T(8,128)}, u32[]{:S(2)}, u32[]{:S(2)}) collective-permute-start(f32[14,128,128]{2,1,0:T(8,128)S(1)} %get-tuple-element.13), channel_id=1, source_target_pairs={{1,0},{2,1},{3,2},{4,3},{5,4},{6,5},{7,6},{8,7},{9,8},{10,9},{11,1... | collective-permute-start | bytes 2752520 | tf_op jit(solution)/shard_map/ppermute | solution.py:18
  11.6 39.0 %collective-permute-start.3 = (f32[3,128,128]{2,1,0:T(8,128)}, f32[3,128,128]{2,1,0:T(8,128)S(1)}, u32[]{:S(2)}, u32[]{:S(2)}) collective-permute-start(f32[3,128,128]{2,1,0:T(8,128)} %get-tuple-element.10), channel_id=1, source_target_pairs={{1,0},{2,1},{3,2},{4,3},{5,4},{6,5},{7,6},{8,7},{9,8},{10,9},{11,1... | collective-permute-start | bytes 589832 | tf_op jit(solution)/shard_map/ppermute | solution.py:18
  13.5 37.1 %collective-permute-start.2 = (f32[3,128,128]{2,1,0:T(8,128)}, f32[3,128,128]{2,1,0:T(8,128)S(1)}, u32[]{:S(2)}, u32[]{:S(2)}) collective-permute-start(f32[3,128,128]{2,1,0:T(8,128)} %get-tuple-element.11), channel_id=1, source_target_pairs={{0,1},{1,2},{2,3},{3,4},{4,5},{5,6},{6,7},{7,8},{8,9},{9,10},{10,1... | collective-permute-start | bytes 589832 | tf_op jit(solution)/shard_map/ppermute | solution.py:18
  32.7 2.4 %copy-start.9 = (f32[36,60]{1,0:T(8,128)S(1)}, f32[36,60]{1,0:T(8,128)}, u32[]{:S(2)}) copy-start(f32[36,60]{1,0:T(8,128)} %constant.28.clone) | copy-start | bytes 25924
  37.6 0.8 copy-start.2
  47.1 3.5 %copy-start = (f32[32,128,128]{2,1,0:T(8,128)}, f32[32,128,128]{2,1,0:T(8,128)S(1)}, u32[]{:S(2)}) copy-start(f32[32,128,128]{2,1,0:T(8,128)S(1)} %get-tuple-element.3.edge_ref) | copy-start | bytes 6291460
  50.6 0.7 copy-start.3
  50.6 0.7 copy-start.4
  76.0 7.7 %collective-permute-start.5 = (f32[3,128,128]{2,1,0:T(8,128)S(1)}, f32[3,128,128]{2,1,0:T(8,128)S(1)}, u32[]{:S(2)}, u32[]{:S(2)}) collective-permute-start(f32[3,128,128]{2,1,0:T(8,128)S(1)} %get-tuple-element.6), channel_id=1, source_target_pairs={{1,0},{2,1},{3,2},{4,3},{5,4},{6,5},{7,6},{8,7},{9,8},{10,9},{11,1... | collective-permute-start | bytes 589832 | tf_op jit(solution)/shard_map/ppermute | solution.py:18
  77.9 7.0 %collective-permute-start.4 = (f32[3,128,128]{2,1,0:T(8,128)S(1)}, f32[3,128,128]{2,1,0:T(8,128)S(1)}, u32[]{:S(2)}, u32[]{:S(2)}) collective-permute-start(f32[3,128,128]{2,1,0:T(8,128)S(1)} %get-tuple-element.7), channel_id=1, source_target_pairs={{0,1},{1,2},{2,3},{3,4},{4,5},{5,6},{6,7},{7,8},{8,9},{9,10},{10,1... | collective-permute-start | bytes 589832 | tf_op jit(solution)/shard_map/ppermute | solution.py:18
  83.8 1.2 copy-start.6
  84.9 0.7 copy-start.8
  110.5 7.7 %collective-permute-start.7 = (f32[3,128,128]{2,1,0:T(8,128)S(1)}, f32[3,128,128]{2,1,0:T(8,128)S(1)}, u32[]{:S(2)}, u32[]{:S(2)}) collective-permute-start(f32[3,128,128]{2,1,0:T(8,128)S(1)} %get-tuple-element.4), channel_id=1, source_target_pairs={{1,0},{2,1},{3,2},{4,3},{5,4},{6,5},{7,6},{8,7},{9,8},{10,9},{11,1... | collective-permute-start | bytes 589832 | tf_op jit(solution)/shard_map/ppermute | solution.py:18
  112.4 7.1 %collective-permute-start.6 = (f32[3,128,128]{2,1,0:T(8,128)S(1)}, f32[3,128,128]{2,1,0:T(8,128)S(1)}, u32[]{:S(2)}, u32[]{:S(2)}) collective-permute-start(f32[3,128,128]{2,1,0:T(8,128)S(1)} %get-tuple-element.5), channel_id=1, source_target_pairs={{0,1},{1,2},{2,3},{3,4},{4,5},{5,6},{6,7},{7,8},{8,9},{9,10},{10,1... | collective-permute-start | bytes 589832 | tf_op jit(solution)/shard_map/ppermute | solution.py:18
  118.2 1.3 copy-start.5
  119.5 0.7 copy-start.7

commit v8 on v7

--- a/solution.py
+++ b/solution.py
@@ -237,8 +237,12 @@
     rows, rows_y, rows_z = volume.shape
     exact = lax.Precision.HIGHEST
     halo = min(rows, RADIUS + 2)
-    low = shifted(volume[rows - halo :], "gx", 1)
-    high = shifted(volume[:halo], "gx", -1)
+    low_all = shifted(
+        jnp.concatenate([volume[rows - halo :], level_set[rows - HALO :]], axis=0), "gx", 1
+    )
+    high_all = shifted(jnp.concatenate([volume[:halo], level_set[:HALO]], axis=0), "gx", -1)
+    low = low_all[:halo]
+    high = high_all[:halo]
     extended = jnp.concatenate([low, volume, high], axis=0)
     wide = rows + 4
     blurred = jnp.dot(
@@ -258,12 +262,13 @@
     edge = edge_wide[1:-1]
     slope = central_grads(edge_wide)
 
-    def step(field, scale_level, scale_step):
-        low = shifted(field[rows - HALO :], "gx", 1)
-        high = shifted(field[:HALO], "gx", -1)
+    def step(field, scale_level, scale_step, low=None, high=None):
+        if low is None:
+            low = shifted(field[rows - HALO :], "gx", 1)
+            high = shifted(field[:HALO], "gx", -1)
         return stage(low, field, high, edge, slope, level_set, scale_level, scale_step)
 
-    section_one = step(level_set, None, None)
+    section_one = step(level_set, None, None, low_all[halo:], high_all[halo:])
     section_two = step(section_one, 0.75, 0.25)
     advanced = step(section_two, 1.0 / 3.0, 2.0 / 3.0)
     return (edge, advanced)

time: 147 us -> 152 us (1.034)
  waiting for transfers between devices: 18.5 us -> 27.6 us
  starting transfers between devices: 24.6 us -> 19.2 us
    ppermute x8 -> x6, waiting for transfers between devices: 18.5 us -> 27.6 us  [shifted(): return lax.ppermute(block, axis, route)]
    ppermute x8 -> x6, starting transfers between devices: 24.6 us -> 19.2 us  [shifted(): return lax.ppermute(block, axis, route)]
    slice x1 -> x6, local copies, waits for them, and re-layouts: 2.69 us -> 6.28 us  [the longest x2 2.3 us: shards(): section_one = step(level_set, None, None, low_all[halo:], high_all[halo:])]
    concatenate x0 -> x2, other arithmetic: none -> 2.18 us  [the longest x1 1.09 us: shards(): jnp.concatenate([volume[:halo], level_set[:HALO]], axis=0)]
    slice x3 -> x2, local copies, waits for them, and re-layouts: 3.89 us -> 2.1 us  [step(): high = shifted(field[:HALO], 'gx', -1)]
    unnamed x23 -> x19, local copies, waits for them, and re-layouts: 5.8 us -> 5.08 us
  transfers between devices with their start and end apart: 8 -> 6, of which waited for: 5 -> 6; matrix products, arithmetic and copies ran while one was open for 15% -> 1% of each run, Pallas kernels for 0% -> 0%
where the time goes in v8:
time: 152 us; the launch traced here: 150 us
  Pallas kernels  71.2 us (47%)
  waiting for transfers between devices  27.6 us (18%)
  starting transfers between devices  19.2 us (13%)
  local copies, waits for them, and re-layouts  13.8 us (9%)
  other arithmetic  9.85 us (6%)
  matrix products  7.06 us (5%)
    pallas_call x3, Pallas kernels, stage(): pl.pallas_call(stage_kernel(scale_level, scale_step, rows_block), grid=(r...  71.2 us
    ppermute x6, waiting for transfers between devices, shifted(): return lax.ppermute(block, axis, route)  27.6 us
    ppermute x6, starting transfers between devices, shifted(): return lax.ppermute(block, axis, route)  19.2 us
    unnamed x19, local copies, waits for them, and re-layouts  5.08 us
    mul x1, other arithmetic, central_grads(): grad_z = (side[:, 1:-1, 2:] - side[:, 1:-1, :-2]) * 0.5  3.49 us
  transfers between devices with their start and end apart: 6, of which 6 were waited for; matrix products, arithmetic and copies ran while one was open for 1% of the time, Pallas kernels for 0%

profile of v8, /device:TPU:1, one launch (start us, length us, event | category | flops | bytes accessed | tf_op | source)
XLA Modules:
  0.0 149.7 jit_solution(15911146505529872105)
XLA Ops:
  1.7 1.6 %fusion.23 = (f32[14,128,128]{2,1,0:T(8,128)S(1)}, f32[14,128,128]{2,1,0:T(8,128)S(1)}) fusion(f32[32,128,128]{2,1,0:T(8,128)} %param.5), kind=kLoop, calls=%fused_computation.38 | loop fusion | bytes 3670016 | tf_op jit(solution)/shard_map/slice | solution.py:241
  4.4 1.9 %collective-permute-start.1 = (f32[17,128,128]{2,1,0:T(8,128)}, f32[17,128,128]{2,1,0:T(8,128)S(1)}, u32[]{:S(2)}, u32[]{:S(2)}) collective-permute-start(f32[17,128,128]{2,1,0:T(8,128)} %pad_maximum_fusion.2), channel_id=1, source_target_pairs={{1,0},{2,1},{3,2},{4,3},{5,4},{6,5},{7,6},{8,7},{9,8},{10,9},{11,1... | collective-permute-start | bytes 3342344 | tf_op jit(solution)/shard_map/ppermute | solution.py:18
  7.4 4.6 %collective-permute-start = (f32[17,128,128]{2,1,0:T(8,128)}, f32[17,128,128]{2,1,0:T(8,128)}, u32[]{:S(2)}, u32[]{:S(2)}) collective-permute-start(f32[17,128,128]{2,1,0:T(8,128)} %pad_maximum_fusion.1), channel_id=1, source_target_pairs={{0,1},{1,2},{2,3},{3,4},{4,5},{5,6},{6,7},{7,8},{8,9},{9,10},{10,1... | collective-permute-start | bytes 3342344 | tf_op jit(solution)/shard_map/ppermute | solution.py:18
  12.2 10.1 %collective-permute-done.1 = f32[17,128,128]{2,1,0:T(8,128)S(1)} collective-permute-done((f32[17,128,128]{2,1,0:T(8,128)}, f32[17,128,128]{2,1,0:T(8,128)S(1)}, u32[]{:S(2)}, u32[]{:S(2)}) %collective-permute-start.1) | collective-permute-done | bytes 1114144 | tf_op jit(solution)/shard_map/ppermute | solution.py:18
  22.4 12.1 %collective-permute-done = f32[17,128,128]{2,1,0:T(8,128)} collective-permute-done((f32[17,128,128]{2,1,0:T(8,128)}, f32[17,128,128]{2,1,0:T(8,128)}, u32[]{:S(2)}, u32[]{:S(2)}) %collective-permute-start) | collective-permute-done | bytes 1114144 | tf_op jit(solution)/shard_map/ppermute | solution.py:18
  34.5 1.2 slice.109
  36.6 2.4 %copy.9 = f32[8,8,128,128]{3,1,2,0:T(8,128)S(1)} copy(f32[8,8,128,128]{3,2,1,0:T(8,128)S(1)} %bitcast.14) | data formatting | bytes 8388608
  39.0 2.5 %fusion.25 = f32[36,16384]{1,0:T(8,128)S(1)} fusion(f32[36,60]{1,0:T(8,128)S(1)} %copy-done.7, f32[60,16384]{1,0:T(8,128)S(1)} %bitcast.15), kind=kOutput, calls=%fused_computation.40 | convolution fusion | flops 424673280 | bytes 6300096 | tf_op jit(solution)/shard_map/dot_general | solution.py:248
  42.4 2.3 %fusion = f32[36,128,128]{1,2,0:T(8,128)S(1)} fusion(f32[128,128,1]{1,0,2:T(8,128)S(1)} %copy-done.2, f32[40,128,128]{2,1,0:T(8,128)S(1)} %bitcast.17), kind=kOutput, calls=%fused_computation.9 | convolution fusion | flops 905969664 | bytes 4784128 | tf_op jit(solution)/shard_map/dot_general | solution.py:253
  44.7 2.2 %select_bitcast_fusion = f32[36,128,128]{2,1,0:T(8,128)S(1)} fusion(f32[36,128,128]{1,2,0:T(8,128)S(1)} %fusion, f32[128,128,1]{1,0,2:T(8,128)S(1)} %copy-done.2, pred[36]{0:T(512)(128)(4,1)S(1)} %compare_and_fusion), kind=kOutput, calls=%fused_computation.11 | convolution fusion | flops 906559488 | bytes 4784164 | tf_op jit(solution)/shard_map/yv,xvz->xyz/dot_general | solution.py:256
  47.2 2.1 %fusion.15 = f32[34,128,128]{2,1,0:T(8,128)S(1)} fusion(f32[34,128,128]{2,1,0:T(8,128)S(1)} %slice.113, f32[36,128,128]{2,1,0:T(8,128)S(1)} %select_bitcast_fusion, pred[34]{0:T(512)(128)(4,1)S(1)} %slice.82), kind=kLoop, calls=%fused_computation.26 | loop fusion | flops 8355840 | bytes 8912930 | tf_op jit(solution)/shard_map/jit(_where)/select_n | solution.py:261
  49.3 1.8 %fusion.20 = (f32[32,128,128]{2,1,0:T(8,128)}, f32[32,128,128]{2,1,0:T(8,128)S(1)}) fusion(f32[34,128,128]{2,1,0:T(8,128)S(1)} %fusion.15), kind=kLoop, calls=%fused_computation.32 | loop fusion | flops 1048576 | bytes 10485760 | tf_op jit(solution)/shard_map/mul | solution.py:68
  51.1 3.5 %fusion.19 = (f32[32,128,128]{2,1,0:T(8,128)}, f32[32,128,128]{2,1,0:T(8,128)}) fusion(f32[32,128,128]{2,1,0:T(8,128)S(1)} %get-tuple-element.3.edge_ref), kind=kLoop, calls=%fused_computation.30 | loop fusion | flops 2097152 | bytes 6291456 | tf_op jit(solution)/shard_map/mul | solution.py:70
  55.3 1.6 %slice.115.low_ref = f32[3,128,128]{2,1,0:T(8,128)} slice(f32[17,128,128]{2,1,0:T(8,128)} %collective-permute-done), slice={[14:17], [0:128], [0:128]} | slice | bytes 393216 | tf_op jit(solution)/shard_map/slice | solution.py:271
  56.9 23.6 %shard_map.68.main_ref = f32[32,128,128]{2,1,0:T(8,128)} custom-call(f32[3,128,128]{2,1,0:T(8,128)} %slice.115.low_ref, f32[32,128,128]{2,1,0:T(8,128)} %ls_ref.5, f32[3,128,128]{2,1,0:T(8,128)} %slice.116.high_ref, f32[32,128,128]{2,1,0:T(8,128)} %copy-done, f32[32,128,128]{2,1,0:T(8,128)} %get-tuple-element.2.sx_ref, ...), custom_call_target="tpu_custom_call" | custom-call | tf_op jit(solution)/shard_map/pallas_call | solution.py:222
  81.6 1.9 %collective-permute-start.3 = (f32[3,128,128]{2,1,0:T(8,128)S(1)}, f32[3,128,128]{2,1,0:T(8,128)S(1)}, u32[]{:S(2)}, u32[]{:S(2)}) collective-permute-start(f32[3,128,128]{2,1,0:T(8,128)S(1)} %get-tuple-element.6), channel_id=1, source_target_pairs={{1,0},{2,1},{3,2},{4,3},{5,4},{6,5},{7,6},{8,7},{9,8},{10,9},{11,1... | collective-permute-start | bytes 589832 | tf_op jit(solution)/shard_map/ppermute | solution.py:18
  83.5 4.4 %collective-permute-start.2 = (f32[3,128,128]{2,1,0:T(8,128)S(1)}, f32[3,128,128]{2,1,0:T(8,128)S(1)}, u32[]{:S(2)}, u32[]{:S(2)}) collective-permute-start(f32[3,128,128]{2,1,0:T(8,128)S(1)} %get-tuple-element.7), channel_id=1, source_target_pairs={{0,1},{1,2},{2,3},{3,4},{4,5},{5,6},{6,7},{7,8},{8,9},{9,10},{10,1... | collective-permute-start | bytes 589832 | tf_op jit(solution)/shard_map/ppermute | solution.py:18
  87.9 1.4 collective-permute-done.3.high_ref
  91.2 23.8 %shard_map.69.main_ref = f32[32,128,128]{2,1,0:T(8,128)} custom-call(f32[3,128,128]{2,1,0:T(8,128)} %copy-done.6, f32[32,128,128]{2,1,0:T(8,128)} %shard_map.68.main_ref, f32[3,128,128]{2,1,0:T(8,128)} %copy-done.4, f32[32,128,128]{2,1,0:T(8,128)} %copy-done, f32[32,128,128]{2,1,0:T(8,128)} %get-tuple-element.2.sx_ref, ...), custom_call_target="tpu_custom_call" | custom-call | tf_op jit(solution)/shard_map/pallas_call | solution.py:222
  116.0 1.9 %collective-permute-start.5 = (f32[3,128,128]{2,1,0:T(8,128)S(1)}, f32[3,128,128]{2,1,0:T(8,128)S(1)}, u32[]{:S(2)}, u32[]{:S(2)}) collective-permute-start(f32[3,128,128]{2,1,0:T(8,128)S(1)} %get-tuple-element.4), channel_id=1, source_target_pairs={{1,0},{2,1},{3,2},{4,3},{5,4},{6,5},{7,6},{8,7},{9,8},{10,9},{11,1... | collective-permute-start | bytes 589832 | tf_op jit(solution)/shard_map/ppermute | solution.py:18
  117.9 4.4 %collective-permute-start.4 = (f32[3,128,128]{2,1,0:T(8,128)S(1)}, f32[3,128,128]{2,1,0:T(8,128)S(1)}, u32[]{:S(2)}, u32[]{:S(2)}) collective-permute-start(f32[3,128,128]{2,1,0:T(8,128)S(1)} %get-tuple-element.5), channel_id=1, source_target_pairs={{0,1},{1,2},{2,3},{3,4},{4,5},{5,6},{6,7},{7,8},{8,9},{9,10},{10,1... | collective-permute-start | bytes 589832 | tf_op jit(solution)/shard_map/ppermute | solution.py:18
  122.3 1.4 collective-permute-done.5.high_ref
  123.8 1.3 collective-permute-done.4.low_ref
  125.7 23.7 %shard_map.70 = f32[32,128,128]{2,1,0:T(8,128)} custom-call(f32[3,128,128]{2,1,0:T(8,128)} %copy-done.5, f32[32,128,128]{2,1,0:T(8,128)} %shard_map.69.main_ref, f32[3,128,128]{2,1,0:T(8,128)} %copy-done.3, f32[32,128,128]{2,1,0:T(8,128)} %copy-done, f32[32,128,128]{2,1,0:T(8,128)} %get-tuple-element.2.sx_ref, f32[32,128,128]{2,1,0:T(8,128)} %get-tuple-element.9.sy_ref, ...), custom_call_target="tpu_custom_call" | custom-call | tf_op jit(solution)/shard_map/pallas_call | solution.py:222
  (30 shorter events, 10.6 us)
Async XLA Ops:
  4.4 17.9 %collective-permute-start.1 = (f32[17,128,128]{2,1,0:T(8,128)}, f32[17,128,128]{2,1,0:T(8,128)S(1)}, u32[]{:S(2)}, u32[]{:S(2)}) collective-permute-start(f32[17,128,128]{2,1,0:T(8,128)} %pad_maximum_fusion.2), channel_id=1, source_target_pairs={{1,0},{2,1},{3,2},{4,3},{5,4},{6,5},{7,6},{8,7},{9,8},{10,9},{11,1... | collective-permute-start | bytes 3342344 | tf_op jit(solution)/shard_map/ppermute | solution.py:18
  7.4 28.4 %copy-start.1 = (f32[32,128,128]{2,1,0:T(8,128)S(1)}, f32[32,128,128]{2,1,0:T(8,128)}, u32[]{:S(2)}) copy-start(f32[32,128,128]{2,1,0:T(8,128)} %param.5) | copy-start | bytes 6291460
  7.4 27.1 %collective-permute-start = (f32[17,128,128]{2,1,0:T(8,128)}, f32[17,128,128]{2,1,0:T(8,128)}, u32[]{:S(2)}, u32[]{:S(2)}) collective-permute-start(f32[17,128,128]{2,1,0:T(8,128)} %pad_maximum_fusion.1), channel_id=1, source_target_pairs={{0,1},{1,2},{2,3},{3,4},{4,5},{5,6},{6,7},{7,8},{8,9},{9,10},{10,1... | collective-permute-start | bytes 3342344 | tf_op jit(solution)/shard_map/ppermute | solution.py:18
  36.6 2.4 %copy-start.7 = (f32[36,60]{1,0:T(8,128)S(1)}, f32[36,60]{1,0:T(8,128)}, u32[]{:S(2)}) copy-start(f32[36,60]{1,0:T(8,128)} %constant.28.clone) | copy-start | bytes 25924
  41.6 0.8 copy-start.2
  51.1 3.5 %copy-start = (f32[32,128,128]{2,1,0:T(8,128)}, f32[32,128,128]{2,1,0:T(8,128)S(1)}, u32[]{:S(2)}) copy-start(f32[32,128,128]{2,1,0:T(8,128)S(1)} %get-tuple-element.3.edge_ref) | copy-start | bytes 6291460
  81.6 7.7 %collective-permute-start.3 = (f32[3,128,128]{2,1,0:T(8,128)S(1)}, f32[3,128,128]{2,1,0:T(8,128)S(1)}, u32[]{:S(2)}, u32[]{:S(2)}) collective-permute-start(f32[3,128,128]{2,1,0:T(8,128)S(1)} %get-tuple-element.6), channel_id=1, source_target_pairs={{1,0},{2,1},{3,2},{4,3},{5,4},{6,5},{7,6},{8,7},{9,8},{10,9},{11,1... | collective-permute-start | bytes 589832 | tf_op jit(solution)/shard_map/ppermute | solution.py:18
  83.5 7.0 %collective-permute-start.2 = (f32[3,128,128]{2,1,0:T(8,128)S(1)}, f32[3,128,128]{2,1,0:T(8,128)S(1)}, u32[]{:S(2)}, u32[]{:S(2)}) collective-permute-start(f32[3,128,128]{2,1,0:T(8,128)S(1)} %get-tuple-element.7), channel_id=1, source_target_pairs={{0,1},{1,2},{2,3},{3,4},{4,5},{5,6},{6,7},{7,8},{8,9},{9,10},{10,1... | collective-permute-start | bytes 589832 | tf_op jit(solution)/shard_map/ppermute | solution.py:18
  89.3 1.2 copy-start.4
  90.5 0.7 copy-start.6
  116.0 7.7 %collective-permute-start.5 = (f32[3,128,128]{2,1,0:T(8,128)S(1)}, f32[3,128,128]{2,1,0:T(8,128)S(1)}, u32[]{:S(2)}, u32[]{:S(2)}) collective-permute-start(f32[3,128,128]{2,1,0:T(8,128)S(1)} %get-tuple-element.4), channel_id=1, source_target_pairs={{1,0},{2,1},{3,2},{4,3},{5,4},{6,5},{7,6},{8,7},{9,8},{10,9},{11,1... | collective-permute-start | bytes 589832 | tf_op jit(solution)/shard_map/ppermute | solution.py:18
  117.9 7.1 %collective-permute-start.4 = (f32[3,128,128]{2,1,0:T(8,128)S(1)}, f32[3,128,128]{2,1,0:T(8,128)S(1)}, u32[]{:S(2)}, u32[]{:S(2)}) collective-permute-start(f32[3,128,128]{2,1,0:T(8,128)S(1)} %get-tuple-element.5), channel_id=1, source_target_pairs={{0,1},{1,2},{2,3},{3,4},{4,5},{5,6},{6,7},{7,8},{8,9},{9,10},{10,1... | collective-permute-start | bytes 589832 | tf_op jit(solution)/shard_map/ppermute | solution.py:18
  123.8 1.3 copy-start.3
  125.1 0.7 copy-start.5

commit v9 on v7

--- a/solution.py
+++ b/solution.py
@@ -119,26 +119,20 @@
 
 
 def stage_kernel(scale_level, scale_step, rows_block):
-    def kernel(
-        low_ref, main_ref, high_ref, edge_ref, sx_ref, sy_ref, sz_ref, ls_ref, out_ref, p_ref, sems
-    ):
+    def kernel(low_ref, main_ref, high_ref, edge_ref, sx_ref, sy_ref, sz_ref, ls_ref, *rest):
+        out_ref = rest[0]
+        p_ref, sems = rest[-2:]
         rows = main_ref.shape[0]
         rows_y = out_ref.shape[1]
         rows_z = out_ref.shape[2]
         block = pl.program_id(0)
+        last = pl.num_programs(0) - 1
+        inner = pl.ds(SUB, rows_y)
 
         @pl.when(block == 0)
         def _():
-            inner = pl.ds(SUB, rows_y)
-            copies = [
-                pltpu.make_async_copy(low_ref, p_ref.at[pl.ds(0, HALO), inner, :], sems.at[0]),
-                pltpu.make_async_copy(main_ref, p_ref.at[pl.ds(HALO, rows), inner, :], sems.at[1]),
-                pltpu.make_async_copy(
-                    high_ref, p_ref.at[pl.ds(HALO + rows, HALO), inner, :], sems.at[2]
-                ),
-            ]
-            for copy in copies:
-                copy.start()
+            copy = pltpu.make_async_copy(main_ref, p_ref.at[pl.ds(HALO, rows), inner, :], sems.at[0])
+            copy.start()
             zeros = jnp.zeros((SUB, rows_z), jnp.float32)
 
             def clear(x, carry):
@@ -147,8 +141,10 @@
                 return carry
 
             lax.fori_loop(0, rows + 2 * HALO, clear, 0)
-            for copy in copies:
-                copy.wait()
+            p_ref[pl.ds(0, HALO), inner, :] = low_ref[...]
+            p_ref[pl.ds(HALO + rows, HALO), inner, :] = high_ref[...]
+            copy.wait()
+
         lane = lax.broadcasted_iota(jnp.int32, (SUB, rows_z), 1)
 
         def along_z(tile, step):
@@ -210,24 +206,37 @@
             return carry
 
         lax.fori_loop(0, rows_block, row, 0)
+        if len(rest) > 3:
+            top_ref, bottom_ref = rest[1], rest[2]
+
+            @pl.when(block == 0)
+            def _():
+                top_ref[...] = out_ref[pl.ds(0, HALO)]
+
+            @pl.when(block == last)
+            def _():
+                bottom_ref[...] = out_ref[pl.ds(rows_block - HALO, HALO)]
 
     return kernel
 
 
-def stage(low, field, high, edge, slope, level_set, scale_level, scale_step):
+def stage(low, field, high, edge, slope, level_set, scale_level, scale_step, sides):
     rows, rows_y, rows_z = level_set.shape
     rows_block = SUB if rows % SUB == 0 else rows
     raw = pl.BlockSpec(memory_space=pl.ANY)
     part = pl.BlockSpec((rows_block, rows_y, rows_z), lambda i: (i, 0, 0))
+    side = pl.BlockSpec((HALO, rows_y, rows_z), lambda i: (0, 0, 0))
+    result = jax.ShapeDtypeStruct(level_set.shape, level_set.dtype)
+    edge_rows = jax.ShapeDtypeStruct((HALO, rows_y, rows_z), level_set.dtype)
     return pl.pallas_call(
         stage_kernel(scale_level, scale_step, rows_block),
         grid=(rows // rows_block,),
-        in_specs=[raw, raw, raw, part, part, part, part, part],
-        out_specs=part,
-        out_shape=jax.ShapeDtypeStruct(level_set.shape, level_set.dtype),
+        in_specs=[side, raw, side, part, part, part, part, part],
+        out_specs=[part, side, side] if sides else part,
+        out_shape=[result, edge_rows, edge_rows] if sides else result,
         scratch_shapes=[
             pltpu.VMEM((rows + 2 * HALO, rows_y + 2 * SUB, rows_z), jnp.float32),
-            pltpu.SemaphoreType.DMA((3,)),
+            pltpu.SemaphoreType.DMA((1,)),
         ],
         compiler_params=pltpu.CompilerParams(dimension_semantics=("arbitrary",)),
     )(low, field, high, edge, slope[0], slope[1], slope[2], level_set)
@@ -258,14 +267,14 @@
     edge = edge_wide[1:-1]
     slope = central_grads(edge_wide)
 
-    def step(field, scale_level, scale_step):
-        low = shifted(field[rows - HALO :], "gx", 1)
-        high = shifted(field[:HALO], "gx", -1)
-        return stage(low, field, high, edge, slope, level_set, scale_level, scale_step)
-
-    section_one = step(level_set, None, None)
-    section_two = step(section_one, 0.75, 0.25)
-    advanced = step(section_two, 1.0 / 3.0, 2.0 / 3.0)
+    def step(field, top, bottom, scale_level, scale_step, sides=True):
+        low = shifted(bottom, "gx", 1)
+        high = shifted(top, "gx", -1)
+        return stage(low, field, high, edge, slope, level_set, scale_level, scale_step, sides)
+
+    section_one, top, bottom = step(level_set, level_set[:HALO], level_set[rows - HALO :], None, None)
+    section_two, top, bottom = step(section_one, top, bottom, 0.75, 0.25)
+    advanced = step(section_two, top, bottom, 1.0 / 3.0, 2.0 / 3.0, sides=False)
     return (edge, advanced)
 
 

time: 147 us -> 146 us (level); the launches traced: 144 us -> 146 us
  waiting for transfers between devices: 18.5 us -> 24 us
  local copies, waits for them, and re-layouts: 12.7 us -> 9.15 us
  starting transfers between devices: 24.6 us -> 22.6 us
  Pallas kernels: 71.2 us -> 72.8 us
    ppermute x8, waiting for transfers between devices: 18.5 us -> 24 us  [shifted(): return lax.ppermute(block, axis, route)]
    slice x3 -> x1, local copies, waits for them, and re-layouts: 3.89 us -> 1.05 us  [shards(): level_set[:HALO]]
    ppermute x8, starting transfers between devices: 24.6 us -> 22.6 us  [shifted(): return lax.ppermute(block, axis, route)]
    pallas_call x3, Pallas kernels: 71.2 us -> 72.8 us  [stage(): pl.pallas_call(stage_kernel(scale_level, scale_step, rows_block), grid=(r...]
    unnamed x23 -> x19, local copies, waits for them, and re-layouts: 5.8 us -> 5.1 us
  transfers between devices with their start and end apart: 8 -> 8, of which waited for: 5 -> 5; matrix products, arithmetic and copies ran while one was open for 15% -> 14% of each run, Pallas kernels for 0% -> 0%
where the time goes in v9:
time: 146 us
  Pallas kernels  72.8 us (50%)
  waiting for transfers between devices  24 us (16%)
  starting transfers between devices  22.6 us (15%)
  local copies, waits for them, and re-layouts  9.15 us (6%)
  other arithmetic  9.03 us (6%)
  matrix products  7.06 us (5%)
    pallas_call x3, Pallas kernels, stage(): pl.pallas_call(stage_kernel(scale_level, scale_step, rows_block), grid=(r...  72.8 us
    ppermute x8, waiting for transfers between devices, shifted(): return lax.ppermute(block, axis, route)  24 us
    ppermute x8, starting transfers between devices, shifted(): return lax.ppermute(block, axis, route)  22.6 us
    unnamed x19, local copies, waits for them, and re-layouts  5.1 us
    mul x1, other arithmetic, central_grads(): grad_z = (side[:, 1:-1, 2:] - side[:, 1:-1, :-2]) * 0.5  3.46 us
  transfers between devices with their start and end apart: 8, of which 5 were waited for; matrix products, arithmetic and copies ran while one was open for 14% of the time, Pallas kernels for 0%

profile of v9, /device:TPU:1, one launch (start us, length us, event | category | flops | bytes accessed | tf_op | source)
XLA Modules:
  0.0 145.6 jit_solution(1117675894573801234)
XLA Ops:
  0.6 2.7 %fusion.22 = (f32[14,128,128]{2,1,0:T(8,128)}, f32[14,128,128]{2,1,0:T(8,128)S(1)}) fusion(f32[32,128,128]{2,1,0:T(8,128)} %param.5), kind=kLoop, calls=%fused_computation.35 | loop fusion | bytes 3670016 | tf_op jit(solution)/shard_map/slice | solution.py:249
  3.3 4.5 %collective-permute-start = (f32[14,128,128]{2,1,0:T(8,128)}, f32[14,128,128]{2,1,0:T(8,128)}, u32[]{:S(2)}, u32[]{:S(2)}) collective-permute-start(f32[14,128,128]{2,1,0:T(8,128)} %get-tuple-element.20), channel_id=1, source_target_pairs={{0,1},{1,2},{2,3},{3,4},{4,5},{5,6},{6,7},{7,8},{8,9},{9,10},{10,1... | collective-permute-start | bytes 2752520 | tf_op jit(solution)/shard_map/ppermute | solution.py:18
  7.9 1.9 %collective-permute-start.1 = (f32[14,128,128]{2,1,0:T(8,128)S(1)}, f32[14,128,128]{2,1,0:T(8,128)}, u32[]{:S(2)}, u32[]{:S(2)}) collective-permute-start(f32[14,128,128]{2,1,0:T(8,128)S(1)} %get-tuple-element.21), channel_id=1, source_target_pairs={{1,0},{2,1},{3,2},{4,3},{5,4},{6,5},{7,6},{8,7},{9,8},{10,9},{11,1... | collective-permute-start | bytes 2752520 | tf_op jit(solution)/shard_map/ppermute | solution.py:18
  9.8 1.1 fusion.21
  10.8 1.9 %collective-permute-start.3 = (f32[3,128,128]{2,1,0:T(8,128)S(1)}, f32[3,128,128]{2,1,0:T(8,128)}, u32[]{:S(2)}, u32[]{:S(2)}) collective-permute-start(f32[3,128,128]{2,1,0:T(8,128)S(1)} %get-tuple-element.18), channel_id=1, source_target_pairs={{1,0},{2,1},{3,2},{4,3},{5,4},{6,5},{7,6},{8,7},{9,8},{10,9},{11,1... | collective-permute-start | bytes 589832 | tf_op jit(solution)/shard_map/ppermute | solution.py:18
  12.8 3.6 %collective-permute-start.2 = (f32[3,128,128]{2,1,0:T(8,128)S(1)}, f32[3,128,128]{2,1,0:T(8,128)}, u32[]{:S(2)}, u32[]{:S(2)}) collective-permute-start(f32[3,128,128]{2,1,0:T(8,128)S(1)} %get-tuple-element.19), channel_id=1, source_target_pairs={{0,1},{1,2},{2,3},{3,4},{4,5},{5,6},{6,7},{7,8},{8,9},{9,10},{10,1... | collective-permute-start | bytes 589832 | tf_op jit(solution)/shard_map/ppermute | solution.py:18
  16.5 13.9 %collective-permute-done = f32[14,128,128]{2,1,0:T(8,128)} collective-permute-done((f32[14,128,128]{2,1,0:T(8,128)}, f32[14,128,128]{2,1,0:T(8,128)}, u32[]{:S(2)}, u32[]{:S(2)}) %collective-permute-start) | collective-permute-done | bytes 917536 | tf_op jit(solution)/shard_map/ppermute | solution.py:18
  30.4 1.7 %pad_maximum_fusion = f32[60,128,128]{2,1,0:T(8,128)S(1)} fusion(f32[14,128,128]{2,1,0:T(8,128)} %collective-permute-done.1, f32[32,128,128]{2,1,0:T(8,128)S(1)} %copy-done.1, f32[14,128,128]{2,1,0:T(8,128)} %collective-permute-done), kind=kLoop, calls=%fused_computation.8 | loop fusion | flops 1966080 | bytes 7864320 | tf_op jit(solution)/shard_map/concatenate | solution.py:251
  32.7 2.4 %copy.9 = f32[8,8,128,128]{3,1,2,0:T(8,128)S(1)} copy(f32[8,8,128,128]{3,2,1,0:T(8,128)S(1)} %bitcast.14) | data formatting | bytes 8388608
  35.1 2.5 %fusion.23 = f32[36,16384]{1,0:T(8,128)S(1)} fusion(f32[36,60]{1,0:T(8,128)S(1)} %copy-done.7, f32[60,16384]{1,0:T(8,128)S(1)} %bitcast.15), kind=kOutput, calls=%fused_computation.36 | convolution fusion | flops 424673280 | bytes 6300096 | tf_op jit(solution)/shard_map/dot_general | solution.py:253
  38.5 2.3 %fusion = f32[36,128,128]{1,2,0:T(8,128)S(1)} fusion(f32[128,128,1]{1,0,2:T(8,128)S(1)} %copy-done.2, f32[40,128,128]{2,1,0:T(8,128)S(1)} %bitcast.17), kind=kOutput, calls=%fused_computation.9 | convolution fusion | flops 905969664 | bytes 4784128 | tf_op jit(solution)/shard_map/dot_general | solution.py:258
  40.7 2.2 %select_bitcast_fusion = f32[36,128,128]{2,1,0:T(8,128)S(1)} fusion(f32[36,128,128]{1,2,0:T(8,128)S(1)} %fusion, f32[128,128,1]{1,0,2:T(8,128)S(1)} %copy-done.2, pred[36]{0:T(512)(128)(4,1)S(1)} %compare_and_fusion), kind=kOutput, calls=%fused_computation.11 | convolution fusion | flops 906559488 | bytes 4784164 | tf_op jit(solution)/shard_map/yv,xvz->xyz/dot_general | solution.py:261
  43.2 2.1 %fusion.15 = f32[34,128,128]{2,1,0:T(8,128)S(1)} fusion(f32[34,128,128]{2,1,0:T(8,128)S(1)} %slice.79, f32[36,128,128]{2,1,0:T(8,128)S(1)} %select_bitcast_fusion, pred[34]{0:T(512)(128)(4,1)S(1)} %slice.58), kind=kLoop, calls=%fused_computation.26 | loop fusion | flops 8355840 | bytes 8912930 | tf_op jit(solution)/shard_map/jit(_where)/select_n | solution.py:266
  45.3 1.8 %fusion.20 = (f32[32,128,128]{2,1,0:T(8,128)}, f32[32,128,128]{2,1,0:T(8,128)S(1)}) fusion(f32[34,128,128]{2,1,0:T(8,128)S(1)} %fusion.15), kind=kLoop, calls=%fused_computation.32 | loop fusion | flops 1048576 | bytes 10485760 | tf_op jit(solution)/shard_map/mul | solution.py:68
  47.1 3.5 %fusion.19 = (f32[32,128,128]{2,1,0:T(8,128)}, f32[32,128,128]{2,1,0:T(8,128)}) fusion(f32[32,128,128]{2,1,0:T(8,128)S(1)} %get-tuple-element.15.edge_ref), kind=kLoop, calls=%fused_computation.30 | loop fusion | flops 2097152 | bytes 6291456 | tf_op jit(solution)/shard_map/mul | solution.py:70
  50.6 24.3 %shard_map.68 = (f32[32,128,128]{2,1,0:T(8,128)}, f32[3,128,128]{2,1,0:T(8,128)}, f32[3,128,128]{2,1,0:T(8,128)}) custom-call(f32[3,128,128]{2,1,0:T(8,128)} %collective-permute-done.2.low_ref, f32[32,128,128]{2,1,0:T(8,128)} %ls_ref.5, f32[3,128,128]{2,1,0:T(8,128)} %collective-permute-done.3.high_ref, f32[32,128,128]{2,1,0:T(8,128)} %copy-done, ...), custom_call_target="tpu_custom_call" | custom-call | tf_op jit(solution)/shard_map/pallas_call | solution.py:231
  74.9 4.4 %collective-permute-start.4 = (f32[3,128,128]{2,1,0:T(8,128)}, f32[3,128,128]{2,1,0:T(8,128)S(1)}, u32[]{:S(2)}, u32[]{:S(2)}) collective-permute-start(f32[3,128,128]{2,1,0:T(8,128)} %get-tuple-element.8), channel_id=1, source_target_pairs={{0,1},{1,2},{2,3},{3,4},{4,5},{5,6},{6,7},{7,8},{8,9},{9,10},{10,1... | collective-permute-start | bytes 589832 | tf_op jit(solution)/shard_map/ppermute | solution.py:18
  79.2 1.9 %collective-permute-start.5 = (f32[3,128,128]{2,1,0:T(8,128)}, f32[3,128,128]{2,1,0:T(8,128)S(1)}, u32[]{:S(2)}, u32[]{:S(2)}) collective-permute-start(f32[3,128,128]{2,1,0:T(8,128)} %get-tuple-element.10), channel_id=1, source_target_pairs={{1,0},{2,1},{3,2},{4,3},{5,4},{6,5},{7,6},{8,7},{9,8},{10,9},{11,1... | collective-permute-start | bytes 589832 | tf_op jit(solution)/shard_map/ppermute | solution.py:18
  82.2 4.3 %collective-permute-done.5.high_ref = f32[3,128,128]{2,1,0:T(8,128)S(1)} collective-permute-done((f32[3,128,128]{2,1,0:T(8,128)}, f32[3,128,128]{2,1,0:T(8,128)S(1)}, u32[]{:S(2)}, u32[]{:S(2)}) %collective-permute-start.5) | collective-permute-done | bytes 196640 | tf_op jit(solution)/shard_map/ppermute | solution.py:18
  87.1 24.4 %shard_map.69 = (f32[32,128,128]{2,1,0:T(8,128)}, f32[3,128,128]{2,1,0:T(8,128)}, f32[3,128,128]{2,1,0:T(8,128)}) custom-call(f32[3,128,128]{2,1,0:T(8,128)} %copy-done.5, f32[32,128,128]{2,1,0:T(8,128)} %get-tuple-element.9.main_ref, f32[3,128,128]{2,1,0:T(8,128)} %copy-done.6, f32[32,128,128]{2,1,0:T(8,128)} %copy-done, ...), custom_call_target="tpu_custom_call" | custom-call | tf_op jit(solution)/shard_map/pallas_call | solution.py:231
  111.5 1.9 %collective-permute-start.6 = (f32[3,128,128]{2,1,0:T(8,128)}, f32[3,128,128]{2,1,0:T(8,128)S(1)}, u32[]{:S(2)}, u32[]{:S(2)}) collective-permute-start(f32[3,128,128]{2,1,0:T(8,128)} %get-tuple-element.11), channel_id=1, source_target_pairs={{0,1},{1,2},{2,3},{3,4},{4,5},{5,6},{6,7},{7,8},{8,9},{9,10},{10,1... | collective-permute-start | bytes 589832 | tf_op jit(solution)/shard_map/ppermute | solution.py:18
  113.5 2.4 %collective-permute-start.7 = (f32[3,128,128]{2,1,0:T(8,128)}, f32[3,128,128]{2,1,0:T(8,128)S(1)}, u32[]{:S(2)}, u32[]{:S(2)}) collective-permute-start(f32[3,128,128]{2,1,0:T(8,128)} %get-tuple-element.13), channel_id=1, source_target_pairs={{1,0},{2,1},{3,2},{4,3},{5,4},{6,5},{7,6},{8,7},{9,8},{10,9},{11,1... | collective-permute-start | bytes 589832 | tf_op jit(solution)/shard_map/ppermute | solution.py:18
  116.4 4.3 %collective-permute-done.7.high_ref = f32[3,128,128]{2,1,0:T(8,128)S(1)} collective-permute-done((f32[3,128,128]{2,1,0:T(8,128)}, f32[3,128,128]{2,1,0:T(8,128)S(1)}, u32[]{:S(2)}, u32[]{:S(2)}) %collective-permute-start.7) | collective-permute-done | bytes 196640 | tf_op jit(solution)/shard_map/ppermute | solution.py:18
  121.3 24.1 %shard_map.70 = f32[32,128,128]{2,1,0:T(8,128)} custom-call(f32[3,128,128]{2,1,0:T(8,128)} %copy-done.3, f32[32,128,128]{2,1,0:T(8,128)} %get-tuple-element.12.main_ref, f32[3,128,128]{2,1,0:T(8,128)} %copy-done.4, f32[32,128,128]{2,1,0:T(8,128)} %copy-done, f32[32,128,128]{2,1,0:T(8,128)} %get-tuple-element.14.sx_ref, ...), custom_call_target="tpu_custom_call" | custom-call | tf_op jit(solution)/shard_map/pallas_call | solution.py:231
  (26 shorter events, 4.5 us)
Async XLA Ops:
  0.6 29.8 %copy-start.1 = (f32[32,128,128]{2,1,0:T(8,128)S(1)}, f32[32,128,128]{2,1,0:T(8,128)}, u32[]{:S(2)}) copy-start(f32[32,128,128]{2,1,0:T(8,128)} %param.5) | copy-start | bytes 6291460
  3.3 27.1 %collective-permute-start = (f32[14,128,128]{2,1,0:T(8,128)}, f32[14,128,128]{2,1,0:T(8,128)}, u32[]{:S(2)}, u32[]{:S(2)}) collective-permute-start(f32[14,128,128]{2,1,0:T(8,128)} %get-tuple-element.20), channel_id=1, source_target_pairs={{0,1},{1,2},{2,3},{3,4},{4,5},{5,6},{6,7},{7,8},{8,9},{9,10},{10,1... | collective-permute-start | bytes 2752520 | tf_op jit(solution)/shard_map/ppermute | solution.py:18
  7.9 22.6 %collective-permute-start.1 = (f32[14,128,128]{2,1,0:T(8,128)S(1)}, f32[14,128,128]{2,1,0:T(8,128)}, u32[]{:S(2)}, u32[]{:S(2)}) collective-permute-start(f32[14,128,128]{2,1,0:T(8,128)S(1)} %get-tuple-element.21), channel_id=1, source_target_pairs={{1,0},{2,1},{3,2},{4,3},{5,4},{6,5},{7,6},{8,7},{9,8},{10,9},{11,1... | collective-permute-start | bytes 2752520 | tf_op jit(solution)/shard_map/ppermute | solution.py:18
  10.8 39.7 %collective-permute-start.3 = (f32[3,128,128]{2,1,0:T(8,128)S(1)}, f32[3,128,128]{2,1,0:T(8,128)}, u32[]{:S(2)}, u32[]{:S(2)}) collective-permute-start(f32[3,128,128]{2,1,0:T(8,128)S(1)} %get-tuple-element.18), channel_id=1, source_target_pairs={{1,0},{2,1},{3,2},{4,3},{5,4},{6,5},{7,6},{8,7},{9,8},{10,9},{11,1... | collective-permute-start | bytes 589832 | tf_op jit(solution)/shard_map/ppermute | solution.py:18
  12.8 37.8 %collective-permute-start.2 = (f32[3,128,128]{2,1,0:T(8,128)S(1)}, f32[3,128,128]{2,1,0:T(8,128)}, u32[]{:S(2)}, u32[]{:S(2)}) collective-permute-start(f32[3,128,128]{2,1,0:T(8,128)S(1)} %get-tuple-element.19), channel_id=1, source_target_pairs={{0,1},{1,2},{2,3},{3,4},{4,5},{5,6},{6,7},{7,8},{8,9},{9,10},{10,1... | collective-permute-start | bytes 589832 | tf_op jit(solution)/shard_map/ppermute | solution.py:18
  32.7 2.4 %copy-start.7 = (f32[36,60]{1,0:T(8,128)S(1)}, f32[36,60]{1,0:T(8,128)}, u32[]{:S(2)}) copy-start(f32[36,60]{1,0:T(8,128)} %constant.28.clone) | copy-start | bytes 25924
  37.6 0.8 copy-start.2
  47.1 3.5 %copy-start = (f32[32,128,128]{2,1,0:T(8,128)}, f32[32,128,128]{2,1,0:T(8,128)S(1)}, u32[]{:S(2)}) copy-start(f32[32,128,128]{2,1,0:T(8,128)S(1)} %get-tuple-element.15.edge_ref) | copy-start | bytes 6291460
  74.9 7.3 %collective-permute-start.4 = (f32[3,128,128]{2,1,0:T(8,128)}, f32[3,128,128]{2,1,0:T(8,128)S(1)}, u32[]{:S(2)}, u32[]{:S(2)}) collective-permute-start(f32[3,128,128]{2,1,0:T(8,128)} %get-tuple-element.8), channel_id=1, source_target_pairs={{0,1},{1,2},{2,3},{3,4},{4,5},{5,6},{6,7},{7,8},{8,9},{9,10},{10,1... | collective-permute-start | bytes 589832 | tf_op jit(solution)/shard_map/ppermute | solution.py:18
  79.2 7.2 %collective-permute-start.5 = (f32[3,128,128]{2,1,0:T(8,128)}, f32[3,128,128]{2,1,0:T(8,128)S(1)}, u32[]{:S(2)}, u32[]{:S(2)}) collective-permute-start(f32[3,128,128]{2,1,0:T(8,128)} %get-tuple-element.10), channel_id=1, source_target_pairs={{1,0},{2,1},{3,2},{4,3},{5,4},{6,5},{7,6},{8,7},{9,8},{10,9},{11,1... | collective-permute-start | bytes 589832 | tf_op jit(solution)/shard_map/ppermute | solution.py:18
  82.2 4.3 %copy-start.5 = (f32[3,128,128]{2,1,0:T(8,128)}, f32[3,128,128]{2,1,0:T(8,128)S(1)}, u32[]{:S(2)}) copy-start(f32[3,128,128]{2,1,0:T(8,128)S(1)} %collective-permute-done.4.low_ref) | copy-start | bytes 589828
  86.4 0.7 copy-start.6
  111.5 4.8 %collective-permute-start.6 = (f32[3,128,128]{2,1,0:T(8,128)}, f32[3,128,128]{2,1,0:T(8,128)S(1)}, u32[]{:S(2)}, u32[]{:S(2)}) collective-permute-start(f32[3,128,128]{2,1,0:T(8,128)} %get-tuple-element.11), channel_id=1, source_target_pairs={{0,1},{1,2},{2,3},{3,4},{4,5},{5,6},{6,7},{7,8},{8,9},{9,10},{10,1... | collective-permute-start | bytes 589832 | tf_op jit(solution)/shard_map/ppermute | solution.py:18
  113.5 7.2 %collective-permute-start.7 = (f32[3,128,128]{2,1,0:T(8,128)}, f32[3,128,128]{2,1,0:T(8,128)S(1)}, u32[]{:S(2)}, u32[]{:S(2)}) collective-permute-start(f32[3,128,128]{2,1,0:T(8,128)} %get-tuple-element.13), channel_id=1, source_target_pairs={{1,0},{2,1},{3,2},{4,3},{5,4},{6,5},{7,6},{8,7},{9,8},{10,9},{11,1... | collective-permute-start | bytes 589832 | tf_op jit(solution)/shard_map/ppermute | solution.py:18
  116.4 4.3 %copy-start.3 = (f32[3,128,128]{2,1,0:T(8,128)}, f32[3,128,128]{2,1,0:T(8,128)S(1)}, u32[]{:S(2)}) copy-start(f32[3,128,128]{2,1,0:T(8,128)S(1)} %collective-permute-done.6.low_ref) | copy-start | bytes 589828
  120.7 0.7 copy-start.4

commit v10 on v9

--- a/solution.py
+++ b/solution.py
@@ -118,10 +118,18 @@
 HALO = 3
 
 
-def stage_kernel(scale_level, scale_step, rows_block):
-    def kernel(low_ref, main_ref, high_ref, edge_ref, sx_ref, sy_ref, sz_ref, ls_ref, *rest):
-        out_ref = rest[0]
-        p_ref, sems = rest[-2:]
+def stage_kernel(scale_level, scale_step, rows_block, first):
+    def kernel(*refs):
+        if first:
+            low_ref, main_ref, high_ref, wide_ref, ls_ref = refs[:5]
+            out_ref, top_ref, bottom_ref, edge_ref, sx_ref, sy_ref, sz_ref = refs[5:12]
+            p_ref, e_ref, sems = refs[12:]
+            rest = (out_ref, top_ref, bottom_ref, p_ref, sems)
+        else:
+            low_ref, main_ref, high_ref, edge_ref, sx_ref, sy_ref, sz_ref, ls_ref = refs[:8]
+            rest = refs[8:]
+            out_ref = rest[0]
+            p_ref, sems = rest[-2:]
         rows = main_ref.shape[0]
         rows_y = out_ref.shape[1]
         rows_z = out_ref.shape[2]
@@ -143,6 +151,19 @@
             lax.fori_loop(0, rows + 2 * HALO, clear, 0)
             p_ref[pl.ds(0, HALO), inner, :] = low_ref[...]
             p_ref[pl.ds(HALO + rows, HALO), inner, :] = high_ref[...]
+            if first:
+                spread = pltpu.make_async_copy(
+                    wide_ref, e_ref.at[pl.ds(0, rows + 2), inner, :], sems.at[1]
+                )
+                spread.start()
+
+                def clear_edge(x, carry):
+                    e_ref[x, pl.ds(0, SUB), :] = zeros
+                    e_ref[x, pl.ds(SUB + rows_y, SUB), :] = zeros
+                    return carry
+
+                lax.fori_loop(0, rows + 2, clear_edge, 0)
+                spread.wait()
             copy.wait()
 
         lane = lax.broadcasted_iota(jnp.int32, (SUB, rows_z), 1)
@@ -165,9 +186,28 @@
                 line_y = [at(0, k) for k in range(-HALO, HALO + 1)]
                 line_z = [along_z(centre, k) for k in range(-HALO, HALO + 1)]
                 here = pl.ds(chunk * SUB, SUB)
-                flow_x = upwind(line_x, sx_ref[r, here, :])
-                flow_y = upwind(line_y, sy_ref[r, here, :])
-                flow_z = upwind(line_z, sz_ref[r, here, :])
+                if first:
+                    edge_row = block * rows_block + r + 1
+
+                    def near(step_x, step_y):
+                        return e_ref[edge_row + step_x, pl.ds(top + step_y, SUB), :]
+
+                    edge_here = near(0, 0)
+                    slope_x = (near(1, 0) - near(-1, 0)) * 0.5
+                    slope_y = (near(0, 1) - near(0, -1)) * 0.5
+                    slope_z = (along_z(edge_here, 1) - along_z(edge_here, -1)) * 0.5
+                    edge_ref[r, here, :] = edge_here
+                    sx_ref[r, here, :] = slope_x
+                    sy_ref[r, here, :] = slope_y
+                    sz_ref[r, here, :] = slope_z
+                else:
+                    edge_here = edge_ref[r, here, :]
+                    slope_x = sx_ref[r, here, :]
+                    slope_y = sy_ref[r, here, :]
+                    slope_z = sz_ref[r, here, :]
+                flow_x = upwind(line_x, slope_x)
+                flow_y = upwind(line_y, slope_y)
+                flow_z = upwind(line_z, slope_z)
                 up_x = line_x[HALO + 1]
                 down_x = line_x[HALO - 1]
                 up_y = line_y[HALO + 1]
@@ -197,7 +237,7 @@
                     + first_y * first_z * mixed_yz
                 )
                 curvature = numerator / (square_x + square_y + square_z + 4.0)
-                rate = edge_ref[r, here, :] * curvature + (flow_x + flow_y + flow_z)
+                rate = edge_here * curvature + (flow_x + flow_y + flow_z)
                 moved = centre + 0.1 * rate
                 if scale_level is None:
                     out_ref[r, here, :] = moved
@@ -228,18 +268,28 @@
     side = pl.BlockSpec((HALO, rows_y, rows_z), lambda i: (0, 0, 0))
     result = jax.ShapeDtypeStruct(level_set.shape, level_set.dtype)
     edge_rows = jax.ShapeDtypeStruct((HALO, rows_y, rows_z), level_set.dtype)
+    first = slope is None
+    scratch = [pltpu.VMEM((rows + 2 * HALO, rows_y + 2 * SUB, rows_z), jnp.float32)]
+    if first:
+        scratch.append(pltpu.VMEM((rows + 2, rows_y + 2 * SUB, rows_z), jnp.float32))
+        in_specs = [side, raw, side, raw, part]
+        operands = (low, field, high, edge, level_set)
+        out_specs = [part, side, side, part, part, part, part]
+        out_shape = [result, edge_rows, edge_rows, result, result, result, result]
+    else:
+        in_specs = [side, raw, side, part, part, part, part, part]
+        operands = (low, field, high, edge, slope[0], slope[1], slope[2], level_set)
+        out_specs = [part, side, side] if sides else part
+        out_shape = [result, edge_rows, edge_rows] if sides else result
     return pl.pallas_call(
-        stage_kernel(scale_level, scale_step, rows_block),
+        stage_kernel(scale_level, scale_step, rows_block, first),
         grid=(rows // rows_block,),
-        in_specs=[side, raw, side, part, part, part, part, part],
-        out_specs=[part, side, side] if sides else part,
-        out_shape=[result, edge_rows, edge_rows] if sides else result,
-        scratch_shapes=[
-            pltpu.VMEM((rows + 2 * HALO, rows_y + 2 * SUB, rows_z), jnp.float32),
-            pltpu.SemaphoreType.DMA((1,)),
-        ],
+        in_specs=in_specs,
+        out_specs=out_specs,
+        out_shape=out_shape,
+        scratch_shapes=scratch + [pltpu.SemaphoreType.DMA((2,))],
         compiler_params=pltpu.CompilerParams(dimension_semantics=("arbitrary",)),
-    )(low, field, high, edge, slope[0], slope[1], slope[2], level_set)
+    )(*operands)
 
 
 def shards(volume, level_set):
@@ -264,15 +314,17 @@
     blurred = jnp.where(inside[:, None, None], blurred, 0.0)
     edge_wide = edge_from(blurred)
     edge_wide = jnp.where(inside[1:-1, None, None], edge_wide, 0.0)
-    edge = edge_wide[1:-1]
-    slope = central_grads(edge_wide)
 
     def step(field, top, bottom, scale_level, scale_step, sides=True):
         low = shifted(bottom, "gx", 1)
         high = shifted(top, "gx", -1)
         return stage(low, field, high, edge, slope, level_set, scale_level, scale_step, sides)
 
-    section_one, top, bottom = step(level_set, level_set[:HALO], level_set[rows - HALO :], None, None)
+    low = shifted(level_set[rows - HALO :], "gx", 1)
+    high = shifted(level_set[:HALO], "gx", -1)
+    section_one, top, bottom, edge, *slope = stage(
+        low, level_set, high, edge_wide, None, level_set, None, None, True
+    )
     section_two, top, bottom = step(section_one, top, bottom, 0.75, 0.25)
     advanced = step(section_two, top, bottom, 1.0 / 3.0, 2.0 / 3.0, sides=False)
     return (edge, advanced)

time: 146 us -> 143 us (0.979)
  other arithmetic: 9.03 us -> 4.77 us
    mul x2 -> x0, other arithmetic: 5.24 us -> none  [the longest x1 3.46 us: central_grads(): grad_z = (side[:, 1:-1, 2:] - side[:, 1:-1, :-2]) * 0.5]
    unnamed x19 -> x17, local copies, waits for them, and re-layouts: 5.1 us -> 5.13 us
  transfers between devices with their start and end apart: 8 -> 8, of which waited for: 5 -> 5; matrix products, arithmetic and copies ran while one was open for 14% -> 12% of each run, Pallas kernels for 0% -> 0%
where the time goes in v10:
time: 143 us
  Pallas kernels  73.9 us (52%)
  waiting for transfers between devices  24 us (17%)
  starting transfers between devices  22.6 us (16%)
  local copies, waits for them, and re-layouts  9.18 us (6%)
  matrix products  7.06 us (5%)
  other arithmetic  4.77 us (3%)
    pallas_call x3, Pallas kernels, stage(): pl.pallas_call(stage_kernel(scale_level, scale_step, rows_block, first),...  73.9 us
    ppermute x8, waiting for transfers between devices, shifted(): return lax.ppermute(block, axis, route)  24 us
    ppermute x8, starting transfers between devices, shifted(): return lax.ppermute(block, axis, route)  22.6 us
    unnamed x17, local copies, waits for them, and re-layouts  5.13 us
    select_n x1, other arithmetic, shards(): edge_wide = jnp.where(inside[1:-1, None, None], edge_wide, 0.0)  3.06 us
  transfers between devices with their start and end apart: 8, of which 5 were waited for; matrix products, arithmetic and copies ran while one was open for 12% of the time, Pallas kernels for 0%

profile of v10, /device:TPU:1, one launch (start us, length us, event | category | flops | bytes accessed | tf_op | source)
XLA Modules:
  0.0 142.5 jit_solution(13948210321632666779)
XLA Ops:
  0.6 2.7 %fusion.16 = (f32[14,128,128]{2,1,0:T(8,128)}, f32[14,128,128]{2,1,0:T(8,128)S(1)}) fusion(f32[32,128,128]{2,1,0:T(8,128)} %param.5), kind=kLoop, calls=%fused_computation.24 | loop fusion | bytes 3670016 | tf_op jit(solution)/shard_map/slice | solution.py:299
  3.3 4.5 %collective-permute-start.2 = (f32[14,128,128]{2,1,0:T(8,128)}, f32[14,128,128]{2,1,0:T(8,128)}, u32[]{:S(2)}, u32[]{:S(2)}) collective-permute-start(f32[14,128,128]{2,1,0:T(8,128)} %get-tuple-element.22), channel_id=1, source_target_pairs={{0,1},{1,2},{2,3},{3,4},{4,5},{5,6},{6,7},{7,8},{8,9},{9,10},{10,1... | collective-permute-start | bytes 2752520 | tf_op jit(solution)/shard_map/ppermute | solution.py:18
  7.9 1.9 %collective-permute-start.3 = (f32[14,128,128]{2,1,0:T(8,128)S(1)}, f32[14,128,128]{2,1,0:T(8,128)}, u32[]{:S(2)}, u32[]{:S(2)}) collective-permute-start(f32[14,128,128]{2,1,0:T(8,128)S(1)} %get-tuple-element.23), channel_id=1, source_target_pairs={{1,0},{2,1},{3,2},{4,3},{5,4},{6,5},{7,6},{8,7},{9,8},{10,9},{11,1... | collective-permute-start | bytes 2752520 | tf_op jit(solution)/shard_map/ppermute | solution.py:18
  9.8 1.1 fusion.17
  10.8 1.9 %collective-permute-start.1 = (f32[3,128,128]{2,1,0:T(8,128)S(1)}, f32[3,128,128]{2,1,0:T(8,128)}, u32[]{:S(2)}, u32[]{:S(2)}) collective-permute-start(f32[3,128,128]{2,1,0:T(8,128)S(1)} %get-tuple-element.24), channel_id=1, source_target_pairs={{1,0},{2,1},{3,2},{4,3},{5,4},{6,5},{7,6},{8,7},{9,8},{10,9},{11,1... | collective-permute-start | bytes 589832 | tf_op jit(solution)/shard_map/ppermute | solution.py:18
  12.8 3.6 %collective-permute-start = (f32[3,128,128]{2,1,0:T(8,128)S(1)}, f32[3,128,128]{2,1,0:T(8,128)}, u32[]{:S(2)}, u32[]{:S(2)}) collective-permute-start(f32[3,128,128]{2,1,0:T(8,128)S(1)} %get-tuple-element.25), channel_id=1, source_target_pairs={{0,1},{1,2},{2,3},{3,4},{4,5},{5,6},{6,7},{7,8},{8,9},{9,10},{10,1... | collective-permute-start | bytes 589832 | tf_op jit(solution)/shard_map/ppermute | solution.py:18
  16.5 13.9 %collective-permute-done.2 = f32[14,128,128]{2,1,0:T(8,128)} collective-permute-done((f32[14,128,128]{2,1,0:T(8,128)}, f32[14,128,128]{2,1,0:T(8,128)}, u32[]{:S(2)}, u32[]{:S(2)}) %collective-permute-start.2) | collective-permute-done | bytes 917536 | tf_op jit(solution)/shard_map/ppermute | solution.py:18
  30.4 1.7 %pad_maximum_fusion = f32[60,128,128]{2,1,0:T(8,128)S(1)} fusion(f32[14,128,128]{2,1,0:T(8,128)} %collective-permute-done.3, f32[32,128,128]{2,1,0:T(8,128)S(1)} %copy-done, f32[14,128,128]{2,1,0:T(8,128)} %collective-permute-done.2), kind=kLoop, calls=%fused_computation.4 | loop fusion | flops 1966080 | bytes 7864320 | tf_op jit(solution)/shard_map/concatenate | solution.py:301
  32.7 2.4 %copy.9 = f32[8,8,128,128]{3,1,2,0:T(8,128)S(1)} copy(f32[8,8,128,128]{3,2,1,0:T(8,128)S(1)} %bitcast.14) | data formatting | bytes 8388608
  35.1 2.5 %fusion.18 = f32[36,16384]{1,0:T(8,128)S(1)} fusion(f32[36,60]{1,0:T(8,128)S(1)} %copy-done.6, f32[60,16384]{1,0:T(8,128)S(1)} %bitcast.15), kind=kOutput, calls=%fused_computation.26 | convolution fusion | flops 424673280 | bytes 6300096 | tf_op jit(solution)/shard_map/dot_general | solution.py:303
  38.5 2.3 %fusion = f32[36,128,128]{1,2,0:T(8,128)S(1)} fusion(f32[128,128,1]{1,0,2:T(8,128)S(1)} %copy-done.1, f32[40,128,128]{2,1,0:T(8,128)S(1)} %bitcast.17), kind=kOutput, calls=%fused_computation.5 | convolution fusion | flops 905969664 | bytes 4784128 | tf_op jit(solution)/shard_map/dot_general | solution.py:308
  40.7 2.2 %select_bitcast_fusion = f32[36,128,128]{2,1,0:T(8,128)S(1)} fusion(f32[36,128,128]{1,2,0:T(8,128)S(1)} %fusion, f32[128,128,1]{1,0,2:T(8,128)S(1)} %copy-done.1, pred[36]{0:T(512)(128)(4,1)S(1)} %compare_and_fusion), kind=kOutput, calls=%fused_computation.7 | convolution fusion | flops 906559488 | bytes 4784164 | tf_op jit(solution)/shard_map/yv,xvz->xyz/dot_general | solution.py:311
  43.2 3.1 %fusion.15.refs_3_ = f32[34,128,128]{2,1,0:T(8,128)} fusion(f32[34,128,128]{2,1,0:T(8,128)S(1)} %slice.50, f32[36,128,128]{2,1,0:T(8,128)S(1)} %select_bitcast_fusion, pred[34]{0:T(512)(128)(4,1)S(1)} %slice.38), kind=kLoop, calls=%fused_computation.22 | loop fusion | flops 8355840 | bytes 8912930 | tf_op jit(solution)/shard_map/jit(_where)/select_n | solution.py:316
  46.3 25.3 %shard_map.68 = (f32[32,128,128]{2,1,0:T(8,128)}, f32[3,128,128]{2,1,0:T(8,128)}, f32[3,128,128]{2,1,0:T(8,128)}, f32[32,128,128]{2,1,0:T(8,128)}, f32[32,128,12...) custom-call(f32[3,128,128]{2,1,0:T(8,128)} %collective-permute-done.refs_0_, ...), custom_call_target="tpu_custom_call" | custom-call | tf_op jit(solution)/shard_map/pallas_call | solution.py:284
  71.6 4.4 %collective-permute-start.4 = (f32[3,128,128]{2,1,0:T(8,128)}, f32[3,128,128]{2,1,0:T(8,128)S(1)}, u32[]{:S(2)}, u32[]{:S(2)}) collective-permute-start(f32[3,128,128]{2,1,0:T(8,128)} %get-tuple-element.13), channel_id=1, source_target_pairs={{0,1},{1,2},{2,3},{3,4},{4,5},{5,6},{6,7},{7,8},{8,9},{9,10},{10,1... | collective-permute-start | bytes 589832 | tf_op jit(solution)/shard_map/ppermute | solution.py:18
  76.0 1.9 %collective-permute-start.5 = (f32[3,128,128]{2,1,0:T(8,128)}, f32[3,128,128]{2,1,0:T(8,128)S(1)}, u32[]{:S(2)}, u32[]{:S(2)}) collective-permute-start(f32[3,128,128]{2,1,0:T(8,128)} %get-tuple-element.15), channel_id=1, source_target_pairs={{1,0},{2,1},{3,2},{4,3},{5,4},{6,5},{7,6},{8,7},{9,8},{10,9},{11,1... | collective-permute-start | bytes 589832 | tf_op jit(solution)/shard_map/ppermute | solution.py:18
  78.0 1.0 collective-permute-done.4.refs_0_
  78.9 4.3 %collective-permute-done.5.refs_2_ = f32[3,128,128]{2,1,0:T(8,128)S(1)} collective-permute-done((f32[3,128,128]{2,1,0:T(8,128)}, f32[3,128,128]{2,1,0:T(8,128)S(1)}, u32[]{:S(2)}, u32[]{:S(2)}) %collective-permute-start.5) | collective-permute-done | bytes 196640 | tf_op jit(solution)/shard_map/ppermute | solution.py:18
  83.2 0.7 copy-done.5
  83.9 24.4 %shard_map.69 = (f32[32,128,128]{2,1,0:T(8,128)}, f32[3,128,128]{2,1,0:T(8,128)}, f32[3,128,128]{2,1,0:T(8,128)}) custom-call(f32[3,128,128]{2,1,0:T(8,128)} %copy-done.4, f32[32,128,128]{2,1,0:T(8,128)} %get-tuple-element.14.refs_1_, f32[3,128,128]{2,1,0:T(8,128)} %copy-done.5, f32[32,128,128]{2,1,0:T(8,128)} %get-tuple-element.10.refs_3_, ...), custom_call_target="tpu_custom_call" | custom-call | tf_op jit(solution)/shard_map/pallas_call | solution.py:284
  108.4 1.9 %collective-permute-start.6 = (f32[3,128,128]{2,1,0:T(8,128)}, f32[3,128,128]{2,1,0:T(8,128)S(1)}, u32[]{:S(2)}, u32[]{:S(2)}) collective-permute-start(f32[3,128,128]{2,1,0:T(8,128)} %get-tuple-element.19), channel_id=1, source_target_pairs={{0,1},{1,2},{2,3},{3,4},{4,5},{5,6},{6,7},{7,8},{8,9},{9,10},{10,1... | collective-permute-start | bytes 589832 | tf_op jit(solution)/shard_map/ppermute | solution.py:18
  110.3 2.4 %collective-permute-start.7 = (f32[3,128,128]{2,1,0:T(8,128)}, f32[3,128,128]{2,1,0:T(8,128)S(1)}, u32[]{:S(2)}, u32[]{:S(2)}) collective-permute-start(f32[3,128,128]{2,1,0:T(8,128)} %get-tuple-element.21), channel_id=1, source_target_pairs={{1,0},{2,1},{3,2},{4,3},{5,4},{6,5},{7,6},{8,7},{9,8},{10,9},{11,1... | collective-permute-start | bytes 589832 | tf_op jit(solution)/shard_map/ppermute | solution.py:18
  113.2 4.3 %collective-permute-done.7.refs_2_ = f32[3,128,128]{2,1,0:T(8,128)S(1)} collective-permute-done((f32[3,128,128]{2,1,0:T(8,128)}, f32[3,128,128]{2,1,0:T(8,128)S(1)}, u32[]{:S(2)}, u32[]{:S(2)}) %collective-permute-start.7) | collective-permute-done | bytes 196640 | tf_op jit(solution)/shard_map/ppermute | solution.py:18
  118.2 24.2 %shard_map.70 = f32[32,128,128]{2,1,0:T(8,128)} custom-call(f32[3,128,128]{2,1,0:T(8,128)} %copy-done.2, f32[32,128,128]{2,1,0:T(8,128)} %get-tuple-element.20.refs_1_, f32[3,128,128]{2,1,0:T(8,128)} %copy-done.3, f32[32,128,128]{2,1,0:T(8,128)} %get-tuple-element.10.refs_3_, f32[32,128,128]{2,1,0:T(8,128)} %get-tuple-element.16.refs_4_, ...), custom_call_target="tpu_custom_call" | custom-call | tf_op jit(solution)/shard_map/pallas_call | solution.py:284
  (22 shorter events, 2.9 us)
Async XLA Ops:
  0.6 29.8 %copy-start = (f32[32,128,128]{2,1,0:T(8,128)S(1)}, f32[32,128,128]{2,1,0:T(8,128)}, u32[]{:S(2)}) copy-start(f32[32,128,128]{2,1,0:T(8,128)} %param.5) | copy-start | bytes 6291460
  3.3 27.1 %collective-permute-start.2 = (f32[14,128,128]{2,1,0:T(8,128)}, f32[14,128,128]{2,1,0:T(8,128)}, u32[]{:S(2)}, u32[]{:S(2)}) collective-permute-start(f32[14,128,128]{2,1,0:T(8,128)} %get-tuple-element.22), channel_id=1, source_target_pairs={{0,1},{1,2},{2,3},{3,4},{4,5},{5,6},{6,7},{7,8},{8,9},{9,10},{10,1... | collective-permute-start | bytes 2752520 | tf_op jit(solution)/shard_map/ppermute | solution.py:18
  7.9 22.6 %collective-permute-start.3 = (f32[14,128,128]{2,1,0:T(8,128)S(1)}, f32[14,128,128]{2,1,0:T(8,128)}, u32[]{:S(2)}, u32[]{:S(2)}) collective-permute-start(f32[14,128,128]{2,1,0:T(8,128)S(1)} %get-tuple-element.23), channel_id=1, source_target_pairs={{1,0},{2,1},{3,2},{4,3},{5,4},{6,5},{7,6},{8,7},{9,8},{10,9},{11,1... | collective-permute-start | bytes 2752520 | tf_op jit(solution)/shard_map/ppermute | solution.py:18
  10.8 35.5 %collective-permute-start.1 = (f32[3,128,128]{2,1,0:T(8,128)S(1)}, f32[3,128,128]{2,1,0:T(8,128)}, u32[]{:S(2)}, u32[]{:S(2)}) collective-permute-start(f32[3,128,128]{2,1,0:T(8,128)S(1)} %get-tuple-element.24), channel_id=1, source_target_pairs={{1,0},{2,1},{3,2},{4,3},{5,4},{6,5},{7,6},{8,7},{9,8},{10,9},{11,1... | collective-permute-start | bytes 589832 | tf_op jit(solution)/shard_map/ppermute | solution.py:18
  12.8 33.5 %collective-permute-start = (f32[3,128,128]{2,1,0:T(8,128)S(1)}, f32[3,128,128]{2,1,0:T(8,128)}, u32[]{:S(2)}, u32[]{:S(2)}) collective-permute-start(f32[3,128,128]{2,1,0:T(8,128)S(1)} %get-tuple-element.25), channel_id=1, source_target_pairs={{0,1},{1,2},{2,3},{3,4},{4,5},{5,6},{6,7},{7,8},{8,9},{9,10},{10,1... | collective-permute-start | bytes 589832 | tf_op jit(solution)/shard_map/ppermute | solution.py:18
  32.7 2.4 %copy-start.6 = (f32[36,60]{1,0:T(8,128)S(1)}, f32[36,60]{1,0:T(8,128)}, u32[]{:S(2)}) copy-start(f32[36,60]{1,0:T(8,128)} %constant.27.clone) | copy-start | bytes 25924
  37.6 0.8 copy-start.1
  71.6 7.3 %collective-permute-start.4 = (f32[3,128,128]{2,1,0:T(8,128)}, f32[3,128,128]{2,1,0:T(8,128)S(1)}, u32[]{:S(2)}, u32[]{:S(2)}) collective-permute-start(f32[3,128,128]{2,1,0:T(8,128)} %get-tuple-element.13), channel_id=1, source_target_pairs={{0,1},{1,2},{2,3},{3,4},{4,5},{5,6},{6,7},{7,8},{8,9},{9,10},{10,1... | collective-permute-start | bytes 589832 | tf_op jit(solution)/shard_map/ppermute | solution.py:18
  76.0 7.2 %collective-permute-start.5 = (f32[3,128,128]{2,1,0:T(8,128)}, f32[3,128,128]{2,1,0:T(8,128)S(1)}, u32[]{:S(2)}, u32[]{:S(2)}) collective-permute-start(f32[3,128,128]{2,1,0:T(8,128)} %get-tuple-element.15), channel_id=1, source_target_pairs={{1,0},{2,1},{3,2},{4,3},{5,4},{6,5},{7,6},{8,7},{9,8},{10,9},{11,1... | collective-permute-start | bytes 589832 | tf_op jit(solution)/shard_map/ppermute | solution.py:18
  78.9 4.3 %copy-start.4 = (f32[3,128,128]{2,1,0:T(8,128)}, f32[3,128,128]{2,1,0:T(8,128)S(1)}, u32[]{:S(2)}) copy-start(f32[3,128,128]{2,1,0:T(8,128)S(1)} %collective-permute-done.4.refs_0_) | copy-start | bytes 589828
  83.2 0.7 copy-start.5
  108.4 4.8 %collective-permute-start.6 = (f32[3,128,128]{2,1,0:T(8,128)}, f32[3,128,128]{2,1,0:T(8,128)S(1)}, u32[]{:S(2)}, u32[]{:S(2)}) collective-permute-start(f32[3,128,128]{2,1,0:T(8,128)} %get-tuple-element.19), channel_id=1, source_target_pairs={{0,1},{1,2},{2,3},{3,4},{4,5},{5,6},{6,7},{7,8},{8,9},{9,10},{10,1... | collective-permute-start | bytes 589832 | tf_op jit(solution)/shard_map/ppermute | solution.py:18
  110.3 7.2 %collective-permute-start.7 = (f32[3,128,128]{2,1,0:T(8,128)}, f32[3,128,128]{2,1,0:T(8,128)S(1)}, u32[]{:S(2)}, u32[]{:S(2)}) collective-permute-start(f32[3,128,128]{2,1,0:T(8,128)} %get-tuple-element.21), channel_id=1, source_target_pairs={{1,0},{2,1},{3,2},{4,3},{5,4},{6,5},{7,6},{8,7},{9,8},{10,9},{11,1... | collective-permute-start | bytes 589832 | tf_op jit(solution)/shard_map/ppermute | solution.py:18
  113.2 4.3 %copy-start.2 = (f32[3,128,128]{2,1,0:T(8,128)}, f32[3,128,128]{2,1,0:T(8,128)S(1)}, u32[]{:S(2)}) copy-start(f32[3,128,128]{2,1,0:T(8,128)S(1)} %collective-permute-done.6.refs_0_) | copy-start | bytes 589828
  117.5 0.7 copy-start.3

commit v11 on v10

--- a/solution.py
+++ b/solution.py
@@ -99,9 +99,9 @@
     square_one = denom_one * denom_one
     square_two = denom_two * denom_two
     square_three = denom_three * denom_three
-    weight_one = 0.1 * (square_two * square_three)
-    weight_two = 0.6 * (square_one * square_three)
-    weight_three = 0.3 * (square_one * square_two)
+    weight_one = square_two * square_three
+    weight_two = 6.0 * (square_one * square_three)
+    weight_three = 3.0 * (square_one * square_two)
     return third + (weight_one * cand_one + weight_two * cand_two + weight_three * cand_three) / (
         6.0 * (weight_one + weight_two + weight_three)
     )

time: 143 us -> 142 us (level)
  no operation moved by 1% of the time
where the time goes in v11:
time: 142 us
  Pallas kernels  73.1 us (51%)
  waiting for transfers between devices  24 us (17%)
  starting transfers between devices  22.6 us (16%)
  local copies, waits for them, and re-layouts  9.18 us (6%)
  matrix products  7.06 us (5%)
  other arithmetic  4.77 us (3%)
    pallas_call x3, Pallas kernels, stage(): pl.pallas_call(stage_kernel(scale_level, scale_step, rows_block, first),...  73.1 us
    ppermute x8, waiting for transfers between devices, shifted(): return lax.ppermute(block, axis, route)  24 us
    ppermute x8, starting transfers between devices, shifted(): return lax.ppermute(block, axis, route)  22.6 us
    unnamed x17, local copies, waits for them, and re-layouts  5.13 us
    select_n x1, other arithmetic, shards(): edge_wide = jnp.where(inside[1:-1, None, None], edge_wide, 0.0)  3.06 us
  transfers between devices with their start and end apart: 8, of which 5 were waited for; matrix products, arithmetic and copies ran while one was open for 12% of the time, Pallas kernels for 0%

profile of v11, /device:TPU:1, one launch (start us, length us, event | category | flops | bytes accessed | tf_op | source)
XLA Modules:
  0.0 141.7 jit_solution(13989613788869418927)
XLA Ops:
  0.6 2.7 %fusion.16 = (f32[14,128,128]{2,1,0:T(8,128)}, f32[14,128,128]{2,1,0:T(8,128)S(1)}) fusion(f32[32,128,128]{2,1,0:T(8,128)} %param.5), kind=kLoop, calls=%fused_computation.24 | loop fusion | bytes 3670016 | tf_op jit(solution)/shard_map/slice | solution.py:299
  3.3 4.5 %collective-permute-start.2 = (f32[14,128,128]{2,1,0:T(8,128)}, f32[14,128,128]{2,1,0:T(8,128)}, u32[]{:S(2)}, u32[]{:S(2)}) collective-permute-start(f32[14,128,128]{2,1,0:T(8,128)} %get-tuple-element.22), channel_id=1, source_target_pairs={{0,1},{1,2},{2,3},{3,4},{4,5},{5,6},{6,7},{7,8},{8,9},{9,10},{10,1... | collective-permute-start | bytes 2752520 | tf_op jit(solution)/shard_map/ppermute | solution.py:18
  7.9 1.9 %collective-permute-start.3 = (f32[14,128,128]{2,1,0:T(8,128)S(1)}, f32[14,128,128]{2,1,0:T(8,128)}, u32[]{:S(2)}, u32[]{:S(2)}) collective-permute-start(f32[14,128,128]{2,1,0:T(8,128)S(1)} %get-tuple-element.23), channel_id=1, source_target_pairs={{1,0},{2,1},{3,2},{4,3},{5,4},{6,5},{7,6},{8,7},{9,8},{10,9},{11,1... | collective-permute-start | bytes 2752520 | tf_op jit(solution)/shard_map/ppermute | solution.py:18
  9.8 1.1 fusion.17
  10.8 1.9 %collective-permute-start.1 = (f32[3,128,128]{2,1,0:T(8,128)S(1)}, f32[3,128,128]{2,1,0:T(8,128)}, u32[]{:S(2)}, u32[]{:S(2)}) collective-permute-start(f32[3,128,128]{2,1,0:T(8,128)S(1)} %get-tuple-element.24), channel_id=1, source_target_pairs={{1,0},{2,1},{3,2},{4,3},{5,4},{6,5},{7,6},{8,7},{9,8},{10,9},{11,1... | collective-permute-start | bytes 589832 | tf_op jit(solution)/shard_map/ppermute | solution.py:18
  12.8 3.6 %collective-permute-start = (f32[3,128,128]{2,1,0:T(8,128)S(1)}, f32[3,128,128]{2,1,0:T(8,128)}, u32[]{:S(2)}, u32[]{:S(2)}) collective-permute-start(f32[3,128,128]{2,1,0:T(8,128)S(1)} %get-tuple-element.25), channel_id=1, source_target_pairs={{0,1},{1,2},{2,3},{3,4},{4,5},{5,6},{6,7},{7,8},{8,9},{9,10},{10,1... | collective-permute-start | bytes 589832 | tf_op jit(solution)/shard_map/ppermute | solution.py:18
  16.5 13.9 %collective-permute-done.2 = f32[14,128,128]{2,1,0:T(8,128)} collective-permute-done((f32[14,128,128]{2,1,0:T(8,128)}, f32[14,128,128]{2,1,0:T(8,128)}, u32[]{:S(2)}, u32[]{:S(2)}) %collective-permute-start.2) | collective-permute-done | bytes 917536 | tf_op jit(solution)/shard_map/ppermute | solution.py:18
  30.4 1.7 %pad_maximum_fusion = f32[60,128,128]{2,1,0:T(8,128)S(1)} fusion(f32[14,128,128]{2,1,0:T(8,128)} %collective-permute-done.3, f32[32,128,128]{2,1,0:T(8,128)S(1)} %copy-done, f32[14,128,128]{2,1,0:T(8,128)} %collective-permute-done.2), kind=kLoop, calls=%fused_computation.4 | loop fusion | flops 1966080 | bytes 7864320 | tf_op jit(solution)/shard_map/concatenate | solution.py:301
  32.7 2.4 %copy.9 = f32[8,8,128,128]{3,1,2,0:T(8,128)S(1)} copy(f32[8,8,128,128]{3,2,1,0:T(8,128)S(1)} %bitcast.14) | data formatting | bytes 8388608
  35.1 2.5 %fusion.18 = f32[36,16384]{1,0:T(8,128)S(1)} fusion(f32[36,60]{1,0:T(8,128)S(1)} %copy-done.6, f32[60,16384]{1,0:T(8,128)S(1)} %bitcast.15), kind=kOutput, calls=%fused_computation.26 | convolution fusion | flops 424673280 | bytes 6300096 | tf_op jit(solution)/shard_map/dot_general | solution.py:303
  38.5 2.3 %fusion = f32[36,128,128]{1,2,0:T(8,128)S(1)} fusion(f32[128,128,1]{1,0,2:T(8,128)S(1)} %copy-done.1, f32[40,128,128]{2,1,0:T(8,128)S(1)} %bitcast.17), kind=kOutput, calls=%fused_computation.5 | convolution fusion | flops 905969664 | bytes 4784128 | tf_op jit(solution)/shard_map/dot_general | solution.py:308
  40.7 2.2 %select_bitcast_fusion = f32[36,128,128]{2,1,0:T(8,128)S(1)} fusion(f32[36,128,128]{1,2,0:T(8,128)S(1)} %fusion, f32[128,128,1]{1,0,2:T(8,128)S(1)} %copy-done.1, pred[36]{0:T(512)(128)(4,1)S(1)} %compare_and_fusion), kind=kOutput, calls=%fused_computation.7 | convolution fusion | flops 906559488 | bytes 4784164 | tf_op jit(solution)/shard_map/yv,xvz->xyz/dot_general | solution.py:311
  43.2 3.1 %fusion.15.refs_3_ = f32[34,128,128]{2,1,0:T(8,128)} fusion(f32[34,128,128]{2,1,0:T(8,128)S(1)} %slice.50, f32[36,128,128]{2,1,0:T(8,128)S(1)} %select_bitcast_fusion, pred[34]{0:T(512)(128)(4,1)S(1)} %slice.38), kind=kLoop, calls=%fused_computation.22 | loop fusion | flops 8355840 | bytes 8912930 | tf_op jit(solution)/shard_map/jit(_where)/select_n | solution.py:316
  46.3 25.0 %shard_map.68 = (f32[32,128,128]{2,1,0:T(8,128)}, f32[3,128,128]{2,1,0:T(8,128)}, f32[3,128,128]{2,1,0:T(8,128)}, f32[32,128,128]{2,1,0:T(8,128)}, f32[32,128,12...) custom-call(f32[3,128,128]{2,1,0:T(8,128)} %collective-permute-done.refs_0_, ...), custom_call_target="tpu_custom_call" | custom-call | tf_op jit(solution)/shard_map/pallas_call | solution.py:284
  71.4 4.4 %collective-permute-start.4 = (f32[3,128,128]{2,1,0:T(8,128)}, f32[3,128,128]{2,1,0:T(8,128)S(1)}, u32[]{:S(2)}, u32[]{:S(2)}) collective-permute-start(f32[3,128,128]{2,1,0:T(8,128)} %get-tuple-element.13), channel_id=1, source_target_pairs={{0,1},{1,2},{2,3},{3,4},{4,5},{5,6},{6,7},{7,8},{8,9},{9,10},{10,1... | collective-permute-start | bytes 589832 | tf_op jit(solution)/shard_map/ppermute | solution.py:18
  75.7 1.9 %collective-permute-start.5 = (f32[3,128,128]{2,1,0:T(8,128)}, f32[3,128,128]{2,1,0:T(8,128)S(1)}, u32[]{:S(2)}, u32[]{:S(2)}) collective-permute-start(f32[3,128,128]{2,1,0:T(8,128)} %get-tuple-element.15), channel_id=1, source_target_pairs={{1,0},{2,1},{3,2},{4,3},{5,4},{6,5},{7,6},{8,7},{9,8},{10,9},{11,1... | collective-permute-start | bytes 589832 | tf_op jit(solution)/shard_map/ppermute | solution.py:18
  77.7 1.0 collective-permute-done.4.refs_0_
  78.7 4.3 %collective-permute-done.5.refs_2_ = f32[3,128,128]{2,1,0:T(8,128)S(1)} collective-permute-done((f32[3,128,128]{2,1,0:T(8,128)}, f32[3,128,128]{2,1,0:T(8,128)S(1)}, u32[]{:S(2)}, u32[]{:S(2)}) %collective-permute-start.5) | collective-permute-done | bytes 196640 | tf_op jit(solution)/shard_map/ppermute | solution.py:18
  83.0 0.7 copy-done.5
  83.7 24.1 %shard_map.69 = (f32[32,128,128]{2,1,0:T(8,128)}, f32[3,128,128]{2,1,0:T(8,128)}, f32[3,128,128]{2,1,0:T(8,128)}) custom-call(f32[3,128,128]{2,1,0:T(8,128)} %copy-done.4, f32[32,128,128]{2,1,0:T(8,128)} %get-tuple-element.14.refs_1_, f32[3,128,128]{2,1,0:T(8,128)} %copy-done.5, f32[32,128,128]{2,1,0:T(8,128)} %get-tuple-element.10.refs_3_, ...), custom_call_target="tpu_custom_call" | custom-call | tf_op jit(solution)/shard_map/pallas_call | solution.py:284
  107.8 1.9 %collective-permute-start.6 = (f32[3,128,128]{2,1,0:T(8,128)}, f32[3,128,128]{2,1,0:T(8,128)S(1)}, u32[]{:S(2)}, u32[]{:S(2)}) collective-permute-start(f32[3,128,128]{2,1,0:T(8,128)} %get-tuple-element.19), channel_id=1, source_target_pairs={{0,1},{1,2},{2,3},{3,4},{4,5},{5,6},{6,7},{7,8},{8,9},{9,10},{10,1... | collective-permute-start | bytes 589832 | tf_op jit(solution)/shard_map/ppermute | solution.py:18
  109.7 2.4 %collective-permute-start.7 = (f32[3,128,128]{2,1,0:T(8,128)}, f32[3,128,128]{2,1,0:T(8,128)S(1)}, u32[]{:S(2)}, u32[]{:S(2)}) collective-permute-start(f32[3,128,128]{2,1,0:T(8,128)} %get-tuple-element.21), channel_id=1, source_target_pairs={{1,0},{2,1},{3,2},{4,3},{5,4},{6,5},{7,6},{8,7},{9,8},{10,9},{11,1... | collective-permute-start | bytes 589832 | tf_op jit(solution)/shard_map/ppermute | solution.py:18
  112.6 4.3 %collective-permute-done.7.refs_2_ = f32[3,128,128]{2,1,0:T(8,128)S(1)} collective-permute-done((f32[3,128,128]{2,1,0:T(8,128)}, f32[3,128,128]{2,1,0:T(8,128)S(1)}, u32[]{:S(2)}, u32[]{:S(2)}) %collective-permute-start.7) | collective-permute-done | bytes 196640 | tf_op jit(solution)/shard_map/ppermute | solution.py:18
  117.6 23.9 %shard_map.70 = f32[32,128,128]{2,1,0:T(8,128)} custom-call(f32[3,128,128]{2,1,0:T(8,128)} %copy-done.2, f32[32,128,128]{2,1,0:T(8,128)} %get-tuple-element.20.refs_1_, f32[3,128,128]{2,1,0:T(8,128)} %copy-done.3, f32[32,128,128]{2,1,0:T(8,128)} %get-tuple-element.10.refs_3_, f32[32,128,128]{2,1,0:T(8,128)} %get-tuple-element.16.refs_4_, ...), custom_call_target="tpu_custom_call" | custom-call | tf_op jit(solution)/shard_map/pallas_call | solution.py:284
  (22 shorter events, 2.9 us)
Async XLA Ops:
  0.6 29.8 %copy-start = (f32[32,128,128]{2,1,0:T(8,128)S(1)}, f32[32,128,128]{2,1,0:T(8,128)}, u32[]{:S(2)}) copy-start(f32[32,128,128]{2,1,0:T(8,128)} %param.5) | copy-start | bytes 6291460
  3.3 27.1 %collective-permute-start.2 = (f32[14,128,128]{2,1,0:T(8,128)}, f32[14,128,128]{2,1,0:T(8,128)}, u32[]{:S(2)}, u32[]{:S(2)}) collective-permute-start(f32[14,128,128]{2,1,0:T(8,128)} %get-tuple-element.22), channel_id=1, source_target_pairs={{0,1},{1,2},{2,3},{3,4},{4,5},{5,6},{6,7},{7,8},{8,9},{9,10},{10,1... | collective-permute-start | bytes 2752520 | tf_op jit(solution)/shard_map/ppermute | solution.py:18
  7.9 22.6 %collective-permute-start.3 = (f32[14,128,128]{2,1,0:T(8,128)S(1)}, f32[14,128,128]{2,1,0:T(8,128)}, u32[]{:S(2)}, u32[]{:S(2)}) collective-permute-start(f32[14,128,128]{2,1,0:T(8,128)S(1)} %get-tuple-element.23), channel_id=1, source_target_pairs={{1,0},{2,1},{3,2},{4,3},{5,4},{6,5},{7,6},{8,7},{9,8},{10,9},{11,1... | collective-permute-start | bytes 2752520 | tf_op jit(solution)/shard_map/ppermute | solution.py:18
  10.8 35.5 %collective-permute-start.1 = (f32[3,128,128]{2,1,0:T(8,128)S(1)}, f32[3,128,128]{2,1,0:T(8,128)}, u32[]{:S(2)}, u32[]{:S(2)}) collective-permute-start(f32[3,128,128]{2,1,0:T(8,128)S(1)} %get-tuple-element.24), channel_id=1, source_target_pairs={{1,0},{2,1},{3,2},{4,3},{5,4},{6,5},{7,6},{8,7},{9,8},{10,9},{11,1... | collective-permute-start | bytes 589832 | tf_op jit(solution)/shard_map/ppermute | solution.py:18
  12.8 33.5 %collective-permute-start = (f32[3,128,128]{2,1,0:T(8,128)S(1)}, f32[3,128,128]{2,1,0:T(8,128)}, u32[]{:S(2)}, u32[]{:S(2)}) collective-permute-start(f32[3,128,128]{2,1,0:T(8,128)S(1)} %get-tuple-element.25), channel_id=1, source_target_pairs={{0,1},{1,2},{2,3},{3,4},{4,5},{5,6},{6,7},{7,8},{8,9},{9,10},{10,1... | collective-permute-start | bytes 589832 | tf_op jit(solution)/shard_map/ppermute | solution.py:18
  32.7 2.4 %copy-start.6 = (f32[36,60]{1,0:T(8,128)S(1)}, f32[36,60]{1,0:T(8,128)}, u32[]{:S(2)}) copy-start(f32[36,60]{1,0:T(8,128)} %constant.27.clone) | copy-start | bytes 25924
  37.6 0.8 copy-start.1
  71.4 7.3 %collective-permute-start.4 = (f32[3,128,128]{2,1,0:T(8,128)}, f32[3,128,128]{2,1,0:T(8,128)S(1)}, u32[]{:S(2)}, u32[]{:S(2)}) collective-permute-start(f32[3,128,128]{2,1,0:T(8,128)} %get-tuple-element.13), channel_id=1, source_target_pairs={{0,1},{1,2},{2,3},{3,4},{4,5},{5,6},{6,7},{7,8},{8,9},{9,10},{10,1... | collective-permute-start | bytes 589832 | tf_op jit(solution)/shard_map/ppermute | solution.py:18
  75.7 7.2 %collective-permute-start.5 = (f32[3,128,128]{2,1,0:T(8,128)}, f32[3,128,128]{2,1,0:T(8,128)S(1)}, u32[]{:S(2)}, u32[]{:S(2)}) collective-permute-start(f32[3,128,128]{2,1,0:T(8,128)} %get-tuple-element.15), channel_id=1, source_target_pairs={{1,0},{2,1},{3,2},{4,3},{5,4},{6,5},{7,6},{8,7},{9,8},{10,9},{11,1... | collective-permute-start | bytes 589832 | tf_op jit(solution)/shard_map/ppermute | solution.py:18
  78.7 4.3 %copy-start.4 = (f32[3,128,128]{2,1,0:T(8,128)}, f32[3,128,128]{2,1,0:T(8,128)S(1)}, u32[]{:S(2)}) copy-start(f32[3,128,128]{2,1,0:T(8,128)S(1)} %collective-permute-done.4.refs_0_) | copy-start | bytes 589828
  82.9 0.7 copy-start.5
  107.8 4.8 %collective-permute-start.6 = (f32[3,128,128]{2,1,0:T(8,128)}, f32[3,128,128]{2,1,0:T(8,128)S(1)}, u32[]{:S(2)}, u32[]{:S(2)}) collective-permute-start(f32[3,128,128]{2,1,0:T(8,128)} %get-tuple-element.19), channel_id=1, source_target_pairs={{0,1},{1,2},{2,3},{3,4},{4,5},{5,6},{6,7},{7,8},{8,9},{9,10},{10,1... | collective-permute-start | bytes 589832 | tf_op jit(solution)/shard_map/ppermute | solution.py:18
  109.7 7.2 %collective-permute-start.7 = (f32[3,128,128]{2,1,0:T(8,128)}, f32[3,128,128]{2,1,0:T(8,128)S(1)}, u32[]{:S(2)}, u32[]{:S(2)}) collective-permute-start(f32[3,128,128]{2,1,0:T(8,128)} %get-tuple-element.21), channel_id=1, source_target_pairs={{1,0},{2,1},{3,2},{4,3},{5,4},{6,5},{7,6},{8,7},{9,8},{10,9},{11,1... | collective-permute-start | bytes 589832 | tf_op jit(solution)/shard_map/ppermute | solution.py:18
  112.6 4.3 %copy-start.2 = (f32[3,128,128]{2,1,0:T(8,128)}, f32[3,128,128]{2,1,0:T(8,128)S(1)}, u32[]{:S(2)}) copy-start(f32[3,128,128]{2,1,0:T(8,128)S(1)} %collective-permute-done.6.refs_0_) | copy-start | bytes 589828
  116.9 0.7 copy-start.3

commit v12 on v11

--- a/solution.py
+++ b/solution.py
@@ -137,10 +137,19 @@
         last = pl.num_programs(0) - 1
         inner = pl.ds(SUB, rows_y)
 
+        blocks = rows // rows_block
+
+        def piece(k):
+            return pltpu.make_async_copy(
+                main_ref.at[pl.ds(k * rows_block, rows_block)],
+                p_ref.at[pl.ds(HALO + k * rows_block, rows_block), inner, :],
+                sems.at[k],
+            )
+
         @pl.when(block == 0)
         def _():
-            copy = pltpu.make_async_copy(main_ref, p_ref.at[pl.ds(HALO, rows), inner, :], sems.at[0])
-            copy.start()
+            for k in range(blocks):
+                piece(k).start()
             zeros = jnp.zeros((SUB, rows_z), jnp.float32)
 
             def clear(x, carry):
@@ -153,7 +162,7 @@
             p_ref[pl.ds(HALO + rows, HALO), inner, :] = high_ref[...]
             if first:
                 spread = pltpu.make_async_copy(
-                    wide_ref, e_ref.at[pl.ds(0, rows + 2), inner, :], sems.at[1]
+                    wide_ref, e_ref.at[pl.ds(0, rows + 2), inner, :], sems.at[blocks]
                 )
                 spread.start()
 
@@ -164,7 +173,12 @@
 
                 lax.fori_loop(0, rows + 2, clear_edge, 0)
                 spread.wait()
-            copy.wait()
+            for k in range(min(blocks, 2)):
+                piece(k).wait()
+
+        @pl.when((block >= 1) & (block + 1 < blocks))
+        def _():
+            piece(block + 1).wait()
 
         lane = lax.broadcasted_iota(jnp.int32, (SUB, rows_z), 1)
 
@@ -287,7 +301,7 @@
         in_specs=in_specs,
         out_specs=out_specs,
         out_shape=out_shape,
-        scratch_shapes=scratch + [pltpu.SemaphoreType.DMA((2,))],
+        scratch_shapes=scratch + [pltpu.SemaphoreType.DMA((rows // rows_block + 1,))],
         compiler_params=pltpu.CompilerParams(dimension_semantics=("arbitrary",)),
     )(*operands)
 

time: 142 us -> 142 us (level)
  no operation moved by 1% of the time
where the time goes in v12:
time: 142 us; the launch traced here: 141 us
  Pallas kernels  72.5 us (51%)
  waiting for transfers between devices  24 us (17%)
  starting transfers between devices  22.6 us (16%)
  local copies, waits for them, and re-layouts  9.18 us (6%)
  matrix products  7.06 us (5%)
  other arithmetic  4.77 us (3%)
    pallas_call x3, Pallas kernels, stage(): pl.pallas_call(stage_kernel(scale_level, scale_step, rows_block, first),...  72.5 us
    ppermute x8, waiting for transfers between devices, shifted(): return lax.ppermute(block, axis, route)  24 us
    ppermute x8, starting transfers between devices, shifted(): return lax.ppermute(block, axis, route)  22.6 us
    unnamed x17, local copies, waits for them, and re-layouts  5.13 us
    select_n x1, other arithmetic, shards(): edge_wide = jnp.where(inside[1:-1, None, None], edge_wide, 0.0)  3.06 us
  transfers between devices with their start and end apart: 8, of which 5 were waited for; matrix products, arithmetic and copies ran while one was open for 12% of the time, Pallas kernels for 0%

profile of v12, /device:TPU:1, one launch (start us, length us, event | category | flops | bytes accessed | tf_op | source)
XLA Modules:
  0.0 141.1 jit_solution(8424877876802926717)
XLA Ops:
  0.6 2.7 %fusion.16 = (f32[14,128,128]{2,1,0:T(8,128)}, f32[14,128,128]{2,1,0:T(8,128)S(1)}) fusion(f32[32,128,128]{2,1,0:T(8,128)} %param.5), kind=kLoop, calls=%fused_computation.24 | loop fusion | bytes 3670016 | tf_op jit(solution)/shard_map/slice | solution.py:313
  3.3 4.5 %collective-permute-start.2 = (f32[14,128,128]{2,1,0:T(8,128)}, f32[14,128,128]{2,1,0:T(8,128)}, u32[]{:S(2)}, u32[]{:S(2)}) collective-permute-start(f32[14,128,128]{2,1,0:T(8,128)} %get-tuple-element.22), channel_id=1, source_target_pairs={{0,1},{1,2},{2,3},{3,4},{4,5},{5,6},{6,7},{7,8},{8,9},{9,10},{10,1... | collective-permute-start | bytes 2752520 | tf_op jit(solution)/shard_map/ppermute | solution.py:18
  7.9 1.9 %collective-permute-start.3 = (f32[14,128,128]{2,1,0:T(8,128)S(1)}, f32[14,128,128]{2,1,0:T(8,128)}, u32[]{:S(2)}, u32[]{:S(2)}) collective-permute-start(f32[14,128,128]{2,1,0:T(8,128)S(1)} %get-tuple-element.23), channel_id=1, source_target_pairs={{1,0},{2,1},{3,2},{4,3},{5,4},{6,5},{7,6},{8,7},{9,8},{10,9},{11,1... | collective-permute-start | bytes 2752520 | tf_op jit(solution)/shard_map/ppermute | solution.py:18
  9.8 1.1 fusion.17
  10.8 1.9 %collective-permute-start.1 = (f32[3,128,128]{2,1,0:T(8,128)S(1)}, f32[3,128,128]{2,1,0:T(8,128)}, u32[]{:S(2)}, u32[]{:S(2)}) collective-permute-start(f32[3,128,128]{2,1,0:T(8,128)S(1)} %get-tuple-element.24), channel_id=1, source_target_pairs={{1,0},{2,1},{3,2},{4,3},{5,4},{6,5},{7,6},{8,7},{9,8},{10,9},{11,1... | collective-permute-start | bytes 589832 | tf_op jit(solution)/shard_map/ppermute | solution.py:18
  12.8 3.6 %collective-permute-start = (f32[3,128,128]{2,1,0:T(8,128)S(1)}, f32[3,128,128]{2,1,0:T(8,128)}, u32[]{:S(2)}, u32[]{:S(2)}) collective-permute-start(f32[3,128,128]{2,1,0:T(8,128)S(1)} %get-tuple-element.25), channel_id=1, source_target_pairs={{0,1},{1,2},{2,3},{3,4},{4,5},{5,6},{6,7},{7,8},{8,9},{9,10},{10,1... | collective-permute-start | bytes 589832 | tf_op jit(solution)/shard_map/ppermute | solution.py:18
  16.5 13.9 %collective-permute-done.2 = f32[14,128,128]{2,1,0:T(8,128)} collective-permute-done((f32[14,128,128]{2,1,0:T(8,128)}, f32[14,128,128]{2,1,0:T(8,128)}, u32[]{:S(2)}, u32[]{:S(2)}) %collective-permute-start.2) | collective-permute-done | bytes 917536 | tf_op jit(solution)/shard_map/ppermute | solution.py:18
  30.4 1.7 %pad_maximum_fusion = f32[60,128,128]{2,1,0:T(8,128)S(1)} fusion(f32[14,128,128]{2,1,0:T(8,128)} %collective-permute-done.3, f32[32,128,128]{2,1,0:T(8,128)S(1)} %copy-done, f32[14,128,128]{2,1,0:T(8,128)} %collective-permute-done.2), kind=kLoop, calls=%fused_computation.4 | loop fusion | flops 1966080 | bytes 7864320 | tf_op jit(solution)/shard_map/concatenate | solution.py:315
  32.7 2.4 %copy.9 = f32[8,8,128,128]{3,1,2,0:T(8,128)S(1)} copy(f32[8,8,128,128]{3,2,1,0:T(8,128)S(1)} %bitcast.14) | data formatting | bytes 8388608
  35.1 2.5 %fusion.18 = f32[36,16384]{1,0:T(8,128)S(1)} fusion(f32[36,60]{1,0:T(8,128)S(1)} %copy-done.6, f32[60,16384]{1,0:T(8,128)S(1)} %bitcast.15), kind=kOutput, calls=%fused_computation.26 | convolution fusion | flops 424673280 | bytes 6300096 | tf_op jit(solution)/shard_map/dot_general | solution.py:317
  38.5 2.3 %fusion = f32[36,128,128]{1,2,0:T(8,128)S(1)} fusion(f32[128,128,1]{1,0,2:T(8,128)S(1)} %copy-done.1, f32[40,128,128]{2,1,0:T(8,128)S(1)} %bitcast.17), kind=kOutput, calls=%fused_computation.5 | convolution fusion | flops 905969664 | bytes 4784128 | tf_op jit(solution)/shard_map/dot_general | solution.py:322
  40.7 2.2 %select_bitcast_fusion = f32[36,128,128]{2,1,0:T(8,128)S(1)} fusion(f32[36,128,128]{1,2,0:T(8,128)S(1)} %fusion, f32[128,128,1]{1,0,2:T(8,128)S(1)} %copy-done.1, pred[36]{0:T(512)(128)(4,1)S(1)} %compare_and_fusion), kind=kOutput, calls=%fused_computation.7 | convolution fusion | flops 906559488 | bytes 4784164 | tf_op jit(solution)/shard_map/yv,xvz->xyz/dot_general | solution.py:325
  43.2 3.1 %fusion.15.refs_3_ = f32[34,128,128]{2,1,0:T(8,128)} fusion(f32[34,128,128]{2,1,0:T(8,128)S(1)} %slice.50, f32[36,128,128]{2,1,0:T(8,128)S(1)} %select_bitcast_fusion, pred[34]{0:T(512)(128)(4,1)S(1)} %slice.38), kind=kLoop, calls=%fused_computation.22 | loop fusion | flops 8355840 | bytes 8912930 | tf_op jit(solution)/shard_map/jit(_where)/select_n | solution.py:330
  46.3 25.1 %shard_map.68 = (f32[32,128,128]{2,1,0:T(8,128)}, f32[3,128,128]{2,1,0:T(8,128)}, f32[3,128,128]{2,1,0:T(8,128)}, f32[32,128,128]{2,1,0:T(8,128)}, f32[32,128,12...) custom-call(f32[3,128,128]{2,1,0:T(8,128)} %collective-permute-done.refs_0_, ...), custom_call_target="tpu_custom_call" | custom-call | tf_op jit(solution)/shard_map/pallas_call | solution.py:298
  71.4 4.4 %collective-permute-start.4 = (f32[3,128,128]{2,1,0:T(8,128)}, f32[3,128,128]{2,1,0:T(8,128)S(1)}, u32[]{:S(2)}, u32[]{:S(2)}) collective-permute-start(f32[3,128,128]{2,1,0:T(8,128)} %get-tuple-element.13), channel_id=1, source_target_pairs={{0,1},{1,2},{2,3},{3,4},{4,5},{5,6},{6,7},{7,8},{8,9},{9,10},{10,1... | collective-permute-start | bytes 589832 | tf_op jit(solution)/shard_map/ppermute | solution.py:18
  75.8 1.9 %collective-permute-start.5 = (f32[3,128,128]{2,1,0:T(8,128)}, f32[3,128,128]{2,1,0:T(8,128)S(1)}, u32[]{:S(2)}, u32[]{:S(2)}) collective-permute-start(f32[3,128,128]{2,1,0:T(8,128)} %get-tuple-element.15), channel_id=1, source_target_pairs={{1,0},{2,1},{3,2},{4,3},{5,4},{6,5},{7,6},{8,7},{9,8},{10,9},{11,1... | collective-permute-start | bytes 589832 | tf_op jit(solution)/shard_map/ppermute | solution.py:18
  77.8 1.0 collective-permute-done.4.refs_0_
  78.8 4.3 %collective-permute-done.5.refs_2_ = f32[3,128,128]{2,1,0:T(8,128)S(1)} collective-permute-done((f32[3,128,128]{2,1,0:T(8,128)}, f32[3,128,128]{2,1,0:T(8,128)S(1)}, u32[]{:S(2)}, u32[]{:S(2)}) %collective-permute-start.5) | collective-permute-done | bytes 196640 | tf_op jit(solution)/shard_map/ppermute | solution.py:18
  83.0 0.7 copy-done.5
  83.7 23.8 %shard_map.69 = (f32[32,128,128]{2,1,0:T(8,128)}, f32[3,128,128]{2,1,0:T(8,128)}, f32[3,128,128]{2,1,0:T(8,128)}) custom-call(f32[3,128,128]{2,1,0:T(8,128)} %copy-done.4, f32[32,128,128]{2,1,0:T(8,128)} %get-tuple-element.14.refs_1_, f32[3,128,128]{2,1,0:T(8,128)} %copy-done.5, f32[32,128,128]{2,1,0:T(8,128)} %get-tuple-element.10.refs_3_, ...), custom_call_target="tpu_custom_call" | custom-call | tf_op jit(solution)/shard_map/pallas_call | solution.py:298
  107.5 1.9 %collective-permute-start.6 = (f32[3,128,128]{2,1,0:T(8,128)}, f32[3,128,128]{2,1,0:T(8,128)S(1)}, u32[]{:S(2)}, u32[]{:S(2)}) collective-permute-start(f32[3,128,128]{2,1,0:T(8,128)} %get-tuple-element.19), channel_id=1, source_target_pairs={{0,1},{1,2},{2,3},{3,4},{4,5},{5,6},{6,7},{7,8},{8,9},{9,10},{10,1... | collective-permute-start | bytes 589832 | tf_op jit(solution)/shard_map/ppermute | solution.py:18
  109.5 2.4 %collective-permute-start.7 = (f32[3,128,128]{2,1,0:T(8,128)}, f32[3,128,128]{2,1,0:T(8,128)S(1)}, u32[]{:S(2)}, u32[]{:S(2)}) collective-permute-start(f32[3,128,128]{2,1,0:T(8,128)} %get-tuple-element.21), channel_id=1, source_target_pairs={{1,0},{2,1},{3,2},{4,3},{5,4},{6,5},{7,6},{8,7},{9,8},{10,9},{11,1... | collective-permute-start | bytes 589832 | tf_op jit(solution)/shard_map/ppermute | solution.py:18
  112.4 4.3 %collective-permute-done.7.refs_2_ = f32[3,128,128]{2,1,0:T(8,128)S(1)} collective-permute-done((f32[3,128,128]{2,1,0:T(8,128)}, f32[3,128,128]{2,1,0:T(8,128)S(1)}, u32[]{:S(2)}, u32[]{:S(2)}) %collective-permute-start.7) | collective-permute-done | bytes 196640 | tf_op jit(solution)/shard_map/ppermute | solution.py:18
  117.4 23.5 %shard_map.70 = f32[32,128,128]{2,1,0:T(8,128)} custom-call(f32[3,128,128]{2,1,0:T(8,128)} %copy-done.2, f32[32,128,128]{2,1,0:T(8,128)} %get-tuple-element.20.refs_1_, f32[3,128,128]{2,1,0:T(8,128)} %copy-done.3, f32[32,128,128]{2,1,0:T(8,128)} %get-tuple-element.10.refs_3_, f32[32,128,128]{2,1,0:T(8,128)} %get-tuple-element.16.refs_4_, ...), custom_call_target="tpu_custom_call" | custom-call | tf_op jit(solution)/shard_map/pallas_call | solution.py:298
  (22 shorter events, 2.9 us)
Async XLA Ops:
  0.6 29.8 %copy-start = (f32[32,128,128]{2,1,0:T(8,128)S(1)}, f32[32,128,128]{2,1,0:T(8,128)}, u32[]{:S(2)}) copy-start(f32[32,128,128]{2,1,0:T(8,128)} %param.5) | copy-start | bytes 6291460
  3.3 27.1 %collective-permute-start.2 = (f32[14,128,128]{2,1,0:T(8,128)}, f32[14,128,128]{2,1,0:T(8,128)}, u32[]{:S(2)}, u32[]{:S(2)}) collective-permute-start(f32[14,128,128]{2,1,0:T(8,128)} %get-tuple-element.22), channel_id=1, source_target_pairs={{0,1},{1,2},{2,3},{3,4},{4,5},{5,6},{6,7},{7,8},{8,9},{9,10},{10,1... | collective-permute-start | bytes 2752520 | tf_op jit(solution)/shard_map/ppermute | solution.py:18
  7.9 22.6 %collective-permute-start.3 = (f32[14,128,128]{2,1,0:T(8,128)S(1)}, f32[14,128,128]{2,1,0:T(8,128)}, u32[]{:S(2)}, u32[]{:S(2)}) collective-permute-start(f32[14,128,128]{2,1,0:T(8,128)S(1)} %get-tuple-element.23), channel_id=1, source_target_pairs={{1,0},{2,1},{3,2},{4,3},{5,4},{6,5},{7,6},{8,7},{9,8},{10,9},{11,1... | collective-permute-start | bytes 2752520 | tf_op jit(solution)/shard_map/ppermute | solution.py:18
  10.8 35.5 %collective-permute-start.1 = (f32[3,128,128]{2,1,0:T(8,128)S(1)}, f32[3,128,128]{2,1,0:T(8,128)}, u32[]{:S(2)}, u32[]{:S(2)}) collective-permute-start(f32[3,128,128]{2,1,0:T(8,128)S(1)} %get-tuple-element.24), channel_id=1, source_target_pairs={{1,0},{2,1},{3,2},{4,3},{5,4},{6,5},{7,6},{8,7},{9,8},{10,9},{11,1... | collective-permute-start | bytes 589832 | tf_op jit(solution)/shard_map/ppermute | solution.py:18
  12.8 33.5 %collective-permute-start = (f32[3,128,128]{2,1,0:T(8,128)S(1)}, f32[3,128,128]{2,1,0:T(8,128)}, u32[]{:S(2)}, u32[]{:S(2)}) collective-permute-start(f32[3,128,128]{2,1,0:T(8,128)S(1)} %get-tuple-element.25), channel_id=1, source_target_pairs={{0,1},{1,2},{2,3},{3,4},{4,5},{5,6},{6,7},{7,8},{8,9},{9,10},{10,1... | collective-permute-start | bytes 589832 | tf_op jit(solution)/shard_map/ppermute | solution.py:18
  32.7 2.4 %copy-start.6 = (f32[36,60]{1,0:T(8,128)S(1)}, f32[36,60]{1,0:T(8,128)}, u32[]{:S(2)}) copy-start(f32[36,60]{1,0:T(8,128)} %constant.27.clone) | copy-start | bytes 25924
  37.6 0.8 copy-start.1
  71.4 7.3 %collective-permute-start.4 = (f32[3,128,128]{2,1,0:T(8,128)}, f32[3,128,128]{2,1,0:T(8,128)S(1)}, u32[]{:S(2)}, u32[]{:S(2)}) collective-permute-start(f32[3,128,128]{2,1,0:T(8,128)} %get-tuple-element.13), channel_id=1, source_target_pairs={{0,1},{1,2},{2,3},{3,4},{4,5},{5,6},{6,7},{7,8},{8,9},{9,10},{10,1... | collective-permute-start | bytes 589832 | tf_op jit(solution)/shard_map/ppermute | solution.py:18
  75.8 7.2 %collective-permute-start.5 = (f32[3,128,128]{2,1,0:T(8,128)}, f32[3,128,128]{2,1,0:T(8,128)S(1)}, u32[]{:S(2)}, u32[]{:S(2)}) collective-permute-start(f32[3,128,128]{2,1,0:T(8,128)} %get-tuple-element.15), channel_id=1, source_target_pairs={{1,0},{2,1},{3,2},{4,3},{5,4},{6,5},{7,6},{8,7},{9,8},{10,9},{11,1... | collective-permute-start | bytes 589832 | tf_op jit(solution)/shard_map/ppermute | solution.py:18
  78.8 4.3 %copy-start.4 = (f32[3,128,128]{2,1,0:T(8,128)}, f32[3,128,128]{2,1,0:T(8,128)S(1)}, u32[]{:S(2)}) copy-start(f32[3,128,128]{2,1,0:T(8,128)S(1)} %collective-permute-done.4.refs_0_) | copy-start | bytes 589828
  83.0 0.7 copy-start.5
  107.5 4.8 %collective-permute-start.6 = (f32[3,128,128]{2,1,0:T(8,128)}, f32[3,128,128]{2,1,0:T(8,128)S(1)}, u32[]{:S(2)}, u32[]{:S(2)}) collective-permute-start(f32[3,128,128]{2,1,0:T(8,128)} %get-tuple-element.19), channel_id=1, source_target_pairs={{0,1},{1,2},{2,3},{3,4},{4,5},{5,6},{6,7},{7,8},{8,9},{9,10},{10,1... | collective-permute-start | bytes 589832 | tf_op jit(solution)/shard_map/ppermute | solution.py:18
  109.5 7.2 %collective-permute-start.7 = (f32[3,128,128]{2,1,0:T(8,128)}, f32[3,128,128]{2,1,0:T(8,128)S(1)}, u32[]{:S(2)}, u32[]{:S(2)}) collective-permute-start(f32[3,128,128]{2,1,0:T(8,128)} %get-tuple-element.21), channel_id=1, source_target_pairs={{1,0},{2,1},{3,2},{4,3},{5,4},{6,5},{7,6},{8,7},{9,8},{10,9},{11,1... | collective-permute-start | bytes 589832 | tf_op jit(solution)/shard_map/ppermute | solution.py:18
  112.4 4.3 %copy-start.2 = (f32[3,128,128]{2,1,0:T(8,128)}, f32[3,128,128]{2,1,0:T(8,128)S(1)}, u32[]{:S(2)}) copy-start(f32[3,128,128]{2,1,0:T(8,128)S(1)} %collective-permute-done.6.refs_0_) | copy-start | bytes 589828
  116.7 0.7 copy-start.3

commit v13 on v12

--- a/solution.py
+++ b/solution.py
@@ -306,12 +306,40 @@
     )(*operands)
 
 
+def ends_kernel(count):
+    def kernel(volume_ref, bottom_ref, top_ref, sems):
+        rows = volume_ref.shape[0]
+        copies = [
+            pltpu.make_async_copy(volume_ref.at[pl.ds(rows - count, count)], bottom_ref, sems.at[0]),
+            pltpu.make_async_copy(volume_ref.at[pl.ds(0, count)], top_ref, sems.at[1]),
+        ]
+        for copy in copies:
+            copy.start()
+        for copy in copies:
+            copy.wait()
+
+    return kernel
+
+
+def ends(volume, count):
+    shape = jax.ShapeDtypeStruct((count,) + volume.shape[1:], volume.dtype)
+    raw = pl.BlockSpec(memory_space=pl.ANY)
+    return pl.pallas_call(
+        ends_kernel(count),
+        in_specs=[raw],
+        out_specs=[raw, raw],
+        out_shape=[shape, shape],
+        scratch_shapes=[pltpu.SemaphoreType.DMA((2,))],
+    )(volume)
+
+
 def shards(volume, level_set):
     rows, rows_y, rows_z = volume.shape
     exact = lax.Precision.HIGHEST
     halo = min(rows, RADIUS + 2)
-    low = shifted(volume[rows - halo :], "gx", 1)
-    high = shifted(volume[:halo], "gx", -1)
+    bottom_rows, top_rows = ends(volume, halo)
+    low = shifted(bottom_rows, "gx", 1)
+    high = shifted(top_rows, "gx", -1)
     extended = jnp.concatenate([low, volume, high], axis=0)
     wide = rows + 4
     blurred = jnp.dot(

time: 142 us -> 196 us (1.38)
  Pallas kernels: 72.5 us -> 129 us
  local copies, waits for them, and re-layouts: 9.18 us -> 6.65 us
    pallas_call x0 -> x1, Pallas kernels: none -> 56.7 us  [ends(): pl.pallas_call(ends_kernel(count), in_specs=[raw], out_specs=[raw, raw],...]
    slice x1 -> x0, local copies, waits for them, and re-layouts: 2.69 us -> none  [shards(): low = shifted(volume[rows - halo:], 'gx', 1)]
  transfers between devices with their start and end apart: 8 -> 8, of which waited for: 5 -> 5; matrix products, arithmetic and copies ran while one was open for 12% -> 9% of each run, Pallas kernels for 0% -> 0%
where the time goes in v13:
time: 196 us; the launch traced here: 195 us
  Pallas kernels  129 us (66%)
  waiting for transfers between devices  24 us (12%)
  starting transfers between devices  22.5 us (11%)
  matrix products  7.06 us (4%)
  local copies, waits for them, and re-layouts  6.65 us (3%)
  other arithmetic  4.64 us (2%)
    pallas_call x3, Pallas kernels, stage(): pl.pallas_call(stage_kernel(scale_level, scale_step, rows_block, first),...  72.5 us
    pallas_call x1, Pallas kernels, ends(): pl.pallas_call(ends_kernel(count), in_specs=[raw], out_specs=[raw, raw],...  56.7 us
    ppermute x8, waiting for transfers between devices, shifted(): return lax.ppermute(block, axis, route)  24 us
    ppermute x8, starting transfers between devices, shifted(): return lax.ppermute(block, axis, route)  22.5 us
    unnamed x17, local copies, waits for them, and re-layouts  5.28 us
  transfers between devices with their start and end apart: 8, of which 5 were waited for; matrix products, arithmetic and copies ran while one was open for 9% of the time, Pallas kernels for 0%

profile of v13, /device:TPU:1, one launch (start us, length us, event | category | flops | bytes accessed | tf_op | source)
XLA Modules:
  0.0 195.0 jit_solution(8492246979854061083)
XLA Ops:
  0.6 56.7 %shard_map.68 = (f32[14,128,128]{2,1,0:T(8,128)}, f32[14,128,128]{2,1,0:T(8,128)}) custom-call(f32[32,128,128]{2,1,0:T(8,128)} %volume_ref.1), custom_call_target="tpu_custom_call" | custom-call | tf_op jit(solution)/shard_map/pallas_call | solution.py:327
  57.4 4.5 %collective-permute-start.2 = (f32[14,128,128]{2,1,0:T(8,128)}, f32[14,128,128]{2,1,0:T(8,128)S(1)}, u32[]{:S(2)}, u32[]{:S(2)}) collective-permute-start(f32[14,128,128]{2,1,0:T(8,128)} %get-tuple-element.14), channel_id=1, source_target_pairs={{0,1},{1,2},{2,3},{3,4},{4,5},{5,6},{6,7},{7,8},{8,9},{9,10},{10,1... | collective-permute-start | bytes 2752520 | tf_op jit(solution)/shard_map/ppermute | solution.py:18
  61.9 1.9 collective-permute-start.3
  63.8 1.1 fusion.16
  64.9 1.9 collective-permute-start.1
  66.8 3.6 %collective-permute-start = (f32[3,128,128]{2,1,0:T(8,128)S(1)}, f32[3,128,128]{2,1,0:T(8,128)}, u32[]{:S(2)}, u32[]{:S(2)}) collective-permute-start(f32[3,128,128]{2,1,0:T(8,128)S(1)} %get-tuple-element.27), channel_id=1, source_target_pairs={{0,1},{1,2},{2,3},{3,4},{4,5},{5,6},{6,7},{7,8},{8,9},{9,10},{10,1... | collective-permute-start | bytes 589832 | tf_op jit(solution)/shard_map/ppermute | solution.py:18
  70.5 13.9 %collective-permute-done.2 = f32[14,128,128]{2,1,0:T(8,128)S(1)} collective-permute-done((f32[14,128,128]{2,1,0:T(8,128)}, f32[14,128,128]{2,1,0:T(8,128)S(1)}, u32[]{:S(2)}, u32[]{:S(2)}) %collective-permute-start.2) | collective-permute-done | bytes 917536 | tf_op jit(solution)/shard_map/ppermute | solution.py:18
  84.5 1.6 pad_maximum_fusion
  86.7 2.4 %copy.9 = f32[8,8,128,128]{3,1,2,0:T(8,128)S(1)} copy(f32[8,8,128,128]{3,2,1,0:T(8,128)S(1)} %bitcast.14) | data formatting | bytes 8388608
  89.1 2.5 %fusion.17 = f32[36,16384]{1,0:T(8,128)S(1)} fusion(f32[36,60]{1,0:T(8,128)S(1)} %copy-done.6, f32[60,16384]{1,0:T(8,128)S(1)} %bitcast.15), kind=kOutput, calls=%fused_computation.25 | convolution fusion | flops 424673280 | bytes 6300096 | tf_op jit(solution)/shard_map/dot_general | solution.py:345
  92.5 2.3 %fusion = f32[36,128,128]{1,2,0:T(8,128)S(1)} fusion(f32[128,128,1]{1,0,2:T(8,128)S(1)} %copy-done.1, f32[40,128,128]{2,1,0:T(8,128)S(1)} %bitcast.17), kind=kOutput, calls=%fused_computation.5 | convolution fusion | flops 905969664 | bytes 4784128 | tf_op jit(solution)/shard_map/dot_general | solution.py:350
  94.8 2.2 %select_bitcast_fusion = f32[36,128,128]{2,1,0:T(8,128)S(1)} fusion(f32[36,128,128]{1,2,0:T(8,128)S(1)} %fusion, f32[128,128,1]{1,0,2:T(8,128)S(1)} %copy-done.1, pred[36]{0:T(512)(128)(4,1)S(1)} %compare_and_fusion), kind=kOutput, calls=%fused_computation.7 | convolution fusion | flops 906559488 | bytes 4784164 | tf_op jit(solution)/shard_map/yv,xvz->xyz/dot_general | solution.py:353
  97.3 3.1 %fusion.15.refs_3_ = f32[34,128,128]{2,1,0:T(8,128)} fusion(f32[34,128,128]{2,1,0:T(8,128)S(1)} %slice.42, f32[36,128,128]{2,1,0:T(8,128)S(1)} %select_bitcast_fusion, pred[34]{0:T(512)(128)(4,1)S(1)} %slice.32), kind=kLoop, calls=%fused_computation.22 | loop fusion | flops 8355840 | bytes 8912930 | tf_op jit(solution)/shard_map/jit(_where)/select_n | solution.py:358
  100.4 25.1 %shard_map.69 = (f32[32,128,128]{2,1,0:T(8,128)}, f32[3,128,128]{2,1,0:T(8,128)}, f32[3,128,128]{2,1,0:T(8,128)}, f32[32,128,128]{2,1,0:T(8,128)}, f32[32,128,12...) custom-call(f32[3,128,128]{2,1,0:T(8,128)} %collective-permute-done.refs_0_, ...), custom_call_target="tpu_custom_call" | custom-call | tf_op jit(solution)/shard_map/pallas_call | solution.py:298
  125.5 4.3 %collective-permute-start.4 = (f32[3,128,128]{2,1,0:T(8,128)}, f32[3,128,128]{2,1,0:T(8,128)S(1)}, u32[]{:S(2)}, u32[]{:S(2)}) collective-permute-start(f32[3,128,128]{2,1,0:T(8,128)} %get-tuple-element.17), channel_id=1, source_target_pairs={{0,1},{1,2},{2,3},{3,4},{4,5},{5,6},{6,7},{7,8},{8,9},{9,10},{10,1... | collective-permute-start | bytes 589832 | tf_op jit(solution)/shard_map/ppermute | solution.py:18
  129.8 1.9 collective-permute-start.5
  131.7 1.0 collective-permute-done.4.refs_0_
  132.7 4.3 %collective-permute-done.5.refs_2_ = f32[3,128,128]{2,1,0:T(8,128)S(1)} collective-permute-done((f32[3,128,128]{2,1,0:T(8,128)}, f32[3,128,128]{2,1,0:T(8,128)S(1)}, u32[]{:S(2)}, u32[]{:S(2)}) %collective-permute-start.5) | collective-permute-done | bytes 196640 | tf_op jit(solution)/shard_map/ppermute | solution.py:18
  137.0 0.7 copy-done.5
  137.7 23.8 %shard_map.70 = (f32[32,128,128]{2,1,0:T(8,128)}, f32[3,128,128]{2,1,0:T(8,128)}, f32[3,128,128]{2,1,0:T(8,128)}) custom-call(f32[3,128,128]{2,1,0:T(8,128)} %copy-done.4, f32[32,128,128]{2,1,0:T(8,128)} %get-tuple-element.18.refs_1_, f32[3,128,128]{2,1,0:T(8,128)} %copy-done.5, f32[32,128,128]{2,1,0:T(8,128)} %get-tuple-element.12.refs_3_, ...), custom_call_target="tpu_custom_call" | custom-call | tf_op jit(solution)/shard_map/pallas_call | solution.py:298
  161.5 1.9 collective-permute-start.6
  163.4 2.4 %collective-permute-start.7 = (f32[3,128,128]{2,1,0:T(8,128)}, f32[3,128,128]{2,1,0:T(8,128)S(1)}, u32[]{:S(2)}, u32[]{:S(2)}) collective-permute-start(f32[3,128,128]{2,1,0:T(8,128)} %get-tuple-element.25), channel_id=1, source_target_pairs={{1,0},{2,1},{3,2},{4,3},{5,4},{6,5},{7,6},{8,7},{9,8},{10,9},{11,1... | collective-permute-start | bytes 589832 | tf_op jit(solution)/shard_map/ppermute | solution.py:18
  166.3 4.3 %collective-permute-done.7.refs_2_ = f32[3,128,128]{2,1,0:T(8,128)S(1)} collective-permute-done((f32[3,128,128]{2,1,0:T(8,128)}, f32[3,128,128]{2,1,0:T(8,128)S(1)}, u32[]{:S(2)}, u32[]{:S(2)}) %collective-permute-start.7) | collective-permute-done | bytes 196640 | tf_op jit(solution)/shard_map/ppermute | solution.py:18
  171.3 23.5 %shard_map.71 = f32[32,128,128]{2,1,0:T(8,128)} custom-call(f32[3,128,128]{2,1,0:T(8,128)} %copy-done.2, f32[32,128,128]{2,1,0:T(8,128)} %get-tuple-element.24.refs_1_, f32[3,128,128]{2,1,0:T(8,128)} %copy-done.3, f32[32,128,128]{2,1,0:T(8,128)} %get-tuple-element.12.refs_3_, f32[32,128,128]{2,1,0:T(8,128)} %get-tuple-element.20.refs_4_, ...), custom_call_target="tpu_custom_call" | custom-call | tf_op jit(solution)/shard_map/pallas_call | solution.py:298
  (22 shorter events, 3.0 us)
Async XLA Ops:
  0.6 83.8 %copy-start = (f32[32,128,128]{2,1,0:T(8,128)S(1)}, f32[32,128,128]{2,1,0:T(8,128)}, u32[]{:S(2)}) copy-start(f32[32,128,128]{2,1,0:T(8,128)} %volume_ref.1) | copy-start | bytes 6291460
  57.4 27.1 %collective-permute-start.2 = (f32[14,128,128]{2,1,0:T(8,128)}, f32[14,128,128]{2,1,0:T(8,128)S(1)}, u32[]{:S(2)}, u32[]{:S(2)}) collective-permute-start(f32[14,128,128]{2,1,0:T(8,128)} %get-tuple-element.14), channel_id=1, source_target_pairs={{0,1},{1,2},{2,3},{3,4},{4,5},{5,6},{6,7},{7,8},{8,9},{9,10},{10,1... | collective-permute-start | bytes 2752520 | tf_op jit(solution)/shard_map/ppermute | solution.py:18
  61.9 22.6 %collective-permute-start.3 = (f32[14,128,128]{2,1,0:T(8,128)}, f32[14,128,128]{2,1,0:T(8,128)}, u32[]{:S(2)}, u32[]{:S(2)}) collective-permute-start(f32[14,128,128]{2,1,0:T(8,128)} %get-tuple-element.15), channel_id=1, source_target_pairs={{1,0},{2,1},{3,2},{4,3},{5,4},{6,5},{7,6},{8,7},{9,8},{10,9},{11,1... | collective-permute-start | bytes 2752520 | tf_op jit(solution)/shard_map/ppermute | solution.py:18
  64.9 35.5 %collective-permute-start.1 = (f32[3,128,128]{2,1,0:T(8,128)S(1)}, f32[3,128,128]{2,1,0:T(8,128)}, u32[]{:S(2)}, u32[]{:S(2)}) collective-permute-start(f32[3,128,128]{2,1,0:T(8,128)S(1)} %get-tuple-element.26), channel_id=1, source_target_pairs={{1,0},{2,1},{3,2},{4,3},{5,4},{6,5},{7,6},{8,7},{9,8},{10,9},{11,1... | collective-permute-start | bytes 589832 | tf_op jit(solution)/shard_map/ppermute | solution.py:18
  66.8 33.6 %collective-permute-start = (f32[3,128,128]{2,1,0:T(8,128)S(1)}, f32[3,128,128]{2,1,0:T(8,128)}, u32[]{:S(2)}, u32[]{:S(2)}) collective-permute-start(f32[3,128,128]{2,1,0:T(8,128)S(1)} %get-tuple-element.27), channel_id=1, source_target_pairs={{0,1},{1,2},{2,3},{3,4},{4,5},{5,6},{6,7},{7,8},{8,9},{9,10},{10,1... | collective-permute-start | bytes 589832 | tf_op jit(solution)/shard_map/ppermute | solution.py:18
  86.7 2.4 %copy-start.6 = (f32[36,60]{1,0:T(8,128)S(1)}, f32[36,60]{1,0:T(8,128)}, u32[]{:S(2)}) copy-start(f32[36,60]{1,0:T(8,128)} %constant.27.clone) | copy-start | bytes 25924
  91.7 0.8 copy-start.1
  125.5 7.2 %collective-permute-start.4 = (f32[3,128,128]{2,1,0:T(8,128)}, f32[3,128,128]{2,1,0:T(8,128)S(1)}, u32[]{:S(2)}, u32[]{:S(2)}) collective-permute-start(f32[3,128,128]{2,1,0:T(8,128)} %get-tuple-element.17), channel_id=1, source_target_pairs={{0,1},{1,2},{2,3},{3,4},{4,5},{5,6},{6,7},{7,8},{8,9},{9,10},{10,1... | collective-permute-start | bytes 589832 | tf_op jit(solution)/shard_map/ppermute | solution.py:18
  129.8 7.2 %collective-permute-start.5 = (f32[3,128,128]{2,1,0:T(8,128)}, f32[3,128,128]{2,1,0:T(8,128)S(1)}, u32[]{:S(2)}, u32[]{:S(2)}) collective-permute-start(f32[3,128,128]{2,1,0:T(8,128)} %get-tuple-element.19), channel_id=1, source_target_pairs={{1,0},{2,1},{3,2},{4,3},{5,4},{6,5},{7,6},{8,7},{9,8},{10,9},{11,1... | collective-permute-start | bytes 589832 | tf_op jit(solution)/shard_map/ppermute | solution.py:18
  132.7 4.3 %copy-start.4 = (f32[3,128,128]{2,1,0:T(8,128)}, f32[3,128,128]{2,1,0:T(8,128)S(1)}, u32[]{:S(2)}) copy-start(f32[3,128,128]{2,1,0:T(8,128)S(1)} %collective-permute-done.4.refs_0_) | copy-start | bytes 589828
  137.0 0.7 copy-start.5
  161.5 4.8 %collective-permute-start.6 = (f32[3,128,128]{2,1,0:T(8,128)}, f32[3,128,128]{2,1,0:T(8,128)S(1)}, u32[]{:S(2)}, u32[]{:S(2)}) collective-permute-start(f32[3,128,128]{2,1,0:T(8,128)} %get-tuple-element.23), channel_id=1, source_target_pairs={{0,1},{1,2},{2,3},{3,4},{4,5},{5,6},{6,7},{7,8},{8,9},{9,10},{10,1... | collective-permute-start | bytes 589832 | tf_op jit(solution)/shard_map/ppermute | solution.py:18
  163.4 7.2 %collective-permute-start.7 = (f32[3,128,128]{2,1,0:T(8,128)}, f32[3,128,128]{2,1,0:T(8,128)S(1)}, u32[]{:S(2)}, u32[]{:S(2)}) collective-permute-start(f32[3,128,128]{2,1,0:T(8,128)} %get-tuple-element.25), channel_id=1, source_target_pairs={{1,0},{2,1},{3,2},{4,3},{5,4},{6,5},{7,6},{8,7},{9,8},{10,9},{11,1... | collective-permute-start | bytes 589832 | tf_op jit(solution)/shard_map/ppermute | solution.py:18
  166.3 4.3 %copy-start.2 = (f32[3,128,128]{2,1,0:T(8,128)}, f32[3,128,128]{2,1,0:T(8,128)S(1)}, u32[]{:S(2)}) copy-start(f32[3,128,128]{2,1,0:T(8,128)S(1)} %collective-permute-done.6.refs_0_) | copy-start | bytes 589828
  170.6 0.7 copy-start.3
